TPU v7x, 512 devices: a whole 4x8x8 slice. The times are simulated.
512 devices in a mesh: ctx: 32 (over y, x), fsdp: 16 (over z, core).
Axes of the slice: x: 4, y: 8, z: 8, core: 2. Of those that a mesh axis runs over, the one named last changes fastest.
Arguments:
- tokens: bfloat16 [131072, 4096], P(('ctx', 'fsdp')), may hold values from -48 to 48
- query_weight: bfloat16 [4096, 512], P('fsdp'), may hold values from -0.09375 to 0.09375
- key_weight: bfloat16 [4096, 128], P('fsdp'), may hold values from -0.09375 to 0.09375
- value_weight: bfloat16 [4096, 128], P('fsdp'), may hold values from -0.09375 to 0.09375
- chosen: int32 [256, 2], replicated, may hold values from 0 to 253, as said below
Outputs:
- attended: bfloat16 [131072, 512], P(('ctx', 'fsdp'))
Inputs may be any that keep to these rules, and one draw needn't show every extreme that they name: `chosen`: for query block q >= 3 both entries are distinct and below q - 1; block 2 names block 0 twice; blocks 0 and 1 name 0 twice, which selects nothing. The last block always selects block 253.
All inputs are finite; a program needn't handle non-finite values.
Results may differ from a plain program's by a relative error of at most 0.0065.
The roundings to bfloat16 on the way count: a program that leaves them out, or rounds other values in their place, can miss the bound.
Values may be sent and summed in bfloat16 or wider, within the bound.
No kernel may reach another device: no remote copies, remote signals or barrier semaphores. Data moves between devices by JAX's collectives and lax.ppermute only.
A program may use at most 64 MiB of HBM per device.

v0:
```python
import jax
import jax.numpy as jnp
from jax import lax
from jax.sharding import PartitionSpec as P

QH = 4


def from_behind(array, axis, by):
    peers = lax.axis_size(axis)
    pairs = [(i, i + by) for i in range(peers) if 0 <= i + by < peers]
    return lax.ppermute(array, axis, pairs)


def project_rows(tokens, pieces):
    return tuple(
        (
            jnp.dot(tokens, weight_piece, preferred_element_type=jnp.float32)
            for weight_piece in pieces
        )
    )


def per_device(tokens, query_weight, key_weight, value_weight, chosen):
    token_rows = tokens.shape[0]
    head_width = key_weight.shape[1]
    pair_width = 2 * head_width
    lane_count = lax.axis_size("fsdp")
    lane_index = lax.axis_index("fsdp")
    group_index = lax.axis_index("ctx")
    blocks_group = lane_count // 2
    my_block = group_index * blocks_group + lane_index // 2
    global_index = group_index * lane_count + lane_index
    projected = project_rows(
        tokens,
        (
            lax.all_gather(query_weight, "fsdp", axis=0, tiled=True),
            lax.all_gather(key_weight, "fsdp", axis=0, tiled=True),
            lax.all_gather(value_weight, "fsdp", axis=0, tiled=True),
        ),
    )
    queries = projected[0].astype(jnp.bfloat16).reshape(token_rows, QH, head_width)
    key_value = jnp.concatenate(
        [projected[1].astype(jnp.bfloat16), projected[2].astype(jnp.bfloat16)], axis=1
    )
    before_pair = from_behind(key_value, ("ctx", "fsdp"), 1)
    own_block = jnp.concatenate([before_pair, key_value], axis=0)
    candidates = lax.all_gather(key_value, "ctx", axis=0, tiled=True).reshape(
        -1, token_rows, pair_width
    )
    wanted = jnp.repeat(
        lax.dynamic_slice_in_dim(chosen, group_index * blocks_group, blocks_group, 0), 2, axis=0
    )
    dest_block = group_index * blocks_group + jnp.arange(lane_count, dtype=jnp.int32) // 2
    live_first = wanted[:, 0] < dest_block - 1
    live_second = (wanted[:, 1] < dest_block - 1) & (wanted[:, 1] != wanted[:, 0])
    mine = lax.dynamic_index_in_dim(chosen, my_block, 0, keepdims=False)
    sending = jnp.stack([live_first, live_second], axis=1) & (
        wanted % blocks_group == lane_index // 2
    )
    outgoing = jnp.take(candidates, (wanted // blocks_group).reshape(-1), axis=0)
    outgoing = outgoing.reshape(lane_count, 2, token_rows, pair_width)
    outgoing = jnp.where(sending[:, :, None, None], outgoing, jnp.zeros_like(outgoing))
    incoming = lax.all_to_all(outgoing, "fsdp", split_axis=0, concat_axis=0, tiled=True)

    def assemble(which):
        place = mine[which] % blocks_group * 2
        column_slot = incoming[:, which]
        return jnp.concatenate(
            [
                lax.dynamic_index_in_dim(column_slot, place, 0, keepdims=False),
                lax.dynamic_index_in_dim(column_slot, place + 1, 0, keepdims=False),
            ],
            axis=0,
        )

    block_first = assemble(0)
    block_second = assemble(1)
    key_rows = jnp.concatenate(
        [own_block[:, :head_width], block_first[:, :head_width], block_second[:, :head_width]],
        axis=0,
    )
    value_rows = jnp.concatenate(
        [own_block[:, head_width:], block_first[:, head_width:], block_second[:, head_width:]],
        axis=0,
    )
    scores = jnp.einsum(
        "qhd,kd->hqk", queries, key_rows, preferred_element_type=jnp.float32
    ) * head_width ** (-0.5)
    window_rows = own_block.shape[0]
    pick_rows = block_first.shape[0]
    row_index = jnp.arange(token_rows, dtype=jnp.int32)
    column = jnp.arange(window_rows, dtype=jnp.int32)
    causal = (column[None, :] <= row_index[:, None] + token_rows) & (
        (column[None, :] >= token_rows) | (global_index > 0)
    )
    first_ok = mine[0] < my_block - 1
    second_ok = (mine[1] < my_block - 1) & (mine[1] != mine[0])
    visible = jnp.concatenate(
        [
            causal,
            jnp.broadcast_to(first_ok, (token_rows, pick_rows)),
            jnp.broadcast_to(second_ok, (token_rows, pick_rows)),
        ],
        axis=1,
    )
    scores = jnp.where(visible[None], scores, -jnp.inf)
    highest = jnp.max(scores, axis=2, keepdims=True)
    probs = jnp.exp(scores - highest)
    denominator = jnp.sum(probs, axis=2, keepdims=True)
    mixed = (
        jnp.einsum(
            "hqk,kd->hqd",
            probs.astype(jnp.bfloat16),
            value_rows,
            preferred_element_type=jnp.float32,
        )
        / denominator
    )
    return jnp.transpose(mixed, (1, 0, 2)).reshape(token_rows, -1).astype(jnp.bfloat16)


def solution(mesh):
    return jax.shard_map(
        per_device,
        mesh=mesh,
        in_specs=(P(("ctx", "fsdp"), None), P("fsdp", None), P("fsdp", None), P("fsdp", None), P()),
        out_specs=P(("ctx", "fsdp"), None),
        check_vma=False,
    )
```

profile of v0, /device:TPU:7, one launch (start us, length us, event | category | flops | bytes accessed | tf_op | source)
XLA Modules:
  0.0 338.4 jit_solution(2382489390191044968)
XLA Ops:
  6.5 0.0 copy-start
  6.5 0.0 copy-start.2
  6.5 0.0 all-gather.7.cloned.1.call-start
  6.5 0.7 all-gather.7.cloned.1.call-update
  7.3 0.0 all-gather.5.cloned.1.call-start
  7.3 0.7 all-gather.5.cloned.1.call-update
  8.0 0.0 all-gather.9.cloned.1.call-start
  8.1 48.4 %all-gather.7.cloned.1.call-done = bf16[4096,128]{1,0:T(8,128)(2,1)} async-done(((bf16[256,128]{1,0:T(8,128)(2,1)}), bf16[4096,128]{1,0:T(8,128)(2,1)}) %all-gather.7.cloned.1.call-update) | async-done | bytes 1048592 | tf_op jit(solution)/shard_map/all_gather | solution.py:39
  56.5 0.0 copy-done
  56.5 2.0 convolution_convert_fusion.1
  58.5 40.2 %all-gather.5.cloned.1.call-done = bf16[4096,128]{1,0:T(8,128)(2,1)} async-done(((bf16[256,128]{1,0:T(8,128)(2,1)}), bf16[4096,128]{1,0:T(8,128)(2,1)}) %all-gather.5.cloned.1.call-update) | async-done | bytes 1048592 | tf_op jit(solution)/shard_map/all_gather | solution.py:38
  98.7 2.0 convolution_convert_fusion.2
  100.8 0.7 pad_maximum_fusion.2
  101.4 0.0 all-gather.9.cloned.1.call-update
  101.4 0.0 all-gather.11.cloned.1.call-start
  101.5 0.5 all-gather.11.cloned.1.call-update
  102.0 0.0 copy-done.2
  102.0 0.1 constant_dynamic-slice_fusion
  102.1 0.1 copy.15
  102.2 0.1 reshape.211
  102.3 0.1 copy.27
  102.4 0.1 copy.17
  102.5 0.1 copy.18
  102.7 82.7 %all-gather.9.cloned.1.call-done = bf16[8192,256]{0,1:T(8,128)(2,1)} async-done(((bf16[256,256]{0,1:T(8,128)(2,1)}), bf16[8192,256]{0,1:T(8,128)(2,1)}) %all-gather.9.cloned.1.call-update) | async-done | bytes 4194320 | tf_op jit(solution)/shard_map/all_gather | solution.py:48
  185.4 6.4 %copy.28 = bf16[8192,256]{1,0:T(8,128)(2,1)} copy(bf16[8192,256]{0,1:T(8,128)(2,1)} %all-gather.9.cloned.1.call-done) | data formatting | bytes 8388608 | tf_op jit(solution)/shard_map/reshape | solution.py:48
  191.8 5.0 %gather_fusion = bf16[32,256,256]{2,1,0:T(8,128)(2,1)} fusion(bf16[32,256,256]{2,1,0:T(8,128)(2,1)} %bitcast.59, s32[1024]{0:T(1024)S(1)} %pad_clamp_fusion), kind=kCustom, calls=%fused_computation | custom fusion | bytes 8388736 | tf_op jit(solution)/shard_map/jit(_take)/gather | solution.py:61
  196.7 6.3 %copy.20 = bf16[16,2,256,256]{2,3,1,0:T(8,128)(2,1)} copy(bf16[16,2,256,256]{3,2,1,0:T(8,128)(2,1)} %bitcast.60) | data formatting | bytes 8388608 | tf_op jit(solution)/shard_map/jit(_take)/gather | solution.py:61
  203.1 4.9 %select_select_fusion = bf16[16,2,256,256]{2,3,1,0:T(8,128)(2,1)} fusion(bf16[16,2,256,256]{2,3,1,0:T(8,128)(2,1)} %copy.20, pred[16,2]{1,0:T(8,128)(4,1)S(1)} %copy.18, pred[16,2]{1,0:T(8,128)(4,1)S(1)} %copy.17), kind=kLoop, calls=%fused_computation.6 | loop fusion | flops 4194304 | bytes 8388672 | tf_op jit(solution)/shard_map/jit(_where)/select_n | solution.py:63
  207.9 0.0 copy-start.1
  207.9 11.5 %all-to-all-start = ((bf16[16,2,256,256]{2,3,1,0:T(8,128)(2,1)}), bf16[16,2,256,256]{2,3,1,0:T(8,128)(2,1)}, u32[]{:S(2)}, u32[]{:S(2)}) async-start(bf16[16,2,256,256]{2,3,1,0:T(8,128)(2,1)} %select_select_fusion), calls=%async_computation | async-start | bytes 8388608 | tf_op jit(solution)/shard_map/all_to_all | solution.py:64
  219.4 0.1 constant_dynamic-slice_fusion.1
  219.5 0.6 fusion.44
  222.7 0.1 fusion.16
  222.8 0.0 copy-done.1
  222.8 3.5 %collective-permute-start = (bf16[256,256]{0,1:T(8,128)(2,1)S(1)}, bf16[256,256]{0,1:T(8,128)(2,1)S(1)}, u32[]{:S(2)}, u32[]{:S(2)}) collective-permute-start(bf16[256,256]{0,1:T(8,128)(2,1)S(1)} %copy-done.1), channel_id=1, source_target_pairs={{0,1},{1,2},{2,3},{3,4},{4,5},{5,6},{6,7},{7,8},{8,9},{9,10},{10,1... | collective-permute-start | bytes 393224 | tf_op jit(solution)/shard_map/ppermute | solution.py:12
  226.4 1.4 add_add_fusion
  231.7 88.8 %collective-permute-done = bf16[256,256]{0,1:T(8,128)(2,1)S(1)} collective-permute-done((bf16[256,256]{0,1:T(8,128)(2,1)S(1)}, bf16[256,256]{0,1:T(8,128)(2,1)S(1)}, u32[]{:S(2)}, u32[]{:S(2)}) %collective-permute-start) | collective-permute-done | bytes 131104 | tf_op jit(solution)/shard_map/ppermute | solution.py:12
  320.5 0.0 all-gather.11.cloned.1.call-done
  320.6 3.4 %fusion.9 = bf16[32,4,8,128]{3,2,1,0:T(8,128)(2,1)S(1)} fusion(bf16[256,4096]{1,0:T(8,128)(2,1)S(1)} %copy-done, bf16[4096,512]{1,0:T(8,128)(2,1)} %all-gather.11.cloned.1.call-done), kind=kOutput, calls=%fused_computation.12 | convolution fusion | flops 1073872896 | bytes 6553600 | tf_op jit(solution)/shard_map/dot_general | solution.py:18
  324.0 0.0 all-to-all-done
  324.0 2.7 fusion.42
  326.8 1.2 fusion.2
  327.9 1.3 fusion
  329.3 1.8 fusion.13
  331.1 0.8 copy.24
  (16 shorter events, 0.2 us)
Async XLA Ops:
  6.5 49.9 %copy-start = (bf16[256,4096]{1,0:T(8,128)(2,1)S(1)}, bf16[256,4096]{1,0:T(8,128)(2,1)}, u32[]{:S(2)}) copy-start(bf16[256,4096]{1,0:T(8,128)(2,1)} %param.5) | copy-start | bytes 6291460
  6.5 95.5 %copy-start.2 = (s32[256,2]{0,1:T(2,128)S(1)}, s32[256,2]{0,1:T(2,128)}, u32[]{:S(2)}) copy-start(s32[256,2]{0,1:T(2,128)} %param.9) | copy-start | bytes 6148
  6.5 49.9 %all-gather.7.cloned.1.call-start = ((), (), s32[]{:S(2)}) async-start(), calls=%async_computation.2 | async-start | bytes 1114112 | tf_op jit(solution)/shard_map/all_gather | solution.py:39
  7.3 91.4 %all-gather.5.cloned.1.call-start = ((), (), s32[]{:S(2)}) async-start(), calls=%async_computation.1 | async-start | bytes 1114112 | tf_op jit(solution)/shard_map/all_gather | solution.py:38
  8.0 177.4 %all-gather.9.cloned.1.call-start = ((), (), s32[]{:S(2)}) async-start(), calls=%async_computation.3 | async-start | bytes 4325376 | tf_op jit(solution)/shard_map/all_gather | solution.py:48
  101.4 219.1 %all-gather.11.cloned.1.call-start = ((), (), s32[]{:S(2)}) async-start(), calls=%async_computation.4 | async-start | bytes 4456448 | tf_op jit(solution)/shard_map/all_gather | solution.py:37
  207.9 14.9 %copy-start.1 = (bf16[256,256]{0,1:T(8,128)(2,1)S(1)}, bf16[256,256]{0,1:T(8,128)(2,1)}, u32[]{:S(2)}) copy-start(bf16[256,256]{0,1:T(8,128)(2,1)} %pad_maximum_fusion.2) | copy-start | bytes 393220
  207.9 116.1 %all-to-all-start = ((bf16[16,2,256,256]{2,3,1,0:T(8,128)(2,1)}), bf16[16,2,256,256]{2,3,1,0:T(8,128)(2,1)}, u32[]{:S(2)}, u32[]{:S(2)}) async-start(bf16[16,2,256,256]{2,3,1,0:T(8,128)(2,1)} %select_select_fusion), calls=%async_computation | async-start | bytes 8388608 | tf_op jit(solution)/shard_map/all_to_all | solution.py:64
  222.8 97.6 %collective-permute-start = (bf16[256,256]{0,1:T(8,128)(2,1)S(1)}, bf16[256,256]{0,1:T(8,128)(2,1)S(1)}, u32[]{:S(2)}, u32[]{:S(2)}) collective-permute-start(bf16[256,256]{0,1:T(8,128)(2,1)S(1)} %copy-done.1), channel_id=1, source_target_pairs={{0,1},{1,2},{2,3},{3,4},{4,5},{5,6},{6,7},{7,8},{8,9},{9,10},{10,1... | collective-permute-start | bytes 393224 | tf_op jit(solution)/shard_map/ppermute | solution.py:12
Sparse Core Ops, SparseCore 0:
  9.5 46.9 all-gather.6
  58.6 40.0 all-gather.4
  101.7 83.5 all-gather.8
  187.3 84.5 all-gather.10
where the time goes:
time: 341 us; the launch traced here: 338 us
  waiting for transfers between devices  262 us (77%)
  local copies, waits for them, and re-layouts  22.5 us (7%)
  between operations  19.7 us (6%)
  starting transfers between devices  15.1 us (4%)
  matrix products  10.5 us (3%)
  other arithmetic  8.56 us (3%)
    ppermute x1, waiting for transfers between devices, from_behind(): return lax.ppermute(array, axis, pairs)  88.8 us
    all_gather x1, waiting for transfers between devices, per_device(): lax.all_gather(key_value, 'ctx', axis=0, tiled=True)  82.7 us
    all_gather x1, waiting for transfers between devices, per_device(): lax.all_gather(value_weight, 'fsdp', axis=0, tiled=True)  48.4 us
    all_gather x1, waiting for transfers between devices, per_device(): lax.all_gather(key_weight, 'fsdp', axis=0, tiled=True)  40.2 us
    all_to_all x1, starting transfers between devices, per_device(): lax.all_to_all(outgoing, 'fsdp', split_axis=0, concat_axis=0, tiled=True)  11.5 us
    gather x2, local copies, waits for them, and re-layouts, per_device(): jnp.take(candidates, (wanted // blocks_group).reshape(-1), axis=0)  11.3 us
    dot_general x3, matrix products, project_rows(): jnp.dot(tokens, weight_piece, preferred_element_type=jnp.float32)  7.53 us
  transfers between devices with their start and end apart: 6, of which 4 were waited for; matrix products, arithmetic and copies ran while one was open for 9% of the time, Pallas kernels for 0%

commit v1 on v0

v1 whole, which is shorter than its diff:
```python
import jax
import jax.numpy as jnp
from jax import lax
from jax.sharding import PartitionSpec as P

QH = 4


def from_behind(array, axis, by):
    peers = lax.axis_size(axis)
    pairs = [(i, i + by) for i in range(peers) if 0 <= i + by < peers]
    return lax.ppermute(array, axis, pairs)


def gather_rows(array, axis):
    peers = lax.axis_size(axis)
    spread = jnp.broadcast_to(array[None], (peers,) + array.shape)
    got = lax.all_to_all(spread, axis, split_axis=0, concat_axis=0, tiled=True)
    return got.reshape((peers * array.shape[0],) + array.shape[1:])


def swap_partner(array, axis):
    peers = lax.axis_size(axis)
    pairs = [(i, i ^ 1) for i in range(peers)]
    return lax.ppermute(array, axis, pairs)


def per_device(tokens, query_weight, key_weight, value_weight, chosen):
    token_rows = tokens.shape[0]
    head_width = key_weight.shape[1]
    lane_count = lax.axis_size("fsdp")
    lane_index = lax.axis_index("fsdp")
    group_index = lax.axis_index("ctx")
    blocks_group = lane_count // 2
    my_block = group_index * blocks_group + lane_index // 2
    global_index = group_index * lane_count + lane_index

    kv_weight = gather_rows(jnp.concatenate([key_weight, value_weight], axis=1), "fsdp")
    kv_f32 = jnp.dot(tokens, kv_weight, preferred_element_type=jnp.float32)
    key_value = kv_f32.astype(jnp.bfloat16)

    query_weight, key_value = lax.optimization_barrier((query_weight, key_value))

    candidates = lax.all_gather(key_value, "ctx", axis=0, tiled=True).reshape(
        -1, token_rows, 2 * head_width
    )
    before_pair = from_behind(key_value, ("ctx", "fsdp"), 1)
    own_block = jnp.concatenate([before_pair, key_value], axis=0)

    q_weight = gather_rows(query_weight, "fsdp")
    queries = jnp.dot(tokens, q_weight, preferred_element_type=jnp.float32)
    queries = queries.astype(jnp.bfloat16).reshape(token_rows, QH, head_width)

    queries, candidates = lax.optimization_barrier((queries, candidates))

    dest_block = group_index * blocks_group + jnp.arange(lane_count, dtype=jnp.int32) // 2
    dest_pick = chosen[dest_block, jnp.arange(lane_count, dtype=jnp.int32) % 2]
    outgoing = jnp.take(candidates, dest_pick // blocks_group, axis=0)
    incoming = lax.all_to_all(outgoing, "fsdp", split_axis=0, concat_axis=0, tiled=True)

    mine = lax.dynamic_index_in_dim(chosen, my_block, 0, keepdims=False)
    my_choice = lane_index % 2
    my_pick = jnp.where(my_choice == 0, mine[0], mine[1])
    place = my_pick % blocks_group * 2
    block_mine = lax.dynamic_slice_in_dim(incoming, place, 2, 0).reshape(
        2 * token_rows, 2 * head_width
    )
    block_partner = swap_partner(block_mine, "fsdp")

    key_rows = jnp.concatenate(
        [own_block[:, :head_width], block_mine[:, :head_width], block_partner[:, :head_width]],
        axis=0,
    )
    value_rows = jnp.concatenate(
        [own_block[:, head_width:], block_mine[:, head_width:], block_partner[:, head_width:]],
        axis=0,
    )
    scores = jnp.einsum(
        "qhd,kd->hqk", queries, key_rows, preferred_element_type=jnp.float32
    ) * head_width ** (-0.5)
    window_rows = own_block.shape[0]
    pick_rows = block_mine.shape[0]
    row_index = jnp.arange(token_rows, dtype=jnp.int32)
    column = jnp.arange(window_rows, dtype=jnp.int32)
    causal = (column[None, :] <= row_index[:, None] + token_rows) & (
        (column[None, :] >= token_rows) | (global_index > 0)
    )
    first_ok = mine[0] < my_block - 1
    second_ok = (mine[1] < my_block - 1) & (mine[1] != mine[0])
    mine_ok = jnp.where(my_choice == 0, first_ok, second_ok)
    partner_ok = jnp.where(my_choice == 0, second_ok, first_ok)
    visible = jnp.concatenate(
        [
            causal,
            jnp.broadcast_to(mine_ok, (token_rows, pick_rows)),
            jnp.broadcast_to(partner_ok, (token_rows, pick_rows)),
        ],
        axis=1,
    )
    scores = jnp.where(visible[None], scores, -jnp.inf)
    highest = jnp.max(scores, axis=2, keepdims=True)
    probs = jnp.exp(scores - highest)
    denominator = jnp.sum(probs, axis=2, keepdims=True)
    mixed = (
        jnp.einsum(
            "hqk,kd->hqd",
            probs.astype(jnp.bfloat16),
            value_rows,
            preferred_element_type=jnp.float32,
        )
        / denominator
    )
    return jnp.transpose(mixed, (1, 0, 2)).reshape(token_rows, -1).astype(jnp.bfloat16)


def solution(mesh):
    return jax.shard_map(
        per_device,
        mesh=mesh,
        in_specs=(P(("ctx", "fsdp"), None), P("fsdp", None), P("fsdp", None), P("fsdp", None), P()),
        out_specs=P(("ctx", "fsdp"), None),
        check_vma=False,
    )
```

time: 341 us -> 268 us (0.79)
  waiting for transfers between devices: 262 us -> 132 us
  blocking collectives: 0 us -> 62 us
    all_to_all x0 -> x1, waiting for transfers between devices: none -> 90.7 us  [gather_rows(): got = lax.all_to_all(spread, axis, split_axis=0, concat_axis=0, tiled=True)]
    all_gather x3 -> x0, waiting for transfers between devices: 88.6 us -> none  [the longest x1 48.4 us: per_device(): lax.all_gather(value_weight, 'fsdp', axis=0, tiled=True)]
    all_gather x1, waiting for transfers between devices: 82.7 us -> 0.02 us  [per_device(): lax.all_gather(key_value, 'ctx', axis=0, tiled=True)]
    all_to_all x0 -> x1, blocking collectives: none -> 62 us  [gather_rows(): got = lax.all_to_all(spread, axis, split_axis=0, concat_axis=0, tiled=True)]
    ppermute x1, waiting for transfers between devices: 88.8 us -> 37.8 us  [from_behind(): return lax.ppermute(array, axis, pairs)]
    optimization_barrier x0 -> x1, local copies, waits for them, and re-layouts: none -> 7.51 us  [per_device(): queries, candidates = lax.optimization_barrier((queries, candidates))]
    reshape x3 -> x1, local copies, waits for them, and re-layouts: 6.57 us -> 0.14 us  [per_device(): lax.dynamic_slice_in_dim(incoming, place, 2, 0)]
    gather x2, local copies, waits for them, and re-layouts: 11.3 us -> 4.87 us  [the longest x1 4.19 us: per_device(): outgoing = jnp.take(candidates, dest_pick // blocks_group, axis=0)]
  transfers between devices with their start and end apart: 6 -> 5, of which waited for: 4 -> 4; matrix products, arithmetic and copies ran while one was open for 9% -> 2% of each run, Pallas kernels for 0% -> 0%
where the time goes in v1:
time: 268 us; the launch traced here: 267 us
  waiting for transfers between devices  132 us (49%)
  blocking collectives  62 us (23%)
  local copies, waits for them, and re-layouts  23.2 us (9%)
  starting transfers between devices  17.5 us (7%)
  between operations  17.2 us (6%)
  matrix products  7.86 us (3%)
  other arithmetic  7.23 us (3%)
    all_to_all x1, waiting for transfers between devices, gather_rows(): got = lax.all_to_all(spread, axis, split_axis=0, concat_axis=0, tiled=True)  90.7 us
    all_to_all x1, blocking collectives, gather_rows(): got = lax.all_to_all(spread, axis, split_axis=0, concat_axis=0, tiled=True)  62 us
    ppermute x1, waiting for transfers between devices, from_behind(): return lax.ppermute(array, axis, pairs)  37.8 us
    optimization_barrier x1, local copies, waits for them, and re-layouts, per_device(): queries, candidates = lax.optimization_barrier((queries, candidates))  7.51 us
    unnamed x10, local copies, waits for them, and re-layouts  5.57 us
    all_to_all x1, starting transfers between devices, per_device(): lax.all_to_all(outgoing, 'fsdp', split_axis=0, concat_axis=0, tiled=True)  5.4 us
  transfers between devices with their start and end apart: 5, of which 4 were waited for; matrix products, arithmetic and copies ran while one was open for 2% of the time, Pallas kernels for 0%

profile of v1, /device:TPU:7, one launch (start us, length us, event | category | flops | bytes accessed | tf_op | source)
XLA Modules:
  0.0 267.1 jit_solution(13137453949653050163)
XLA Ops:
  6.5 0.0 copy-start
  6.5 1.0 pad_maximum_fusion
  7.6 0.2 broadcast_in_dim.51
  7.8 0.0 copy-start.3
  7.8 62.0 %all_to_all.15 = bf16[16,256,256]{2,1,0:T(8,128)(2,1)S(1)} all-to-all(bf16[16,256,256]{2,1,0:T(8,128)(2,1)S(1)} %broadcast_in_dim.51), channel_id=1, replica_groups=mesh['ctx'=32,'fsdp'=16] {'fsdp'}, dimensions={0} | all-to-all | bytes 4194304 | tf_op jit(solution)/shard_map/all_to_all | solution.py:18
  69.7 0.0 copy-done
  69.7 1.4 fusion.9
  71.2 0.0 copy-done.3
  71.2 2.4 broadcast_in_dim.53
  73.5 0.0 copy-start.1
  73.5 4.6 %all-to-all-start.1 = ((bf16[16,256,512]{2,1,0:T(8,128)(2,1)}), bf16[16,256,512]{2,1,0:T(8,128)(2,1)}, u32[]{:S(2)}, u32[]{:S(2)}) async-start(bf16[16,256,512]{2,1,0:T(8,128)(2,1)} %broadcast_in_dim.53), calls=%async_computation.1 | async-start | bytes 8388608 | tf_op jit(solution)/shard_map/all_to_all | solution.py:18
  78.1 0.0 all-gather.2.cloned.1.call-start
  78.2 0.7 all-gather.2.cloned.1.call-update
  78.9 0.0 copy-done.1
  78.9 0.7 gather_fusion
  79.7 90.7 %all-to-all-done.1 = bf16[16,256,512]{2,1,0:T(8,128)(2,1)} async-done(((bf16[16,256,512]{2,1,0:T(8,128)(2,1)}), bf16[16,256,512]{2,1,0:T(8,128)(2,1)}, u32[]{:S(2)}, u32[]{:S(2)}) %all-to-all-start.1) | async-done | bytes 4194336 | tf_op jit(solution)/shard_map/all_to_all | solution.py:18
  170.4 3.5 %convolution_convert_fusion = bf16[512,256]{1,0:T(8,128)(2,1)S(1)} fusion(bf16[4096,512]{1,0:T(8,128)(2,1)} %bitcast.5, bf16[256,4096]{1,0:T(8,128)(2,1)S(1)} %copy-done), kind=kOutput, calls=%fused_computation.12 | convolution fusion | flops 1073872896 | bytes 6553600 | tf_op jit(solution)/shard_map/dot_general | solution.py:51
  173.9 0.0 all-gather.2.cloned.1.call-done
  173.9 5.5 %copy.21 = bf16[32,8,32,256]{3,2,1,0:T(8,128)(2,1)} copy(bf16[32,8,32,256]{3,1,2,0:T(8,128)(2,1)} %bitcast.65) | data formatting | bytes 8388608
  179.4 7.5 %copy.10 = bf16[32,256,256]{2,1,0:T(8,128)(2,1)} copy(bf16[32,256,256]{1,0,2:T(8,128)(2,1)} %bitcast.64) | data formatting | bytes 8388608 | tf_op jit(solution)/shard_map/optimization_barrier | solution.py:54
  187.0 4.2 %gather_fusion.1 = bf16[16,256,256]{2,1,0:T(8,128)(2,1)} fusion(bf16[32,256,256]{2,1,0:T(8,128)(2,1)} %copy.10, s32[1024]{0:T(1024)S(1)} %pad_clamp_fusion), kind=kCustom, calls=%fused_computation.1 | custom fusion | bytes 4194368 | tf_op jit(solution)/shard_map/jit(_take)/gather | solution.py:58
  191.1 0.0 copy-start.2
  191.1 3.2 %broadcast_select_fusion = bf16[16,256,256]{2,1,0:T(8,128)(2,1)} fusion(bf16[16,256,256]{2,1,0:T(8,128)(2,1)} %gather_fusion.1, pred[16]{0:T(512)(128)(4,1)S(1)} %compare_and_fusion), kind=kLoop, calls=%fused_computation.9 | loop fusion | flops 1048576 | bytes 4194320 | tf_op jit(solution)/shard_map/jit(_take)/select_n | solution.py:58
  194.4 5.4 %all-to-all-start.2 = ((bf16[16,256,256]{2,1,0:T(8,128)(2,1)}), bf16[16,256,256]{2,1,0:T(8,128)(2,1)}, u32[]{:S(2)}, u32[]{:S(2)}) async-start(bf16[16,256,256]{2,1,0:T(8,128)(2,1)} %broadcast_select_fusion), calls=%async_computation.2 | async-start | bytes 4194304 | tf_op jit(solution)/shard_map/all_to_all | solution.py:59
  199.8 0.1 constant_dynamic-slice_fusion.1
  199.8 0.5 fusion.42
  202.9 0.1 fusion.16
  203.0 0.0 copy-done.2
  203.0 3.5 %collective-permute-start = (bf16[256,256]{0,1:T(8,128)(2,1)S(1)}, bf16[256,256]{0,1:T(8,128)(2,1)S(1)}, u32[]{:S(2)}, u32[]{:S(2)}) collective-permute-start(bf16[256,256]{0,1:T(8,128)(2,1)S(1)} %copy-done.2), channel_id=1, source_target_pairs={{0,1},{1,2},{2,3},{3,4},{4,5},{5,6},{6,7},{7,8},{8,9},{9,10},{10,1... | collective-permute-start | bytes 393224 | tf_op jit(solution)/shard_map/ppermute | solution.py:12
  206.6 1.4 add_add_fusion
  209.2 37.8 %collective-permute-done = bf16[256,256]{0,1:T(8,128)(2,1)S(1)} collective-permute-done((bf16[256,256]{0,1:T(8,128)(2,1)S(1)}, bf16[256,256]{0,1:T(8,128)(2,1)S(1)}, u32[]{:S(2)}, u32[]{:S(2)}) %collective-permute-start) | collective-permute-done | bytes 131104 | tf_op jit(solution)/shard_map/ppermute | solution.py:12
  247.0 1.8 all-to-all-done.2
  248.8 1.0 constant_dynamic-slice_fusion
  249.8 0.1 copy.19
  249.9 4.0 %collective-permute-start.1 = (bf16[512,256]{0,1:T(8,128)(2,1)S(1)}, bf16[512,256]{0,1:T(8,128)(2,1)S(1)}, u32[]{:S(2)}, u32[]{:S(2)}) collective-permute-start(bf16[512,256]{0,1:T(8,128)(2,1)S(1)} %copy.19), channel_id=1, source_target_pairs={{0,1},{1,0},{2,3},{3,2},{4,5},{5,4},{6,7},{7,6},{8,9},{9,8},{10,11... | collective-permute-start | bytes 786440 | tf_op jit(solution)/shard_map/ppermute | solution.py:25
  254.0 1.1 collective-permute-done.1
  255.1 1.2 fusion.2
  256.2 1.3 fusion
  257.6 1.8 fusion.13
  259.4 0.8 copy.15
  (15 shorter events, 0.2 us)
Async XLA Ops:
  6.5 63.2 %copy-start = (bf16[256,4096]{1,0:T(8,128)(2,1)S(1)}, bf16[256,4096]{1,0:T(8,128)(2,1)}, u32[]{:S(2)}) copy-start(bf16[256,4096]{1,0:T(8,128)(2,1)} %param.5) | copy-start | bytes 6291460
  7.8 63.4 %copy-start.3 = (bf16[256,512]{1,0:T(8,128)(2,1)S(1)}, bf16[256,512]{1,0:T(8,128)(2,1)}, u32[]{:S(2)}) copy-start(bf16[256,512]{1,0:T(8,128)(2,1)} %param.6) | copy-start | bytes 786436
  73.5 5.4 %copy-start.1 = (s32[256,2]{0,1:T(2,128)S(1)}, s32[256,2]{0,1:T(2,128)}, u32[]{:S(2)}) copy-start(s32[256,2]{0,1:T(2,128)} %param.9) | copy-start | bytes 6148
  73.5 96.8 %all-to-all-start.1 = ((bf16[16,256,512]{2,1,0:T(8,128)(2,1)}), bf16[16,256,512]{2,1,0:T(8,128)(2,1)}, u32[]{:S(2)}, u32[]{:S(2)}) async-start(bf16[16,256,512]{2,1,0:T(8,128)(2,1)} %broadcast_in_dim.53), calls=%async_computation.1 | async-start | bytes 8388608 | tf_op jit(solution)/shard_map/all_to_all | solution.py:18
  78.1 95.8 %all-gather.2.cloned.1.call-start = ((), (), s32[]{:S(2)}) async-start(), calls=%async_computation.3 | async-start | bytes 4325376 | tf_op jit(solution)/shard_map/all_gather | solution.py:44
  191.1 11.9 %copy-start.2 = (bf16[256,256]{0,1:T(8,128)(2,1)S(1)}, bf16[256,256]{0,1:T(8,128)(2,1)}, u32[]{:S(2)}) copy-start(bf16[256,256]{0,1:T(8,128)(2,1)} %fusion.9) | copy-start | bytes 393220
  194.4 54.5 %all-to-all-start.2 = ((bf16[16,256,256]{2,1,0:T(8,128)(2,1)}), bf16[16,256,256]{2,1,0:T(8,128)(2,1)}, u32[]{:S(2)}, u32[]{:S(2)}) async-start(bf16[16,256,256]{2,1,0:T(8,128)(2,1)} %broadcast_select_fusion), calls=%async_computation.2 | async-start | bytes 4194304 | tf_op jit(solution)/shard_map/all_to_all | solution.py:59
  203.0 44.0 %collective-permute-start = (bf16[256,256]{0,1:T(8,128)(2,1)S(1)}, bf16[256,256]{0,1:T(8,128)(2,1)S(1)}, u32[]{:S(2)}, u32[]{:S(2)}) collective-permute-start(bf16[256,256]{0,1:T(8,128)(2,1)S(1)} %copy-done.2), channel_id=1, source_target_pairs={{0,1},{1,2},{2,3},{3,4},{4,5},{5,6},{6,7},{7,8},{8,9},{9,10},{10,1... | collective-permute-start | bytes 393224 | tf_op jit(solution)/shard_map/ppermute | solution.py:12
  249.9 5.1 %collective-permute-start.1 = (bf16[512,256]{0,1:T(8,128)(2,1)S(1)}, bf16[512,256]{0,1:T(8,128)(2,1)S(1)}, u32[]{:S(2)}, u32[]{:S(2)}) collective-permute-start(bf16[512,256]{0,1:T(8,128)(2,1)S(1)} %copy.19), channel_id=1, source_target_pairs={{0,1},{1,0},{2,3},{3,2},{4,5},{5,4},{6,7},{7,6},{8,9},{9,8},{10,11... | collective-permute-start | bytes 786440 | tf_op jit(solution)/shard_map/ppermute | solution.py:25
Sparse Core Ops, SparseCore 0:
  82.0 85.1 all-gather.1

commit v2 on v1

--- a/solution.py
+++ b/solution.py
@@ -19,6 +19,37 @@
     return got.reshape((peers * array.shape[0],) + array.shape[1:])
 
 
+def ring_gather_rows(array, axis):
+    peers = lax.axis_size(axis)
+    chips = peers // 2
+    shift_pairs = lambda by: [(i, (i + by) % peers) for i in range(peers)]
+    ahead = array
+    behind = array
+    from_ahead = []
+    from_behind_ = []
+    for step in range(chips // 2):
+        ahead = lax.ppermute(ahead, axis, shift_pairs(2))
+        from_ahead.append(ahead)
+        if step < chips // 2 - 1:
+            behind = lax.ppermute(behind, axis, shift_pairs(-2))
+            from_behind_.append(behind)
+    mine = jnp.stack(from_ahead[::-1] + [array] + from_behind_, axis=0)
+    other = lax.ppermute(mine, axis, [(i, i ^ 1) for i in range(peers)])
+    lane = lax.axis_index(axis)
+    start = (lane // 2 - chips // 2) % chips
+
+    def natural(stacked):
+        doubled = jnp.concatenate([stacked, stacked], axis=0)
+        return lax.dynamic_slice_in_dim(doubled, chips - start, chips, 0)
+
+    mine, other = natural(mine), natural(other)
+    core = lane % 2
+    first = jnp.where(core == 0, mine, other)
+    second = jnp.where(core == 0, other, mine)
+    full = jnp.stack([first, second], axis=1)
+    return full.reshape((peers * array.shape[0],) + array.shape[1:])
+
+
 def swap_partner(array, axis):
     peers = lax.axis_size(axis)
     pairs = [(i, i ^ 1) for i in range(peers)]
@@ -35,27 +66,26 @@
     my_block = group_index * blocks_group + lane_index // 2
     global_index = group_index * lane_count + lane_index
 
-    kv_weight = gather_rows(jnp.concatenate([key_weight, value_weight], axis=1), "fsdp")
+    kv_weight = lax.all_gather(
+        jnp.concatenate([key_weight, value_weight], axis=1), "fsdp", axis=0, tiled=True
+    )
     kv_f32 = jnp.dot(tokens, kv_weight, preferred_element_type=jnp.float32)
     key_value = kv_f32.astype(jnp.bfloat16)
 
-    query_weight, key_value = lax.optimization_barrier((query_weight, key_value))
-
-    candidates = lax.all_gather(key_value, "ctx", axis=0, tiled=True).reshape(
-        -1, token_rows, 2 * head_width
-    )
+    candidates = lax.all_gather(key_value[None], "ctx", axis=0, tiled=True)
     before_pair = from_behind(key_value, ("ctx", "fsdp"), 1)
     own_block = jnp.concatenate([before_pair, key_value], axis=0)
 
-    q_weight = gather_rows(query_weight, "fsdp")
+    query_weight, key_value = lax.optimization_barrier((query_weight, key_value))
+    q_weight = ring_gather_rows(query_weight, "fsdp")
     queries = jnp.dot(tokens, q_weight, preferred_element_type=jnp.float32)
     queries = queries.astype(jnp.bfloat16).reshape(token_rows, QH, head_width)
 
-    queries, candidates = lax.optimization_barrier((queries, candidates))
+    queries, chosen = lax.optimization_barrier((queries, chosen))
 
     dest_block = group_index * blocks_group + jnp.arange(lane_count, dtype=jnp.int32) // 2
     dest_pick = chosen[dest_block, jnp.arange(lane_count, dtype=jnp.int32) % 2]
-    outgoing = jnp.take(candidates, dest_pick // blocks_group, axis=0)
+    outgoing = jnp.take(candidates, dest_pick // blocks_group, axis=0, mode="clip")
     incoming = lax.all_to_all(outgoing, "fsdp", split_axis=0, concat_axis=0, tiled=True)
 
     mine = lax.dynamic_index_in_dim(chosen, my_block, 0, keepdims=False)

time: 268 us -> 230 us (0.86)
  blocking collectives: 62 us -> 0 us
  starting transfers between devices: 17.5 us -> 47.8 us
  waiting for transfers between devices: 132 us -> 122 us
    all_to_all x1 -> x0, waiting for transfers between devices: 90.7 us -> none  [gather_rows(): got = lax.all_to_all(spread, axis, split_axis=0, concat_axis=0, tiled=True)]
    all_gather x1 -> x2, waiting for transfers between devices: 0.02 us -> 62.6 us  [the longest x1 49.4 us: per_device(): lax.all_gather(jnp.concatenate([key_weight, value_weight], axis=1), 'fsdp...]
    all_to_all x1 -> x0, blocking collectives: 62 us -> none  [gather_rows(): got = lax.all_to_all(spread, axis, split_axis=0, concat_axis=0, tiled=True)]
    ppermute x0 -> x8, starting transfers between devices: none -> 27.6 us  [the longest x3 13.7 us: ring_gather_rows(): behind = lax.ppermute(behind, axis, shift_pairs(-2))]
    ppermute x0 -> x8, waiting for transfers between devices: none -> 16.2 us  [the longest x4 16.2 us: ring_gather_rows(): ahead = lax.ppermute(ahead, axis, shift_pairs(2))]
    unnamed x10 -> x28, local copies, waits for them, and re-layouts: 5.57 us -> 13.8 us
    optimization_barrier x1 -> x0, local copies, waits for them, and re-layouts: 7.51 us -> none  [per_device(): queries, candidates = lax.optimization_barrier((queries, candidates))]
    ppermute x1, waiting for transfers between devices: 37.8 us -> 43.5 us  [from_behind(): return lax.ppermute(array, axis, pairs)]
  transfers between devices with their start and end apart: 5 -> 13, of which waited for: 4 -> 7; matrix products, arithmetic and copies ran while one was open for 2% -> 11% of each run, Pallas kernels for 0% -> 0%
where the time goes in v2:
time: 230 us; the launch traced here: 228 us
  waiting for transfers between devices  122 us (53%)
  starting transfers between devices  47.8 us (21%)
  local copies, waits for them, and re-layouts  23.8 us (10%)
  between operations  17.6 us (8%)
  other arithmetic  9.61 us (4%)
  matrix products  6.9 us (3%)
    all_gather x1, waiting for transfers between devices, per_device(): lax.all_gather(jnp.concatenate([key_weight, value_weight], axis=1), 'fsdp...  49.4 us
    ppermute x1, waiting for transfers between devices, from_behind(): return lax.ppermute(array, axis, pairs)  43.5 us
    ppermute x4, waiting for transfers between devices, ring_gather_rows(): ahead = lax.ppermute(ahead, axis, shift_pairs(2))  16.2 us
    unnamed x28, local copies, waits for them, and re-layouts  13.8 us
    ppermute x3, starting transfers between devices, ring_gather_rows(): behind = lax.ppermute(behind, axis, shift_pairs(-2))  13.7 us
    all_gather x1, waiting for transfers between devices, per_device(): candidates = lax.all_gather(key_value[None], 'ctx', axis=0, tiled=True)  13.2 us
    all_to_all x1, starting transfers between devices, per_device(): lax.all_to_all(outgoing, 'fsdp', split_axis=0, concat_axis=0, tiled=True)  10.6 us
    ppermute x4, starting transfers between devices, ring_gather_rows(): ahead = lax.ppermute(ahead, axis, shift_pairs(2))  8.19 us
  transfers between devices with their start and end apart: 13, of which 7 were waited for; matrix products, arithmetic and copies ran while one was open for 11% of the time, Pallas kernels for 0%

profile of v2, /device:TPU:7, one launch (start us, length us, event | category | flops | bytes accessed | tf_op | source)
XLA Modules:
  0.0 228.1 jit_solution(8332170298167504349)
XLA Ops:
  6.5 1.7 pad_maximum_fusion.2
  8.2 0.0 all-gather.4.cloned.1.call-update
  8.3 0.0 all-gather.6.cloned.1.call-start
  8.3 49.4 %all-gather.4.cloned.1.call-done = bf16[4096,256]{1,0:T(8,128)(2,1)} async-done(((bf16[256,256]{1,0:T(8,128)(2,1)}), bf16[4096,256]{1,0:T(8,128)(2,1)}) %all-gather.4.cloned.1.call-update) | async-done | bytes 2097168 | tf_op jit(solution)/shard_map/all_gather | solution.py:69
  57.7 0.0 copy-done
  57.7 3.0 %fusion.10 = bf16[256,256]{1,0:T(8,128)(2,1)} fusion(bf16[256,4096]{1,0:T(8,128)(2,1)S(1)} %copy-done, bf16[4096,256]{1,0:T(8,128)(2,1)} %all-gather.4.cloned.1.call-done), kind=kOutput, calls=%fused_computation.19 | convolution fusion | flops 536936448 | bytes 4325376 | tf_op jit(solution)/shard_map/dot_general | solution.py:72
  60.7 0.0 all-gather.6.cloned.1.call-update
  60.7 2.5 %collective-permute-start = (bf16[256,512]{1,0:T(8,128)(2,1)S(1)}, bf16[256,512]{1,0:T(8,128)(2,1)S(1)}, u32[]{:S(2)}, u32[]{:S(2)}) collective-permute-start(bf16[256,512]{1,0:T(8,128)(2,1)S(1)} %copy-done.2), channel_id=1, source_target_pairs={{0,2},{1,3},{2,4},{3,5},{4,6},{5,7},{6,8},{7,9},{8,10},{9,11},{10,... | collective-permute-start | bytes 786440 | tf_op jit(solution)/shard_map/ppermute | solution.py:31
  63.2 8.3 %collective-permute-done = bf16[256,512]{1,0:T(8,128)(2,1)S(1)} collective-permute-done((bf16[256,512]{1,0:T(8,128)(2,1)S(1)}, bf16[256,512]{1,0:T(8,128)(2,1)S(1)}, u32[]{:S(2)}, u32[]{:S(2)}) %collective-permute-start) | collective-permute-done | bytes 262176 | tf_op jit(solution)/shard_map/ppermute | solution.py:31
  71.5 1.9 collective-permute-start.1
  73.4 4.6 %collective-permute-start.4 = (bf16[256,512]{1,0:T(8,128)(2,1)S(1)}, bf16[256,512]{1,0:T(8,128)(2,1)S(1)}, u32[]{:S(2)}, u32[]{:S(2)}) collective-permute-start(bf16[256,512]{1,0:T(8,128)(2,1)S(1)} %copy-done.2), channel_id=1, source_target_pairs={{0,14},{1,15},{2,0},{3,1},{4,2},{5,3},{6,4},{7,5},{8,6},{9,7},{10,... | collective-permute-start | bytes 786440 | tf_op jit(solution)/shard_map/ppermute | solution.py:34
  78.0 3.4 %collective-permute-done.1 = bf16[256,512]{1,0:T(8,128)(2,1)S(1)} collective-permute-done((bf16[256,512]{1,0:T(8,128)(2,1)S(1)}, bf16[256,512]{1,0:T(8,128)(2,1)S(1)}, u32[]{:S(2)}, u32[]{:S(2)}) %collective-permute-start.1) | collective-permute-done | bytes 262176 | tf_op jit(solution)/shard_map/ppermute | solution.py:31
  81.4 1.9 collective-permute-start.2
  83.3 0.0 collective-permute-done.4
  83.3 4.6 %collective-permute-start.5 = (bf16[256,512]{1,0:T(8,128)(2,1)S(1)}, bf16[256,512]{1,0:T(8,128)(2,1)S(1)}, u32[]{:S(2)}, u32[]{:S(2)}) collective-permute-start(bf16[256,512]{1,0:T(8,128)(2,1)S(1)} %collective-permute-done.4), channel_id=1, source_target_pairs={{0,14},{1,15},{2,0},{3,1},{4,2},{5,3},{6,4},{7,5},{8,6},{9,7},{10,... | collective-permute-start | bytes 786440 | tf_op jit(solution)/shard_map/ppermute | solution.py:34
  87.9 2.5 %collective-permute-done.2 = bf16[256,512]{1,0:T(8,128)(2,1)S(1)} collective-permute-done((bf16[256,512]{1,0:T(8,128)(2,1)S(1)}, bf16[256,512]{1,0:T(8,128)(2,1)S(1)}, u32[]{:S(2)}, u32[]{:S(2)}) %collective-permute-start.2) | collective-permute-done | bytes 262176 | tf_op jit(solution)/shard_map/ppermute | solution.py:31
  90.4 1.9 collective-permute-start.3
  92.3 0.0 collective-permute-done.5
  92.3 4.6 %collective-permute-start.6 = (bf16[256,512]{1,0:T(8,128)(2,1)S(1)}, bf16[256,512]{1,0:T(8,128)(2,1)S(1)}, u32[]{:S(2)}, u32[]{:S(2)}) collective-permute-start(bf16[256,512]{1,0:T(8,128)(2,1)S(1)} %collective-permute-done.5), channel_id=1, source_target_pairs={{0,14},{1,15},{2,0},{3,1},{4,2},{5,3},{6,4},{7,5},{8,6},{9,7},{10,... | collective-permute-start | bytes 786440 | tf_op jit(solution)/shard_map/ppermute | solution.py:34
  96.9 2.0 collective-permute-done.3
  98.9 0.9 bitcast_dynamic-update-slice_fusion.22
  99.8 0.8 bitcast_dynamic-update-slice_fusion.19
  100.6 0.9 bitcast_dynamic-update-slice_fusion.16
  101.5 0.8 bitcast_dynamic-update-slice_fusion.13
  102.3 0.8 bitcast_dynamic-update-slice_fusion.10
  103.2 0.9 bitcast_dynamic-update-slice_fusion.7
  104.0 0.9 bitcast_dynamic-update-slice_fusion.4
  104.9 0.0 collective-permute-done.6
  104.9 0.7 copy-done.4
  105.6 0.8 bitcast_dynamic-update-slice_fusion.1
  106.5 0.0 copy-done.5
  106.5 5.7 %collective-permute-start.7 = (bf16[8,256,512]{2,1,0:T(8,128)(2,1)}, bf16[8,256,512]{2,1,0:T(8,128)(2,1)}, u32[]{:S(2)}, u32[]{:S(2)}) collective-permute-start(bf16[8,256,512]{2,1,0:T(8,128)(2,1)} %get-tuple-element.17), channel_id=1, source_target_pairs={{0,1},{1,0},{2,3},{3,2},{4,5},{5,4},{6,7},{7,6},{8,9},{9,8},{10,11... | collective-permute-start | bytes 6291464 | tf_op jit(solution)/shard_map/ppermute | solution.py:37
  112.2 1.7 bitcast_dynamic-update-slice_fusion.23
  113.9 1.7 bitcast_dynamic-update-slice_fusion.20
  115.6 0.7 bitcast_dynamic-update-slice_fusion.17
  116.3 0.7 bitcast_dynamic-update-slice_fusion.14
  117.0 0.7 bitcast_dynamic-update-slice_fusion.11
  117.8 0.7 bitcast_dynamic-update-slice_fusion.8
  118.5 0.8 bitcast_dynamic-update-slice_fusion.5
  119.3 1.7 bitcast_dynamic-update-slice_fusion.2
  120.9 0.0 collective-permute-done.7
  120.9 4.6 %select_bitcast_fusion.1 = (bf16[8,1,256,512]{3,2,1,0:T(8,128)(2,1)S(1)}, bf16[8,1,256,512]{3,2,1,0:T(8,128)(2,1)S(1)}) fusion(pred[]{:T(512)S(6)} %eq.14, bf16[16,256,512]{2,1,0:T(8,128)(2,1)} %bitcast_dynamic-update-slice_fusion.2, s32[]{:T(128)S(6)} %select_n.118, bf16[8,256,512]{2,1,0:T(8,128)(2,1)} %collective-permute-done.7), kind=kLoop, calls=%fused_computation.14 | loop fusion | flops 4194304 | bytes 8388613 | tf_op jit(solution)/shard_map/stack | solution.py:49
  125.5 0.4 pad_maximum_fusion
  125.9 0.0 copy-start.1
  125.9 1.3 convolution_convert_fusion
  127.2 0.0 copy-done.1
  127.2 0.7 gather_fusion
  127.9 13.2 %all-gather.6.cloned.1.call-done = bf16[8192,256]{1,0:T(8,128)(2,1)} async-done(((bf16[256,256]{1,0:T(8,128)(2,1)}), bf16[8192,256]{1,0:T(8,128)(2,1)}) %all-gather.6.cloned.1.call-update) | async-done | bytes 4194320 | tf_op jit(solution)/shard_map/all_gather | solution.py:75
  141.2 4.3 %gather_fusion.1 = bf16[16,256,256]{2,1,0:T(8,128)(2,1)} fusion(bf16[32,256,256]{2,1,0:T(8,128)(2,1)} %bitcast.101, s32[1024]{0:T(1024)S(1)} %pad_clamp_fusion), kind=kCustom, calls=%fused_computation.1 | custom fusion | bytes 4194368 | tf_op jit(solution)/shard_map/jit(_take)/gather | solution.py:88
  145.5 10.6 %all-to-all-start = ((bf16[16,256,256]{2,1,0:T(8,128)(2,1)}), bf16[16,256,256]{2,1,0:T(8,128)(2,1)}, u32[]{:S(2)}, u32[]{:S(2)}) async-start(bf16[16,256,256]{2,1,0:T(8,128)(2,1)} %gather_fusion.1), calls=%async_computation | async-start | bytes 4194304 | tf_op jit(solution)/shard_map/all_to_all | solution.py:89
  156.1 3.5 %collective-permute-start.8 = (bf16[256,256]{1,0:T(8,128)(2,1)S(1)}, bf16[256,256]{1,0:T(8,128)(2,1)S(1)}, u32[]{:S(2)}, u32[]{:S(2)}) collective-permute-start(bf16[256,256]{1,0:T(8,128)(2,1)S(1)} %copy-done.6), channel_id=1, source_target_pairs={{0,1},{1,2},{2,3},{3,4},{4,5},{5,6},{6,7},{7,8},{8,9},{9,10},{10,1... | collective-permute-start | bytes 393224 | tf_op jit(solution)/shard_map/ppermute | solution.py:12
  159.6 0.1 fusion.17
  159.8 43.5 %collective-permute-done.8 = bf16[256,256]{1,0:T(8,128)(2,1)S(1)} collective-permute-done((bf16[256,256]{1,0:T(8,128)(2,1)S(1)}, bf16[256,256]{1,0:T(8,128)(2,1)S(1)}, u32[]{:S(2)}, u32[]{:S(2)}) %collective-permute-start.8) | collective-permute-done | bytes 131104 | tf_op jit(solution)/shard_map/ppermute | solution.py:12
  203.2 0.1 constant_dynamic-slice_fusion.1
  203.3 0.6 fusion.46
  207.8 0.0 all-to-all-done
  207.8 1.0 constant_dynamic-slice_fusion
  208.8 6.1 %collective-permute-start.9 = (bf16[512,256]{1,0:T(8,128)(2,1)S(1)}, bf16[512,256]{1,0:T(8,128)(2,1)S(1)}, u32[]{:S(2)}, u32[]{:S(2)}) collective-permute-start(bf16[512,256]{1,0:T(8,128)(2,1)S(1)} %bitcast.99), channel_id=1, source_target_pairs={{0,1},{1,0},{2,3},{3,2},{4,5},{5,4},{6,7},{7,6},{8,9},{9,8},{10,11... | collective-permute-start | bytes 786440 | tf_op jit(solution)/shard_map/ppermute | solution.py:56
  214.9 1.4 add_add_fusion
  216.4 0.0 collective-permute-done.9
  216.5 1.1 fusion.2
  217.6 1.3 fusion
  218.9 1.6 fusion.14
  220.5 0.8 copy.14
  (22 shorter events, 0.1 us)
Async XLA Ops:
  6.5 51.2 %copy-start = (bf16[256,4096]{1,0:T(8,128)(2,1)S(1)}, bf16[256,4096]{1,0:T(8,128)(2,1)}, u32[]{:S(2)}) copy-start(bf16[256,4096]{1,0:T(8,128)(2,1)} %param.5) | copy-start | bytes 6291460
  6.5 54.2 %copy-start.2 = (bf16[256,512]{1,0:T(8,128)(2,1)S(1)}, bf16[256,512]{1,0:T(8,128)(2,1)}, u32[]{:S(2)}) copy-start(bf16[256,512]{1,0:T(8,128)(2,1)} %param.6) | copy-start | bytes 786436
  6.5 51.2 %all-gather.4.cloned.1.call-start = ((), (), s32[]{:S(2)}) async-start(), calls=%async_computation.1 | async-start | bytes 2228224 | tf_op jit(solution)/shard_map/all_gather | solution.py:69
  8.3 132.9 %all-gather.6.cloned.1.call-start = ((), (), s32[]{:S(2)}) async-start(), calls=%async_computation.2 | async-start | bytes 4325376 | tf_op jit(solution)/shard_map/all_gather | solution.py:75
  60.7 10.8 %collective-permute-start = (bf16[256,512]{1,0:T(8,128)(2,1)S(1)}, bf16[256,512]{1,0:T(8,128)(2,1)S(1)}, u32[]{:S(2)}, u32[]{:S(2)}) collective-permute-start(bf16[256,512]{1,0:T(8,128)(2,1)S(1)} %copy-done.2), channel_id=1, source_target_pairs={{0,2},{1,3},{2,4},{3,5},{4,6},{5,7},{6,8},{7,9},{8,10},{9,11},{10,... | collective-permute-start | bytes 786440 | tf_op jit(solution)/shard_map/ppermute | solution.py:31
  71.5 9.9 %collective-permute-start.1 = (bf16[256,512]{1,0:T(8,128)(2,1)S(1)}, bf16[256,512]{1,0:T(8,128)(2,1)S(1)}, u32[]{:S(2)}, u32[]{:S(2)}) collective-permute-start(bf16[256,512]{1,0:T(8,128)(2,1)S(1)} %collective-permute-done), channel_id=1, source_target_pairs={{0,2},{1,3},{2,4},{3,5},{4,6},{5,7},{6,8},{7,9},{8,10},{9,11},{10,... | collective-permute-start | bytes 786440 | tf_op jit(solution)/shard_map/ppermute | solution.py:31
  73.4 9.9 %collective-permute-start.4 = (bf16[256,512]{1,0:T(8,128)(2,1)S(1)}, bf16[256,512]{1,0:T(8,128)(2,1)S(1)}, u32[]{:S(2)}, u32[]{:S(2)}) collective-permute-start(bf16[256,512]{1,0:T(8,128)(2,1)S(1)} %copy-done.2), channel_id=1, source_target_pairs={{0,14},{1,15},{2,0},{3,1},{4,2},{5,3},{6,4},{7,5},{8,6},{9,7},{10,... | collective-permute-start | bytes 786440 | tf_op jit(solution)/shard_map/ppermute | solution.py:34
  81.4 9.0 %collective-permute-start.2 = (bf16[256,512]{1,0:T(8,128)(2,1)S(1)}, bf16[256,512]{1,0:T(8,128)(2,1)S(1)}, u32[]{:S(2)}, u32[]{:S(2)}) collective-permute-start(bf16[256,512]{1,0:T(8,128)(2,1)S(1)} %collective-permute-done.1), channel_id=1, source_target_pairs={{0,2},{1,3},{2,4},{3,5},{4,6},{5,7},{6,8},{7,9},{8,10},{9,11},{10,... | collective-permute-start | bytes 786440 | tf_op jit(solution)/shard_map/ppermute | solution.py:31
  83.3 9.0 %collective-permute-start.5 = (bf16[256,512]{1,0:T(8,128)(2,1)S(1)}, bf16[256,512]{1,0:T(8,128)(2,1)S(1)}, u32[]{:S(2)}, u32[]{:S(2)}) collective-permute-start(bf16[256,512]{1,0:T(8,128)(2,1)S(1)} %collective-permute-done.4), channel_id=1, source_target_pairs={{0,14},{1,15},{2,0},{3,1},{4,2},{5,3},{6,4},{7,5},{8,6},{9,7},{10,... | collective-permute-start | bytes 786440 | tf_op jit(solution)/shard_map/ppermute | solution.py:34
  90.4 14.5 %copy-start.3 = (bf16[256,512]{1,0:T(8,128)(2,1)}, bf16[256,512]{1,0:T(8,128)(2,1)S(1)}, u32[]{:S(2)}) copy-start(bf16[256,512]{1,0:T(8,128)(2,1)S(1)} %collective-permute-done.2) | copy-start | bytes 786436
  90.4 8.5 %collective-permute-start.3 = (bf16[256,512]{1,0:T(8,128)(2,1)S(1)}, bf16[256,512]{1,0:T(8,128)(2,1)S(1)}, u32[]{:S(2)}, u32[]{:S(2)}) collective-permute-start(bf16[256,512]{1,0:T(8,128)(2,1)S(1)} %collective-permute-done.2), channel_id=1, source_target_pairs={{0,2},{1,3},{2,4},{3,5},{4,6},{5,7},{6,8},{7,9},{8,10},{9,11},{10,... | collective-permute-start | bytes 786440 | tf_op jit(solution)/shard_map/ppermute | solution.py:31
  92.3 12.6 %collective-permute-start.6 = (bf16[256,512]{1,0:T(8,128)(2,1)S(1)}, bf16[256,512]{1,0:T(8,128)(2,1)S(1)}, u32[]{:S(2)}, u32[]{:S(2)}) collective-permute-start(bf16[256,512]{1,0:T(8,128)(2,1)S(1)} %collective-permute-done.5), channel_id=1, source_target_pairs={{0,14},{1,15},{2,0},{3,1},{4,2},{5,3},{6,4},{7,5},{8,6},{9,7},{10,... | collective-permute-start | bytes 786440 | tf_op jit(solution)/shard_map/ppermute | solution.py:34
  98.9 7.6 %copy-start.5 = (bf16[256,512]{1,0:T(8,128)(2,1)}, bf16[256,512]{1,0:T(8,128)(2,1)S(1)}, u32[]{:S(2)}) copy-start(bf16[256,512]{1,0:T(8,128)(2,1)S(1)} %collective-permute-done.3) | copy-start | bytes 786436
  104.9 0.7 copy-start.4
  106.5 14.5 %collective-permute-start.7 = (bf16[8,256,512]{2,1,0:T(8,128)(2,1)}, bf16[8,256,512]{2,1,0:T(8,128)(2,1)}, u32[]{:S(2)}, u32[]{:S(2)}) collective-permute-start(bf16[8,256,512]{2,1,0:T(8,128)(2,1)} %get-tuple-element.17), channel_id=1, source_target_pairs={{0,1},{1,0},{2,3},{3,2},{4,5},{5,4},{6,7},{7,6},{8,9},{9,8},{10,11... | collective-permute-start | bytes 6291464 | tf_op jit(solution)/shard_map/ppermute | solution.py:37
  125.9 1.3 copy-start.1
  141.2 14.9 %copy-start.6 = (bf16[256,256]{1,0:T(8,128)(2,1)S(1)}, bf16[256,256]{1,0:T(8,128)(2,1)}, u32[]{:S(2)}) copy-start(bf16[256,256]{1,0:T(8,128)(2,1)} %fusion.10) | copy-start | bytes 393220
  145.5 62.4 %all-to-all-start = ((bf16[16,256,256]{2,1,0:T(8,128)(2,1)}), bf16[16,256,256]{2,1,0:T(8,128)(2,1)}, u32[]{:S(2)}, u32[]{:S(2)}) async-start(bf16[16,256,256]{2,1,0:T(8,128)(2,1)} %gather_fusion.1), calls=%async_computation | async-start | bytes 4194304 | tf_op jit(solution)/shard_map/all_to_all | solution.py:89
  156.1 47.2 %collective-permute-start.8 = (bf16[256,256]{1,0:T(8,128)(2,1)S(1)}, bf16[256,256]{1,0:T(8,128)(2,1)S(1)}, u32[]{:S(2)}, u32[]{:S(2)}) collective-permute-start(bf16[256,256]{1,0:T(8,128)(2,1)S(1)} %copy-done.6), channel_id=1, source_target_pairs={{0,1},{1,2},{2,3},{3,4},{4,5},{5,6},{6,7},{7,8},{8,9},{9,10},{10,1... | collective-permute-start | bytes 393224 | tf_op jit(solution)/shard_map/ppermute | solution.py:12
  208.8 7.6 %collective-permute-start.9 = (bf16[512,256]{1,0:T(8,128)(2,1)S(1)}, bf16[512,256]{1,0:T(8,128)(2,1)S(1)}, u32[]{:S(2)}, u32[]{:S(2)}) collective-permute-start(bf16[512,256]{1,0:T(8,128)(2,1)S(1)} %bitcast.99), channel_id=1, source_target_pairs={{0,1},{1,0},{2,3},{3,2},{4,5},{5,4},{6,7},{7,6},{8,9},{9,8},{10,11... | collective-permute-start | bytes 786440 | tf_op jit(solution)/shard_map/ppermute | solution.py:56
Sparse Core Ops, SparseCore 0:
  9.5 48.1 all-gather.3
  60.9 80.2 all-gather.5

commit v3 on v2

--- a/solution.py
+++ b/solution.py
@@ -1,7 +1,7 @@
 import jax
 import jax.numpy as jnp
 from jax import lax
-from jax.sharding import PartitionSpec as P
+from jax.sharding import Mesh, PartitionSpec as P
 
 QH = 4
 
@@ -61,7 +61,7 @@
     head_width = key_weight.shape[1]
     lane_count = lax.axis_size("fsdp")
     lane_index = lax.axis_index("fsdp")
-    group_index = lax.axis_index("ctx")
+    group_index = lax.axis_index(("cy", "cx"))
     blocks_group = lane_count // 2
     my_block = group_index * blocks_group + lane_index // 2
     global_index = group_index * lane_count + lane_index
@@ -72,8 +72,11 @@
     kv_f32 = jnp.dot(tokens, kv_weight, preferred_element_type=jnp.float32)
     key_value = kv_f32.astype(jnp.bfloat16)
 
-    candidates = lax.all_gather(key_value[None], "ctx", axis=0, tiled=True)
-    before_pair = from_behind(key_value, ("ctx", "fsdp"), 1)
+    along_x = lax.all_gather(key_value[None], "cx", axis=0, tiled=True)
+    candidates = lax.all_gather(along_x[None], "cy", axis=0, tiled=True).reshape(
+        (-1,) + key_value.shape
+    )
+    before_pair = from_behind(key_value, ("cy", "cx", "fsdp"), 1)
     own_block = jnp.concatenate([before_pair, key_value], axis=0)
 
     query_weight, key_value = lax.optimization_barrier((query_weight, key_value))
@@ -143,11 +146,24 @@
     return jnp.transpose(mixed, (1, 0, 2)).reshape(token_rows, -1).astype(jnp.bfloat16)
 
 
+def split_ctx(mesh):
+    column = mesh.devices[:, 0]
+    coords = [getattr(device, "coords", None) for device in column]
+    if any(c is None for c in coords):
+        across = 1
+    else:
+        across = len({c[0] for c in coords})
+    groups, lanes = mesh.devices.shape
+    return Mesh(mesh.devices.reshape(groups // across, across, lanes), ("cy", "cx", "fsdp"))
+
+
 def solution(mesh):
+    split = split_ctx(mesh)
+    rows = P(("cy", "cx", "fsdp"), None)
     return jax.shard_map(
         per_device,
-        mesh=mesh,
-        in_specs=(P(("ctx", "fsdp"), None), P("fsdp", None), P("fsdp", None), P("fsdp", None), P()),
-        out_specs=P(("ctx", "fsdp"), None),
+        mesh=split,
+        in_specs=(rows, P("fsdp", None), P("fsdp", None), P("fsdp", None), P()),
+        out_specs=rows,
         check_vma=False,
     )

time: 230 us -> 220 us (0.957)
  waiting for transfers between devices: 122 us -> 105 us
  blocking collectives: 0 us -> 10.6 us
  starting transfers between devices: 47.8 us -> 42.9 us
    all_gather x1, waiting for transfers between devices: 13.2 us -> 0.02 us  [per_device(): lax.all_gather(along_x[None], 'cy', axis=0, tiled=True)]
    all_gather x0 -> x1, blocking collectives: none -> 10.6 us  [per_device(): along_x = lax.all_gather(key_value[None], 'cx', axis=0, tiled=True)]
    all_to_all x1, starting transfers between devices: 10.6 us -> 4.32 us  [per_device(): lax.all_to_all(outgoing, 'fsdp', split_axis=0, concat_axis=0, tiled=True)]
    ppermute x4, waiting for transfers between devices: 16.2 us -> 12.4 us  [ring_gather_rows(): ahead = lax.ppermute(ahead, axis, shift_pairs(2))]
    ppermute x1, starting transfers between devices: 5.67 us -> 9.05 us  [ring_gather_rows(): other = lax.ppermute(mine, axis, [(i, i ^ 1) for i in range(peers)])]
    unnamed x28 -> x26, local copies, waits for them, and re-layouts: 13.8 us -> 13.6 us
  transfers between devices with their start and end apart: 13 -> 13, of which waited for: 7 -> 6; matrix products, arithmetic and copies ran while one was open for 11% -> 12% of each run, Pallas kernels for 0% -> 0%
where the time goes in v3:
time: 220 us; the launch traced here: 217 us
  waiting for transfers between devices  105 us (48%)
  starting transfers between devices  42.9 us (20%)
  local copies, waits for them, and re-layouts  23.6 us (11%)
  between operations  17.5 us (8%)
  blocking collectives  10.6 us (5%)
  other arithmetic  9.59 us (4%)
  matrix products  7.89 us (4%)
    all_gather x1, waiting for transfers between devices, per_device(): lax.all_gather(jnp.concatenate([key_weight, value_weight], axis=1), 'fsdp...  49.4 us
    ppermute x1, waiting for transfers between devices, from_behind(): return lax.ppermute(array, axis, pairs)  43.5 us
    ppermute x3, starting transfers between devices, ring_gather_rows(): behind = lax.ppermute(behind, axis, shift_pairs(-2))  13.7 us
    unnamed x26, local copies, waits for them, and re-layouts  13.6 us
    ppermute x4, waiting for transfers between devices, ring_gather_rows(): ahead = lax.ppermute(ahead, axis, shift_pairs(2))  12.4 us
    all_gather x1, blocking collectives, per_device(): along_x = lax.all_gather(key_value[None], 'cx', axis=0, tiled=True)  10.6 us
    ppermute x1, starting transfers between devices, ring_gather_rows(): other = lax.ppermute(mine, axis, [(i, i ^ 1) for i in range(peers)])  9.05 us
    ppermute x4, starting transfers between devices, ring_gather_rows(): ahead = lax.ppermute(ahead, axis, shift_pairs(2))  8.19 us
  transfers between devices with their start and end apart: 13, of which 6 were waited for; matrix products, arithmetic and copies ran while one was open for 12% of the time, Pallas kernels for 0%

profile of v3, /device:TPU:7, one launch (start us, length us, event | category | flops | bytes accessed | tf_op | source)
XLA Modules:
  0.0 217.5 jit_solution(12992685433595538269)
XLA Ops:
  6.5 1.7 pad_maximum_fusion.2
  8.2 0.0 all-gather.5.cloned.1.call-update
  8.3 0.0 all-gather.7.cloned.1.call-start
  8.3 49.4 %all-gather.5.cloned.1.call-done = bf16[4096,256]{1,0:T(8,128)(2,1)} async-done(((bf16[256,256]{1,0:T(8,128)(2,1)}), bf16[4096,256]{1,0:T(8,128)(2,1)}) %all-gather.5.cloned.1.call-update) | async-done | bytes 2097168 | tf_op jit(solution)/shard_map/all_gather | solution.py:69
  57.7 0.0 copy-done
  57.7 2.3 %fusion.10 = bf16[256,256]{1,0:T(8,128)(2,1)S(1)} fusion(bf16[256,4096]{1,0:T(8,128)(2,1)S(1)} %copy-done, bf16[4096,256]{1,0:T(8,128)(2,1)} %all-gather.5.cloned.1.call-done), kind=kOutput, calls=%fused_computation.19 | convolution fusion | flops 536936448 | bytes 4325376 | tf_op jit(solution)/shard_map/dot_general | solution.py:72
  60.0 10.6 %all-gather = bf16[1024,256]{1,0:T(8,128)(2,1)} all-gather(bf16[256,256]{1,0:T(8,128)(2,1)S(1)} %fusion.10), channel_id=2, replica_groups=mesh['cy'=8,'cx'=4,'fsdp'=16] {'cx'}, dimensions={0}, use_global_device_ids=true | all-gather | bytes 655360 | tf_op jit(solution)/shard_map/all_gather | solution.py:75
  70.6 0.0 all-gather.7.cloned.1.call-update
  70.7 2.5 %collective-permute-start = (bf16[256,512]{1,0:T(8,128)(2,1)S(1)}, bf16[256,512]{1,0:T(8,128)(2,1)S(1)}, u32[]{:S(2)}, u32[]{:S(2)}) collective-permute-start(bf16[256,512]{1,0:T(8,128)(2,1)S(1)} %copy-done.2), channel_id=1, source_target_pairs={{0,2},{1,3},{2,4},{3,5},{4,6},{5,7},{6,8},{7,9},{8,10},{9,11},{10,... | collective-permute-start | bytes 786440 | tf_op jit(solution)/shard_map/ppermute | solution.py:31
  73.2 5.9 %collective-permute-done = bf16[256,512]{1,0:T(8,128)(2,1)S(1)} collective-permute-done((bf16[256,512]{1,0:T(8,128)(2,1)S(1)}, bf16[256,512]{1,0:T(8,128)(2,1)S(1)}, u32[]{:S(2)}, u32[]{:S(2)}) %collective-permute-start) | collective-permute-done | bytes 262176 | tf_op jit(solution)/shard_map/ppermute | solution.py:31
  79.0 1.9 collective-permute-start.1
  80.9 4.6 %collective-permute-start.4 = (bf16[256,512]{1,0:T(8,128)(2,1)S(1)}, bf16[256,512]{1,0:T(8,128)(2,1)S(1)}, u32[]{:S(2)}, u32[]{:S(2)}) collective-permute-start(bf16[256,512]{1,0:T(8,128)(2,1)S(1)} %copy-done.2), channel_id=1, source_target_pairs={{0,14},{1,15},{2,0},{3,1},{4,2},{5,3},{6,4},{7,5},{8,6},{9,7},{10,... | collective-permute-start | bytes 786440 | tf_op jit(solution)/shard_map/ppermute | solution.py:34
  85.5 1.8 collective-permute-done.1
  87.3 1.9 collective-permute-start.2
  89.2 0.0 collective-permute-done.4
  89.3 4.6 %collective-permute-start.5 = (bf16[256,512]{1,0:T(8,128)(2,1)S(1)}, bf16[256,512]{1,0:T(8,128)(2,1)S(1)}, u32[]{:S(2)}, u32[]{:S(2)}) collective-permute-start(bf16[256,512]{1,0:T(8,128)(2,1)S(1)} %collective-permute-done.4), channel_id=1, source_target_pairs={{0,14},{1,15},{2,0},{3,1},{4,2},{5,3},{6,4},{7,5},{8,6},{9,7},{10,... | collective-permute-start | bytes 786440 | tf_op jit(solution)/shard_map/ppermute | solution.py:34
  93.8 2.2 %collective-permute-done.2 = bf16[256,512]{1,0:T(8,128)(2,1)S(1)} collective-permute-done((bf16[256,512]{1,0:T(8,128)(2,1)S(1)}, bf16[256,512]{1,0:T(8,128)(2,1)S(1)}, u32[]{:S(2)}, u32[]{:S(2)}) %collective-permute-start.2) | collective-permute-done | bytes 262176 | tf_op jit(solution)/shard_map/ppermute | solution.py:31
  96.0 1.9 collective-permute-start.3
  98.0 0.0 collective-permute-done.5
  98.0 4.6 %collective-permute-start.6 = (bf16[256,512]{1,0:T(8,128)(2,1)S(1)}, bf16[256,512]{1,0:T(8,128)(2,1)S(1)}, u32[]{:S(2)}, u32[]{:S(2)}) collective-permute-start(bf16[256,512]{1,0:T(8,128)(2,1)S(1)} %collective-permute-done.5), channel_id=1, source_target_pairs={{0,14},{1,15},{2,0},{3,1},{4,2},{5,3},{6,4},{7,5},{8,6},{9,7},{10,... | collective-permute-start | bytes 786440 | tf_op jit(solution)/shard_map/ppermute | solution.py:34
  102.6 2.5 %collective-permute-done.3 = bf16[256,512]{1,0:T(8,128)(2,1)S(1)} collective-permute-done((bf16[256,512]{1,0:T(8,128)(2,1)S(1)}, bf16[256,512]{1,0:T(8,128)(2,1)S(1)}, u32[]{:S(2)}, u32[]{:S(2)}) %collective-permute-start.3) | collective-permute-done | bytes 262176 | tf_op jit(solution)/shard_map/ppermute | solution.py:31
  105.0 0.9 bitcast_dynamic-update-slice_fusion.22
  105.9 0.8 bitcast_dynamic-update-slice_fusion.19
  106.8 0.9 bitcast_dynamic-update-slice_fusion.16
  107.6 0.8 bitcast_dynamic-update-slice_fusion.13
  108.5 0.8 bitcast_dynamic-update-slice_fusion.10
  109.3 0.8 bitcast_dynamic-update-slice_fusion.7
  110.1 0.9 bitcast_dynamic-update-slice_fusion.4
  111.0 0.0 collective-permute-done.6
  111.0 0.0 copy-done.3
  111.0 0.7 copy-done.4
  111.7 0.8 bitcast_dynamic-update-slice_fusion.1
  112.5 9.0 %collective-permute-start.7 = (bf16[8,256,512]{2,1,0:T(8,128)(2,1)}, bf16[8,256,512]{2,1,0:T(8,128)(2,1)}, u32[]{:S(2)}, u32[]{:S(2)}) collective-permute-start(bf16[8,256,512]{2,1,0:T(8,128)(2,1)} %get-tuple-element.17), channel_id=1, source_target_pairs={{0,1},{1,0},{2,3},{3,2},{4,5},{5,4},{6,7},{7,6},{8,9},{9,8},{10,11... | collective-permute-start | bytes 6291464 | tf_op jit(solution)/shard_map/ppermute | solution.py:37
  121.7 1.7 bitcast_dynamic-update-slice_fusion.23
  123.3 1.7 bitcast_dynamic-update-slice_fusion.20
  125.0 0.7 bitcast_dynamic-update-slice_fusion.17
  125.8 0.7 bitcast_dynamic-update-slice_fusion.14
  126.5 0.7 bitcast_dynamic-update-slice_fusion.11
  127.2 0.7 bitcast_dynamic-update-slice_fusion.8
  127.9 0.7 bitcast_dynamic-update-slice_fusion.5
  128.6 1.7 bitcast_dynamic-update-slice_fusion.2
  130.3 0.0 collective-permute-done.7
  130.3 4.5 %select_bitcast_fusion.1 = (bf16[8,1,256,512]{3,2,1,0:T(8,128)(2,1)S(1)}, bf16[8,1,256,512]{3,2,1,0:T(8,128)(2,1)S(1)}) fusion(pred[]{:T(512)S(6)} %eq.14, bf16[16,256,512]{2,1,0:T(8,128)(2,1)} %bitcast_dynamic-update-slice_fusion.2, s32[]{:T(128)S(6)} %select_n.118, bf16[8,256,512]{2,1,0:T(8,128)(2,1)} %collective-permute-done.7), kind=kLoop, calls=%fused_computation.14 | loop fusion | flops 4194304 | bytes 8388613 | tf_op jit(solution)/shard_map/stack | solution.py:49
  134.9 0.4 pad_maximum_fusion
  135.2 0.0 copy-start.1
  135.3 2.0 convolution_convert_fusion
  137.3 0.7 gather_fusion
  138.0 0.0 all-gather.7.cloned.1.call-done
  138.0 4.2 %gather_fusion.1 = bf16[16,256,256]{2,1,0:T(8,128)(2,1)} fusion(bf16[32,256,256]{2,1,0:T(8,128)(2,1)} %all-gather.7.cloned.1.call-done, s32[1024]{0:T(1024)S(1)} %pad_clamp_fusion), kind=kCustom, calls=%fused_computation.1 | custom fusion | bytes 4194368 | tf_op jit(solution)/shard_map/jit(_take)/gather | solution.py:91
  142.2 4.3 %all-to-all-start = ((bf16[16,256,256]{2,1,0:T(8,128)(2,1)}), bf16[16,256,256]{2,1,0:T(8,128)(2,1)}, u32[]{:S(2)}, u32[]{:S(2)}) async-start(bf16[16,256,256]{2,1,0:T(8,128)(2,1)} %gather_fusion.1), calls=%async_computation | async-start | bytes 4194304 | tf_op jit(solution)/shard_map/all_to_all | solution.py:92
  146.6 3.5 %collective-permute-start.8 = (bf16[256,256]{1,0:T(8,128)(2,1)S(1)}, bf16[256,256]{1,0:T(8,128)(2,1)S(1)}, u32[]{:S(2)}, u32[]{:S(2)}) collective-permute-start(bf16[256,256]{1,0:T(8,128)(2,1)S(1)} %fusion.10), channel_id=1, source_target_pairs={{0,1},{1,2},{2,3},{3,4},{4,5},{5,6},{6,7},{7,8},{8,9},{9,10},{10,1... | collective-permute-start | bytes 393224 | tf_op jit(solution)/shard_map/ppermute | solution.py:12
  150.1 0.1 fusion.17
  150.2 43.5 %collective-permute-done.8 = bf16[256,256]{1,0:T(8,128)(2,1)S(1)} collective-permute-done((bf16[256,256]{1,0:T(8,128)(2,1)S(1)}, bf16[256,256]{1,0:T(8,128)(2,1)S(1)}, u32[]{:S(2)}, u32[]{:S(2)}) %collective-permute-start.8) | collective-permute-done | bytes 131104 | tf_op jit(solution)/shard_map/ppermute | solution.py:12
  193.7 0.1 constant_dynamic-slice_fusion.1
  193.8 0.6 fusion.46
  198.2 0.0 all-to-all-done
  198.2 1.0 constant_dynamic-slice_fusion
  199.2 4.1 %collective-permute-start.9 = (bf16[512,256]{1,0:T(8,128)(2,1)S(1)}, bf16[512,256]{1,0:T(8,128)(2,1)S(1)}, u32[]{:S(2)}, u32[]{:S(2)}) collective-permute-start(bf16[512,256]{1,0:T(8,128)(2,1)S(1)} %bitcast.100), channel_id=1, source_target_pairs={{0,1},{1,0},{2,3},{3,2},{4,5},{5,4},{6,7},{7,6},{8,9},{9,8},{10,11... | collective-permute-start | bytes 786440 | tf_op jit(solution)/shard_map/ppermute | solution.py:56
  203.3 1.4 add_add_fusion
  204.8 0.0 collective-permute-done.9
  204.8 2.0 fusion.2
  206.9 1.3 fusion
  208.2 1.6 fusion.14
  209.8 0.8 copy.19
  (21 shorter events, 0.1 us)
Async XLA Ops:
  6.5 51.2 %copy-start = (bf16[256,4096]{1,0:T(8,128)(2,1)S(1)}, bf16[256,4096]{1,0:T(8,128)(2,1)}, u32[]{:S(2)}) copy-start(bf16[256,4096]{1,0:T(8,128)(2,1)} %param.5) | copy-start | bytes 6291460
  6.5 64.1 %copy-start.2 = (bf16[256,512]{1,0:T(8,128)(2,1)S(1)}, bf16[256,512]{1,0:T(8,128)(2,1)}, u32[]{:S(2)}) copy-start(bf16[256,512]{1,0:T(8,128)(2,1)} %param.6) | copy-start | bytes 786436
  6.5 51.2 %all-gather.5.cloned.1.call-start = ((), (), s32[]{:S(2)}) async-start(), calls=%async_computation.1 | async-start | bytes 2228224 | tf_op jit(solution)/shard_map/all_gather | solution.py:69
  8.3 129.7 %all-gather.7.cloned.1.call-start = ((), (), s32[]{:S(2)}) async-start(), calls=%async_computation.2 | async-start | bytes 4718592 | tf_op jit(solution)/shard_map/all_gather | solution.py:76
  70.7 8.3 %collective-permute-start = (bf16[256,512]{1,0:T(8,128)(2,1)S(1)}, bf16[256,512]{1,0:T(8,128)(2,1)S(1)}, u32[]{:S(2)}, u32[]{:S(2)}) collective-permute-start(bf16[256,512]{1,0:T(8,128)(2,1)S(1)} %copy-done.2), channel_id=1, source_target_pairs={{0,2},{1,3},{2,4},{3,5},{4,6},{5,7},{6,8},{7,9},{8,10},{9,11},{10,... | collective-permute-start | bytes 786440 | tf_op jit(solution)/shard_map/ppermute | solution.py:31
  79.0 8.3 %collective-permute-start.1 = (bf16[256,512]{1,0:T(8,128)(2,1)S(1)}, bf16[256,512]{1,0:T(8,128)(2,1)S(1)}, u32[]{:S(2)}, u32[]{:S(2)}) collective-permute-start(bf16[256,512]{1,0:T(8,128)(2,1)S(1)} %collective-permute-done), channel_id=1, source_target_pairs={{0,2},{1,3},{2,4},{3,5},{4,6},{5,7},{6,8},{7,9},{8,10},{9,11},{10,... | collective-permute-start | bytes 786440 | tf_op jit(solution)/shard_map/ppermute | solution.py:31
  80.9 8.3 %collective-permute-start.4 = (bf16[256,512]{1,0:T(8,128)(2,1)S(1)}, bf16[256,512]{1,0:T(8,128)(2,1)S(1)}, u32[]{:S(2)}, u32[]{:S(2)}) collective-permute-start(bf16[256,512]{1,0:T(8,128)(2,1)S(1)} %copy-done.2), channel_id=1, source_target_pairs={{0,14},{1,15},{2,0},{3,1},{4,2},{5,3},{6,4},{7,5},{8,6},{9,7},{10,... | collective-permute-start | bytes 786440 | tf_op jit(solution)/shard_map/ppermute | solution.py:34
  87.3 8.7 %collective-permute-start.2 = (bf16[256,512]{1,0:T(8,128)(2,1)S(1)}, bf16[256,512]{1,0:T(8,128)(2,1)S(1)}, u32[]{:S(2)}, u32[]{:S(2)}) collective-permute-start(bf16[256,512]{1,0:T(8,128)(2,1)S(1)} %collective-permute-done.1), channel_id=1, source_target_pairs={{0,2},{1,3},{2,4},{3,5},{4,6},{5,7},{6,8},{7,9},{8,10},{9,11},{10,... | collective-permute-start | bytes 786440 | tf_op jit(solution)/shard_map/ppermute | solution.py:31
  89.3 8.7 %collective-permute-start.5 = (bf16[256,512]{1,0:T(8,128)(2,1)S(1)}, bf16[256,512]{1,0:T(8,128)(2,1)S(1)}, u32[]{:S(2)}, u32[]{:S(2)}) collective-permute-start(bf16[256,512]{1,0:T(8,128)(2,1)S(1)} %collective-permute-done.4), channel_id=1, source_target_pairs={{0,14},{1,15},{2,0},{3,1},{4,2},{5,3},{6,4},{7,5},{8,6},{9,7},{10,... | collective-permute-start | bytes 786440 | tf_op jit(solution)/shard_map/ppermute | solution.py:34
  96.0 15.0 %copy-start.3 = (bf16[256,512]{1,0:T(8,128)(2,1)}, bf16[256,512]{1,0:T(8,128)(2,1)S(1)}, u32[]{:S(2)}) copy-start(bf16[256,512]{1,0:T(8,128)(2,1)S(1)} %collective-permute-done.2) | copy-start | bytes 786436
  96.0 9.0 %collective-permute-start.3 = (bf16[256,512]{1,0:T(8,128)(2,1)S(1)}, bf16[256,512]{1,0:T(8,128)(2,1)S(1)}, u32[]{:S(2)}, u32[]{:S(2)}) collective-permute-start(bf16[256,512]{1,0:T(8,128)(2,1)S(1)} %collective-permute-done.2), channel_id=1, source_target_pairs={{0,2},{1,3},{2,4},{3,5},{4,6},{5,7},{6,8},{7,9},{8,10},{9,11},{10,... | collective-permute-start | bytes 786440 | tf_op jit(solution)/shard_map/ppermute | solution.py:31
  98.0 13.0 %collective-permute-start.6 = (bf16[256,512]{1,0:T(8,128)(2,1)S(1)}, bf16[256,512]{1,0:T(8,128)(2,1)S(1)}, u32[]{:S(2)}, u32[]{:S(2)}) collective-permute-start(bf16[256,512]{1,0:T(8,128)(2,1)S(1)} %collective-permute-done.5), channel_id=1, source_target_pairs={{0,14},{1,15},{2,0},{3,1},{4,2},{5,3},{6,4},{7,5},{8,6},{9,7},{10,... | collective-permute-start | bytes 786440 | tf_op jit(solution)/shard_map/ppermute | solution.py:34
  105.0 7.5 %copy-start.5 = (bf16[256,512]{1,0:T(8,128)(2,1)}, bf16[256,512]{1,0:T(8,128)(2,1)S(1)}, u32[]{:S(2)}) copy-start(bf16[256,512]{1,0:T(8,128)(2,1)S(1)} %collective-permute-done.3) | copy-start | bytes 786436
  111.0 0.7 copy-start.4
  112.5 17.8 %collective-permute-start.7 = (bf16[8,256,512]{2,1,0:T(8,128)(2,1)}, bf16[8,256,512]{2,1,0:T(8,128)(2,1)}, u32[]{:S(2)}, u32[]{:S(2)}) collective-permute-start(bf16[8,256,512]{2,1,0:T(8,128)(2,1)} %get-tuple-element.17), channel_id=1, source_target_pairs={{0,1},{1,0},{2,3},{3,2},{4,5},{5,4},{6,7},{7,6},{8,9},{9,8},{10,11... | collective-permute-start | bytes 6291464 | tf_op jit(solution)/shard_map/ppermute | solution.py:37
  135.2 2.0 copy-start.1
  142.2 56.0 %all-to-all-start = ((bf16[16,256,256]{2,1,0:T(8,128)(2,1)}), bf16[16,256,256]{2,1,0:T(8,128)(2,1)}, u32[]{:S(2)}, u32[]{:S(2)}) async-start(bf16[16,256,256]{2,1,0:T(8,128)(2,1)} %gather_fusion.1), calls=%async_computation | async-start | bytes 4194304 | tf_op jit(solution)/shard_map/all_to_all | solution.py:92
  146.6 47.1 %collective-permute-start.8 = (bf16[256,256]{1,0:T(8,128)(2,1)S(1)}, bf16[256,256]{1,0:T(8,128)(2,1)S(1)}, u32[]{:S(2)}, u32[]{:S(2)}) collective-permute-start(bf16[256,256]{1,0:T(8,128)(2,1)S(1)} %fusion.10), channel_id=1, source_target_pairs={{0,1},{1,2},{2,3},{3,4},{4,5},{5,6},{6,7},{7,8},{8,9},{9,10},{10,1... | collective-permute-start | bytes 393224 | tf_op jit(solution)/shard_map/ppermute | solution.py:12
  199.2 5.6 %collective-permute-start.9 = (bf16[512,256]{1,0:T(8,128)(2,1)S(1)}, bf16[512,256]{1,0:T(8,128)(2,1)S(1)}, u32[]{:S(2)}, u32[]{:S(2)}) collective-permute-start(bf16[512,256]{1,0:T(8,128)(2,1)S(1)} %bitcast.100), channel_id=1, source_target_pairs={{0,1},{1,0},{2,3},{3,2},{4,5},{5,4},{6,7},{7,6},{8,9},{9,8},{10,11... | collective-permute-start | bytes 786440 | tf_op jit(solution)/shard_map/ppermute | solution.py:56
Sparse Core Ops, SparseCore 0:
  9.5 48.1 all-gather.4
  70.8 57.6 all-gather.6

commit v4 on v3

--- a/solution.py
+++ b/solution.py
@@ -19,7 +19,7 @@
     return got.reshape((peers * array.shape[0],) + array.shape[1:])
 
 
-def ring_gather_rows(array, axis):
+def ring_gather_rows(array, axis, early_steps, tied):
     peers = lax.axis_size(axis)
     chips = peers // 2
     shift_pairs = lambda by: [(i, (i + by) % peers) for i in range(peers)]
@@ -28,6 +28,11 @@
     from_ahead = []
     from_behind_ = []
     for step in range(chips // 2):
+        if step == early_steps:
+            ahead, behind, tied = lax.optimization_barrier((ahead, behind, tied))
+            from_ahead[-1] = ahead
+            if from_behind_:
+                from_behind_[-1] = behind
         ahead = lax.ppermute(ahead, axis, shift_pairs(2))
         from_ahead.append(ahead)
         if step < chips // 2 - 1:
@@ -47,7 +52,7 @@
     first = jnp.where(core == 0, mine, other)
     second = jnp.where(core == 0, other, mine)
     full = jnp.stack([first, second], axis=1)
-    return full.reshape((peers * array.shape[0],) + array.shape[1:])
+    return full.reshape((peers * array.shape[0],) + array.shape[1:]), tied
 
 
 def swap_partner(array, axis):
@@ -69,6 +74,7 @@
     kv_weight = lax.all_gather(
         jnp.concatenate([key_weight, value_weight], axis=1), "fsdp", axis=0, tiled=True
     )
+    q_weight, kv_weight = ring_gather_rows(query_weight, "fsdp", 2, kv_weight)
     kv_f32 = jnp.dot(tokens, kv_weight, preferred_element_type=jnp.float32)
     key_value = kv_f32.astype(jnp.bfloat16)
 
@@ -79,8 +85,6 @@
     before_pair = from_behind(key_value, ("cy", "cx", "fsdp"), 1)
     own_block = jnp.concatenate([before_pair, key_value], axis=0)
 
-    query_weight, key_value = lax.optimization_barrier((query_weight, key_value))
-    q_weight = ring_gather_rows(query_weight, "fsdp")
     queries = jnp.dot(tokens, q_weight, preferred_element_type=jnp.float32)
     queries = queries.astype(jnp.bfloat16).reshape(token_rows, QH, head_width)
 

time: 220 us -> 215 us (0.977)
  waiting for transfers between devices: 105 us -> 91.2 us
  starting transfers between devices: 42.9 us -> 53.7 us
    all_gather x1, waiting for transfers between devices: 49.4 us -> 20.6 us  [per_device(): lax.all_gather(jnp.concatenate([key_weight, value_weight], axis=1), 'fsdp...]
    all_gather x1, waiting for transfers between devices: 0.02 us -> 10.3 us  [per_device(): lax.all_gather(along_x[None], 'cy', axis=0, tiled=True)]
    ppermute x4, waiting for transfers between devices: 12.4 us -> 16.6 us  [ring_gather_rows(): ahead = lax.ppermute(ahead, axis, shift_pairs(2))]
    ppermute x3, starting transfers between devices: 13.7 us -> 17.7 us  [ring_gather_rows(): behind = lax.ppermute(behind, axis, shift_pairs(-2))]
    all_to_all x1, starting transfers between devices: 4.32 us -> 8.07 us  [per_device(): lax.all_to_all(outgoing, 'fsdp', split_axis=0, concat_axis=0, tiled=True)]
    ppermute x4, starting transfers between devices: 8.19 us -> 11 us  [ring_gather_rows(): ahead = lax.ppermute(ahead, axis, shift_pairs(2))]
  transfers between devices with their start and end apart: 13 -> 13, of which waited for: 6 -> 8; matrix products, arithmetic and copies ran while one was open for 12% -> 12% of each run, Pallas kernels for 0% -> 0%
where the time goes in v4:
time: 215 us; the launch traced here: 214 us
  waiting for transfers between devices  91.2 us (42%)
  starting transfers between devices  53.7 us (25%)
  local copies, waits for them, and re-layouts  23.6 us (11%)
  between operations  17.5 us (8%)
  blocking collectives  10.6 us (5%)
  other arithmetic  9.59 us (4%)
  matrix products  7.92 us (4%)
    ppermute x1, waiting for transfers between devices, from_behind(): return lax.ppermute(array, axis, pairs)  43.5 us
    all_gather x1, waiting for transfers between devices, per_device(): lax.all_gather(jnp.concatenate([key_weight, value_weight], axis=1), 'fsdp...  20.6 us
    ppermute x3, starting transfers between devices, ring_gather_rows(): behind = lax.ppermute(behind, axis, shift_pairs(-2))  17.7 us
    ppermute x4, waiting for transfers between devices, ring_gather_rows(): ahead = lax.ppermute(ahead, axis, shift_pairs(2))  16.6 us
    unnamed x26, local copies, waits for them, and re-layouts  13.7 us
    ppermute x4, starting transfers between devices, ring_gather_rows(): ahead = lax.ppermute(ahead, axis, shift_pairs(2))  11 us
    all_gather x1, blocking collectives, per_device(): along_x = lax.all_gather(key_value[None], 'cx', axis=0, tiled=True)  10.6 us
    all_gather x1, waiting for transfers between devices, per_device(): lax.all_gather(along_x[None], 'cy', axis=0, tiled=True)  10.3 us
  transfers between devices with their start and end apart: 13, of which 8 were waited for; matrix products, arithmetic and copies ran while one was open for 12% of the time, Pallas kernels for 0%

profile of v4, /device:TPU:7, one launch (start us, length us, event | category | flops | bytes accessed | tf_op | source)
XLA Modules:
  0.0 214.2 jit_solution(11489306046105473867)
XLA Ops:
  6.5 0.0 all-gather.5.cloned.1.call-start
  6.5 1.7 pad_maximum_fusion.2
  8.2 0.0 all-gather.5.cloned.1.call-update
  8.3 0.0 copy-start.2
  8.3 0.0 all-gather.7.cloned.1.call-start
  8.3 4.1 %collective-permute-start = (bf16[256,512]{1,0:T(8,128)(2,1)}, bf16[256,512]{1,0:T(8,128)(2,1)S(1)}, u32[]{:S(2)}, u32[]{:S(2)}) collective-permute-start(bf16[256,512]{1,0:T(8,128)(2,1)} %param.6), channel_id=1, source_target_pairs={{0,2},{1,3},{2,4},{3,5},{4,6},{5,7},{6,8},{7,9},{8,10},{9,11},{10,... | collective-permute-start | bytes 786440 | tf_op jit(solution)/shard_map/ppermute | solution.py:36
  12.5 8.6 %collective-permute-start.2 = (bf16[256,512]{1,0:T(8,128)(2,1)}, bf16[256,512]{1,0:T(8,128)(2,1)S(1)}, u32[]{:S(2)}, u32[]{:S(2)}) collective-permute-start(bf16[256,512]{1,0:T(8,128)(2,1)} %param.6), channel_id=1, source_target_pairs={{0,14},{1,15},{2,0},{3,1},{4,2},{5,3},{6,4},{7,5},{8,6},{9,7},{10,... | collective-permute-start | bytes 786440 | tf_op jit(solution)/shard_map/ppermute | solution.py:39
  21.1 4.3 %collective-permute-done = bf16[256,512]{1,0:T(8,128)(2,1)S(1)} collective-permute-done((bf16[256,512]{1,0:T(8,128)(2,1)}, bf16[256,512]{1,0:T(8,128)(2,1)S(1)}, u32[]{:S(2)}, u32[]{:S(2)}) %collective-permute-start) | collective-permute-done | bytes 262176 | tf_op jit(solution)/shard_map/ppermute | solution.py:36
  25.4 1.9 collective-permute-start.1
  27.3 0.0 collective-permute-done.2
  27.3 4.6 %collective-permute-start.3 = (bf16[256,512]{1,0:T(8,128)(2,1)S(1)}, bf16[256,512]{1,0:T(8,128)(2,1)S(1)}, u32[]{:S(2)}, u32[]{:S(2)}) collective-permute-start(bf16[256,512]{1,0:T(8,128)(2,1)S(1)} %collective-permute-done.2), channel_id=1, source_target_pairs={{0,14},{1,15},{2,0},{3,1},{4,2},{5,3},{6,4},{7,5},{8,6},{9,7},{10,... | collective-permute-start | bytes 786440 | tf_op jit(solution)/shard_map/ppermute | solution.py:39
  31.9 5.2 %collective-permute-done.1 = bf16[256,512]{1,0:T(8,128)(2,1)S(1)} collective-permute-done((bf16[256,512]{1,0:T(8,128)(2,1)S(1)}, bf16[256,512]{1,0:T(8,128)(2,1)S(1)}, u32[]{:S(2)}, u32[]{:S(2)}) %collective-permute-start.1) | collective-permute-done | bytes 262176 | tf_op jit(solution)/shard_map/ppermute | solution.py:36
  37.0 0.2 collective-permute-done.3
  37.2 20.6 %all-gather.5.cloned.1.call-done = bf16[4096,256]{1,0:T(8,128)(2,1)} async-done(((bf16[256,256]{1,0:T(8,128)(2,1)}), bf16[4096,256]{1,0:T(8,128)(2,1)}) %all-gather.5.cloned.1.call-update) | async-done | bytes 2097168 | tf_op jit(solution)/shard_map/all_gather | solution.py:74
  57.8 2.3 %fusion.10 = bf16[256,256]{1,0:T(8,128)(2,1)S(1)} fusion(bf16[256,4096]{1,0:T(8,128)(2,1)S(1)} %copy-done, bf16[4096,256]{1,0:T(8,128)(2,1)} %all-gather.5.cloned.1.call-done), kind=kOutput, calls=%fused_computation.19 | convolution fusion | flops 536936448 | bytes 4325376 | tf_op jit(solution)/shard_map/dot_general | solution.py:78
  60.1 10.6 %all-gather = bf16[1024,256]{1,0:T(8,128)(2,1)} all-gather(bf16[256,256]{1,0:T(8,128)(2,1)S(1)} %fusion.10), channel_id=2, replica_groups=mesh['cy'=8,'cx'=4,'fsdp'=16] {'cx'}, dimensions={0}, use_global_device_ids=true | all-gather | bytes 655360 | tf_op jit(solution)/shard_map/all_gather | solution.py:81
  70.8 0.0 all-gather.7.cloned.1.call-update
  70.8 3.0 %collective-permute-start.4 = (bf16[256,512]{1,0:T(8,128)(2,1)S(1)}, bf16[256,512]{1,0:T(8,128)(2,1)S(1)}, u32[]{:S(2)}, u32[]{:S(2)}) collective-permute-start(bf16[256,512]{1,0:T(8,128)(2,1)S(1)} %collective-permute-done.1), channel_id=1, source_target_pairs={{0,2},{1,3},{2,4},{3,5},{4,6},{5,7},{6,8},{7,9},{8,10},{9,11},{10,... | collective-permute-start | bytes 786440 | tf_op jit(solution)/shard_map/ppermute | solution.py:36
  73.8 5.3 %collective-permute-done.4 = bf16[256,512]{1,0:T(8,128)(2,1)S(1)} collective-permute-done((bf16[256,512]{1,0:T(8,128)(2,1)S(1)}, bf16[256,512]{1,0:T(8,128)(2,1)S(1)}, u32[]{:S(2)}, u32[]{:S(2)}) %collective-permute-start.4) | collective-permute-done | bytes 262176 | tf_op jit(solution)/shard_map/ppermute | solution.py:36
  79.1 1.9 collective-permute-start.5
  81.0 4.6 %collective-permute-start.6 = (bf16[256,512]{1,0:T(8,128)(2,1)S(1)}, bf16[256,512]{1,0:T(8,128)(2,1)S(1)}, u32[]{:S(2)}, u32[]{:S(2)}) collective-permute-start(bf16[256,512]{1,0:T(8,128)(2,1)S(1)} %collective-permute-done.3), channel_id=1, source_target_pairs={{0,14},{1,15},{2,0},{3,1},{4,2},{5,3},{6,4},{7,5},{8,6},{9,7},{10,... | collective-permute-start | bytes 786440 | tf_op jit(solution)/shard_map/ppermute | solution.py:39
  85.6 1.8 collective-permute-done.5
  87.4 0.9 bitcast_dynamic-update-slice_fusion.22
  88.3 0.8 bitcast_dynamic-update-slice_fusion.19
  89.1 0.9 bitcast_dynamic-update-slice_fusion.16
  90.0 0.8 bitcast_dynamic-update-slice_fusion.13
  90.9 0.8 bitcast_dynamic-update-slice_fusion.10
  91.7 0.8 bitcast_dynamic-update-slice_fusion.7
  92.5 0.9 bitcast_dynamic-update-slice_fusion.4
  93.4 0.0 collective-permute-done.6
  93.4 0.7 copy-done.3
  94.1 0.8 bitcast_dynamic-update-slice_fusion.1
  94.9 7.6 %collective-permute-start.7 = (bf16[8,256,512]{2,1,0:T(8,128)(2,1)}, bf16[8,256,512]{2,1,0:T(8,128)(2,1)}, u32[]{:S(2)}, u32[]{:S(2)}) collective-permute-start(bf16[8,256,512]{2,1,0:T(8,128)(2,1)} %get-tuple-element.21), channel_id=1, source_target_pairs={{0,1},{1,0},{2,3},{3,2},{4,5},{5,4},{6,7},{7,6},{8,9},{9,8},{10,11... | collective-permute-start | bytes 6291464 | tf_op jit(solution)/shard_map/ppermute | solution.py:42
  102.6 1.7 bitcast_dynamic-update-slice_fusion.23
  104.3 1.7 bitcast_dynamic-update-slice_fusion.20
  106.0 0.7 bitcast_dynamic-update-slice_fusion.17
  106.7 0.7 bitcast_dynamic-update-slice_fusion.14
  107.4 0.7 bitcast_dynamic-update-slice_fusion.11
  108.1 0.7 bitcast_dynamic-update-slice_fusion.8
  108.8 0.7 bitcast_dynamic-update-slice_fusion.5
  109.6 1.7 bitcast_dynamic-update-slice_fusion.2
  111.2 0.0 collective-permute-done.7
  111.2 4.5 %select_bitcast_fusion.1 = (bf16[8,1,256,512]{3,2,1,0:T(8,128)(2,1)S(1)}, bf16[8,1,256,512]{3,2,1,0:T(8,128)(2,1)S(1)}) fusion(pred[]{:T(512)S(6)} %eq.14, bf16[16,256,512]{2,1,0:T(8,128)(2,1)} %bitcast_dynamic-update-slice_fusion.2, s32[]{:T(128)S(6)} %select_n.118, bf16[8,256,512]{2,1,0:T(8,128)(2,1)} %collective-permute-done.7), kind=kLoop, calls=%fused_computation.14 | loop fusion | flops 4194304 | bytes 8388613 | tf_op jit(solution)/shard_map/stack | solution.py:54
  115.8 0.4 pad_maximum_fusion
  116.2 0.0 copy-start.1
  116.2 2.0 convolution_convert_fusion
  118.2 0.7 gather_fusion
  118.9 10.3 %all-gather.7.cloned.1.call-done = bf16[32,256,256]{2,1,0:T(8,128)(2,1)} async-done(((bf16[4,256,256]{2,1,0:T(8,128)(2,1)}), bf16[32,256,256]{2,1,0:T(8,128)(2,1)}) %all-gather.7.cloned.1.call-update) | async-done | bytes 4194320 | tf_op jit(solution)/shard_map/all_gather | solution.py:82
  129.2 4.2 %gather_fusion.1 = bf16[16,256,256]{2,1,0:T(8,128)(2,1)} fusion(bf16[32,256,256]{2,1,0:T(8,128)(2,1)} %all-gather.7.cloned.1.call-done, s32[1024]{0:T(1024)S(1)} %pad_clamp_fusion), kind=kCustom, calls=%fused_computation.1 | custom fusion | bytes 4194368 | tf_op jit(solution)/shard_map/jit(_take)/gather | solution.py:95
  133.4 8.1 %all-to-all-start = ((bf16[16,256,256]{2,1,0:T(8,128)(2,1)}), bf16[16,256,256]{2,1,0:T(8,128)(2,1)}, u32[]{:S(2)}, u32[]{:S(2)}) async-start(bf16[16,256,256]{2,1,0:T(8,128)(2,1)} %gather_fusion.1), calls=%async_computation | async-start | bytes 4194304 | tf_op jit(solution)/shard_map/all_to_all | solution.py:96
  141.5 3.5 %collective-permute-start.8 = (bf16[256,256]{1,0:T(8,128)(2,1)S(1)}, bf16[256,256]{1,0:T(8,128)(2,1)S(1)}, u32[]{:S(2)}, u32[]{:S(2)}) collective-permute-start(bf16[256,256]{1,0:T(8,128)(2,1)S(1)} %fusion.10), channel_id=1, source_target_pairs={{0,1},{1,2},{2,3},{3,4},{4,5},{5,6},{6,7},{7,8},{8,9},{9,10},{10,1... | collective-permute-start | bytes 393224 | tf_op jit(solution)/shard_map/ppermute | solution.py:12
  145.0 0.1 fusion.17
  145.2 43.5 %collective-permute-done.8 = bf16[256,256]{1,0:T(8,128)(2,1)S(1)} collective-permute-done((bf16[256,256]{1,0:T(8,128)(2,1)S(1)}, bf16[256,256]{1,0:T(8,128)(2,1)S(1)}, u32[]{:S(2)}, u32[]{:S(2)}) %collective-permute-start.8) | collective-permute-done | bytes 131104 | tf_op jit(solution)/shard_map/ppermute | solution.py:12
  188.7 0.1 constant_dynamic-slice_fusion.1
  188.8 0.6 fusion.46
  193.2 0.0 all-to-all-done
  193.2 1.0 constant_dynamic-slice_fusion
  194.2 5.8 %collective-permute-start.9 = (bf16[512,256]{1,0:T(8,128)(2,1)S(1)}, bf16[512,256]{1,0:T(8,128)(2,1)S(1)}, u32[]{:S(2)}, u32[]{:S(2)}) collective-permute-start(bf16[512,256]{1,0:T(8,128)(2,1)S(1)} %bitcast.100), channel_id=1, source_target_pairs={{0,1},{1,0},{2,3},{3,2},{4,5},{5,4},{6,7},{7,6},{8,9},{9,8},{10,11... | collective-permute-start | bytes 786440 | tf_op jit(solution)/shard_map/ppermute | solution.py:61
  200.0 1.4 add_add_fusion
  201.5 0.0 collective-permute-done.9
  201.5 2.0 fusion.2
  203.5 1.3 fusion
  204.9 1.6 fusion.14
  206.5 0.8 copy.19
  (21 shorter events, 0.1 us)
Async XLA Ops:
  6.5 51.3 %copy-start = (bf16[256,4096]{1,0:T(8,128)(2,1)S(1)}, bf16[256,4096]{1,0:T(8,128)(2,1)}, u32[]{:S(2)}) copy-start(bf16[256,4096]{1,0:T(8,128)(2,1)} %param.5) | copy-start | bytes 6291460
  6.5 51.3 %all-gather.5.cloned.1.call-start = ((), (), s32[]{:S(2)}) async-start(), calls=%async_computation.1 | async-start | bytes 2228224 | tf_op jit(solution)/shard_map/all_gather | solution.py:74
  8.3 82.6 %copy-start.2 = (bf16[256,512]{1,0:T(8,128)(2,1)S(1)}, bf16[256,512]{1,0:T(8,128)(2,1)}, u32[]{:S(2)}) copy-start(bf16[256,512]{1,0:T(8,128)(2,1)} %param.6) | copy-start | bytes 786436
  8.3 120.9 %all-gather.7.cloned.1.call-start = ((), (), s32[]{:S(2)}) async-start(), calls=%async_computation.2 | async-start | bytes 4718592 | tf_op jit(solution)/shard_map/all_gather | solution.py:82
  8.3 17.0 %collective-permute-start = (bf16[256,512]{1,0:T(8,128)(2,1)}, bf16[256,512]{1,0:T(8,128)(2,1)S(1)}, u32[]{:S(2)}, u32[]{:S(2)}) collective-permute-start(bf16[256,512]{1,0:T(8,128)(2,1)} %param.6), channel_id=1, source_target_pairs={{0,2},{1,3},{2,4},{3,5},{4,6},{5,7},{6,8},{7,9},{8,10},{9,11},{10,... | collective-permute-start | bytes 786440 | tf_op jit(solution)/shard_map/ppermute | solution.py:36
  12.5 14.8 %collective-permute-start.2 = (bf16[256,512]{1,0:T(8,128)(2,1)}, bf16[256,512]{1,0:T(8,128)(2,1)S(1)}, u32[]{:S(2)}, u32[]{:S(2)}) collective-permute-start(bf16[256,512]{1,0:T(8,128)(2,1)} %param.6), channel_id=1, source_target_pairs={{0,14},{1,15},{2,0},{3,1},{4,2},{5,3},{6,4},{7,5},{8,6},{9,7},{10,... | collective-permute-start | bytes 786440 | tf_op jit(solution)/shard_map/ppermute | solution.py:39
  25.4 11.7 %collective-permute-start.1 = (bf16[256,512]{1,0:T(8,128)(2,1)S(1)}, bf16[256,512]{1,0:T(8,128)(2,1)S(1)}, u32[]{:S(2)}, u32[]{:S(2)}) collective-permute-start(bf16[256,512]{1,0:T(8,128)(2,1)S(1)} %collective-permute-done), channel_id=1, source_target_pairs={{0,2},{1,3},{2,4},{3,5},{4,6},{5,7},{6,8},{7,9},{8,10},{9,11},{10,... | collective-permute-start | bytes 786440 | tf_op jit(solution)/shard_map/ppermute | solution.py:36
  27.3 9.9 %collective-permute-start.3 = (bf16[256,512]{1,0:T(8,128)(2,1)S(1)}, bf16[256,512]{1,0:T(8,128)(2,1)S(1)}, u32[]{:S(2)}, u32[]{:S(2)}) collective-permute-start(bf16[256,512]{1,0:T(8,128)(2,1)S(1)} %collective-permute-done.2), channel_id=1, source_target_pairs={{0,14},{1,15},{2,0},{3,1},{4,2},{5,3},{6,4},{7,5},{8,6},{9,7},{10,... | collective-permute-start | bytes 786440 | tf_op jit(solution)/shard_map/ppermute | solution.py:39
  70.8 8.3 %collective-permute-start.4 = (bf16[256,512]{1,0:T(8,128)(2,1)S(1)}, bf16[256,512]{1,0:T(8,128)(2,1)S(1)}, u32[]{:S(2)}, u32[]{:S(2)}) collective-permute-start(bf16[256,512]{1,0:T(8,128)(2,1)S(1)} %collective-permute-done.1), channel_id=1, source_target_pairs={{0,2},{1,3},{2,4},{3,5},{4,6},{5,7},{6,8},{7,9},{8,10},{9,11},{10,... | collective-permute-start | bytes 786440 | tf_op jit(solution)/shard_map/ppermute | solution.py:36
  79.1 15.8 %copy-start.4 = (bf16[256,512]{1,0:T(8,128)(2,1)}, bf16[256,512]{1,0:T(8,128)(2,1)S(1)}, u32[]{:S(2)}) copy-start(bf16[256,512]{1,0:T(8,128)(2,1)S(1)} %collective-permute-done.4) | copy-start | bytes 786436
  79.1 8.3 %collective-permute-start.5 = (bf16[256,512]{1,0:T(8,128)(2,1)S(1)}, bf16[256,512]{1,0:T(8,128)(2,1)S(1)}, u32[]{:S(2)}, u32[]{:S(2)}) collective-permute-start(bf16[256,512]{1,0:T(8,128)(2,1)S(1)} %collective-permute-done.4), channel_id=1, source_target_pairs={{0,2},{1,3},{2,4},{3,5},{4,6},{5,7},{6,8},{7,9},{8,10},{9,11},{10,... | collective-permute-start | bytes 786440 | tf_op jit(solution)/shard_map/ppermute | solution.py:36
  81.0 12.4 %collective-permute-start.6 = (bf16[256,512]{1,0:T(8,128)(2,1)S(1)}, bf16[256,512]{1,0:T(8,128)(2,1)S(1)}, u32[]{:S(2)}, u32[]{:S(2)}) collective-permute-start(bf16[256,512]{1,0:T(8,128)(2,1)S(1)} %collective-permute-done.3), channel_id=1, source_target_pairs={{0,14},{1,15},{2,0},{3,1},{4,2},{5,3},{6,4},{7,5},{8,6},{9,7},{10,... | collective-permute-start | bytes 786440 | tf_op jit(solution)/shard_map/ppermute | solution.py:39
  87.4 7.5 %copy-start.5 = (bf16[256,512]{1,0:T(8,128)(2,1)}, bf16[256,512]{1,0:T(8,128)(2,1)S(1)}, u32[]{:S(2)}) copy-start(bf16[256,512]{1,0:T(8,128)(2,1)S(1)} %collective-permute-done.5) | copy-start | bytes 786436
  93.4 0.7 copy-start.3
  94.9 16.3 %collective-permute-start.7 = (bf16[8,256,512]{2,1,0:T(8,128)(2,1)}, bf16[8,256,512]{2,1,0:T(8,128)(2,1)}, u32[]{:S(2)}, u32[]{:S(2)}) collective-permute-start(bf16[8,256,512]{2,1,0:T(8,128)(2,1)} %get-tuple-element.21), channel_id=1, source_target_pairs={{0,1},{1,0},{2,3},{3,2},{4,5},{5,4},{6,7},{7,6},{8,9},{9,8},{10,11... | collective-permute-start | bytes 6291464 | tf_op jit(solution)/shard_map/ppermute | solution.py:42
  116.2 2.0 copy-start.1
  133.4 59.8 %all-to-all-start = ((bf16[16,256,256]{2,1,0:T(8,128)(2,1)}), bf16[16,256,256]{2,1,0:T(8,128)(2,1)}, u32[]{:S(2)}, u32[]{:S(2)}) async-start(bf16[16,256,256]{2,1,0:T(8,128)(2,1)} %gather_fusion.1), calls=%async_computation | async-start | bytes 4194304 | tf_op jit(solution)/shard_map/all_to_all | solution.py:96
  141.5 47.2 %collective-permute-start.8 = (bf16[256,256]{1,0:T(8,128)(2,1)S(1)}, bf16[256,256]{1,0:T(8,128)(2,1)S(1)}, u32[]{:S(2)}, u32[]{:S(2)}) collective-permute-start(bf16[256,256]{1,0:T(8,128)(2,1)S(1)} %fusion.10), channel_id=1, source_target_pairs={{0,1},{1,2},{2,3},{3,4},{4,5},{5,6},{6,7},{7,8},{8,9},{9,10},{10,1... | collective-permute-start | bytes 393224 | tf_op jit(solution)/shard_map/ppermute | solution.py:12
  194.2 7.3 %collective-permute-start.9 = (bf16[512,256]{1,0:T(8,128)(2,1)S(1)}, bf16[512,256]{1,0:T(8,128)(2,1)S(1)}, u32[]{:S(2)}, u32[]{:S(2)}) collective-permute-start(bf16[512,256]{1,0:T(8,128)(2,1)S(1)} %bitcast.100), channel_id=1, source_target_pairs={{0,1},{1,0},{2,3},{3,2},{4,5},{5,4},{6,7},{7,6},{8,9},{9,8},{10,11... | collective-permute-start | bytes 786440 | tf_op jit(solution)/shard_map/ppermute | solution.py:61
Sparse Core Ops, SparseCore 0:
  9.5 48.2 all-gather.4
  70.9 58.2 all-gather.6

commit v5 on v4

--- a/solution.py
+++ b/solution.py
@@ -92,7 +92,13 @@
 
     dest_block = group_index * blocks_group + jnp.arange(lane_count, dtype=jnp.int32) // 2
     dest_pick = chosen[dest_block, jnp.arange(lane_count, dtype=jnp.int32) % 2]
-    outgoing = jnp.take(candidates, dest_pick // blocks_group, axis=0, mode="clip")
+    sources = candidates.shape[0]
+    pick_hot = (
+        (dest_pick // blocks_group)[:, None] == jnp.arange(sources, dtype=jnp.int32)[None, :]
+    ).astype(candidates.dtype)
+    outgoing = jnp.dot(
+        pick_hot, candidates.reshape(sources, -1), preferred_element_type=jnp.float32
+    ).astype(candidates.dtype).reshape((lane_count,) + candidates.shape[1:])
     incoming = lax.all_to_all(outgoing, "fsdp", split_axis=0, concat_axis=0, tiled=True)
 
     mine = lax.dynamic_index_in_dim(chosen, my_block, 0, keepdims=False)
@@ -104,17 +110,20 @@
     )
     block_partner = swap_partner(block_mine, "fsdp")
 
-    key_rows = jnp.concatenate(
-        [own_block[:, :head_width], block_mine[:, :head_width], block_partner[:, :head_width]],
-        axis=0,
-    )
+    scale = head_width ** (-0.5)
+    scores = jnp.concatenate(
+        [
+            jnp.einsum(
+                "qhd,kd->hqk", queries, rows[:, :head_width], preferred_element_type=jnp.float32
+            )
+            for rows in (own_block, block_mine, block_partner)
+        ],
+        axis=2,
+    ) * scale
     value_rows = jnp.concatenate(
         [own_block[:, head_width:], block_mine[:, head_width:], block_partner[:, head_width:]],
         axis=0,
     )
-    scores = jnp.einsum(
-        "qhd,kd->hqk", queries, key_rows, preferred_element_type=jnp.float32
-    ) * head_width ** (-0.5)
     window_rows = own_block.shape[0]
     pick_rows = block_mine.shape[0]
     row_index = jnp.arange(token_rows, dtype=jnp.int32)

time: 215 us -> 215 us (level)
  waiting for transfers between devices: 91.2 us -> 87.7 us
  local copies, waits for them, and re-layouts: 23.6 us -> 25.8 us
    unnamed x26 -> x30, local copies, waits for them, and re-layouts: 13.7 us -> 19.9 us
    ppermute x1, waiting for transfers between devices: 43.5 us -> 38.8 us  [from_behind(): return lax.ppermute(array, axis, pairs)]
    gather x1 -> x0, local copies, waits for them, and re-layouts: 4.24 us -> none  [per_device(): jnp.take(candidates, dest_pick // blocks_group, axis=0, mode='clip')]
  transfers between devices with their start and end apart: 13 -> 13, of which waited for: 8 -> 9; matrix products, arithmetic and copies ran while one was open for 12% -> 12% of each run, Pallas kernels for 0% -> 0%
where the time goes in v5:
time: 215 us
  waiting for transfers between devices  87.7 us (41%)
  starting transfers between devices  53.9 us (25%)
  local copies, waits for them, and re-layouts  25.8 us (12%)
  between operations  17.8 us (8%)
  blocking collectives  10.6 us (5%)
  other arithmetic  10.4 us (5%)
  matrix products  8.55 us (4%)
    ppermute x1, waiting for transfers between devices, from_behind(): return lax.ppermute(array, axis, pairs)  38.8 us
    all_gather x1, waiting for transfers between devices, per_device(): lax.all_gather(jnp.concatenate([key_weight, value_weight], axis=1), 'fsdp...  20.6 us
    unnamed x30, local copies, waits for them, and re-layouts  19.9 us
    ppermute x3, starting transfers between devices, ring_gather_rows(): behind = lax.ppermute(behind, axis, shift_pairs(-2))  17.7 us
    ppermute x4, waiting for transfers between devices, ring_gather_rows(): ahead = lax.ppermute(ahead, axis, shift_pairs(2))  16.6 us
    all_gather x1, waiting for transfers between devices, per_device(): lax.all_gather(along_x[None], 'cy', axis=0, tiled=True)  11 us
    ppermute x4, starting transfers between devices, ring_gather_rows(): ahead = lax.ppermute(ahead, axis, shift_pairs(2))  11 us
    all_gather x1, blocking collectives, per_device(): along_x = lax.all_gather(key_value[None], 'cx', axis=0, tiled=True)  10.6 us
  transfers between devices with their start and end apart: 13, of which 9 were waited for; matrix products, arithmetic and copies ran while one was open for 12% of the time, Pallas kernels for 0%

profile of v5, /device:TPU:7, one launch (start us, length us, event | category | flops | bytes accessed | tf_op | source)
XLA Modules:
  0.0 214.7 jit_solution(15430753683779347419)
XLA Ops:
  6.5 1.7 pad_maximum_fusion.2
  8.2 0.0 all-gather.5.cloned.1.call-update
  8.3 0.0 copy-start.3
  8.3 0.0 all-gather.7.cloned.1.call-start
  8.3 4.1 %collective-permute-start = (bf16[256,512]{1,0:T(8,128)(2,1)}, bf16[256,512]{1,0:T(8,128)(2,1)S(1)}, u32[]{:S(2)}, u32[]{:S(2)}) collective-permute-start(bf16[256,512]{1,0:T(8,128)(2,1)} %param.6), channel_id=1, source_target_pairs={{0,2},{1,3},{2,4},{3,5},{4,6},{5,7},{6,8},{7,9},{8,10},{9,11},{10,... | collective-permute-start | bytes 786440 | tf_op jit(solution)/shard_map/ppermute | solution.py:36
  12.5 8.6 %collective-permute-start.2 = (bf16[256,512]{1,0:T(8,128)(2,1)}, bf16[256,512]{1,0:T(8,128)(2,1)S(1)}, u32[]{:S(2)}, u32[]{:S(2)}) collective-permute-start(bf16[256,512]{1,0:T(8,128)(2,1)} %param.6), channel_id=1, source_target_pairs={{0,14},{1,15},{2,0},{3,1},{4,2},{5,3},{6,4},{7,5},{8,6},{9,7},{10,... | collective-permute-start | bytes 786440 | tf_op jit(solution)/shard_map/ppermute | solution.py:39
  21.1 4.3 %collective-permute-done = bf16[256,512]{1,0:T(8,128)(2,1)S(1)} collective-permute-done((bf16[256,512]{1,0:T(8,128)(2,1)}, bf16[256,512]{1,0:T(8,128)(2,1)S(1)}, u32[]{:S(2)}, u32[]{:S(2)}) %collective-permute-start) | collective-permute-done | bytes 262176 | tf_op jit(solution)/shard_map/ppermute | solution.py:36
  25.4 1.9 collective-permute-start.1
  27.3 4.6 %collective-permute-start.3 = (bf16[256,512]{1,0:T(8,128)(2,1)S(1)}, bf16[256,512]{1,0:T(8,128)(2,1)S(1)}, u32[]{:S(2)}, u32[]{:S(2)}) collective-permute-start(bf16[256,512]{1,0:T(8,128)(2,1)S(1)} %collective-permute-done.2), channel_id=1, source_target_pairs={{0,14},{1,15},{2,0},{3,1},{4,2},{5,3},{6,4},{7,5},{8,6},{9,7},{10,... | collective-permute-start | bytes 786440 | tf_op jit(solution)/shard_map/ppermute | solution.py:39
  31.9 5.2 %collective-permute-done.1 = bf16[256,512]{1,0:T(8,128)(2,1)S(1)} collective-permute-done((bf16[256,512]{1,0:T(8,128)(2,1)S(1)}, bf16[256,512]{1,0:T(8,128)(2,1)S(1)}, u32[]{:S(2)}, u32[]{:S(2)}) %collective-permute-start.1) | collective-permute-done | bytes 262176 | tf_op jit(solution)/shard_map/ppermute | solution.py:36
  37.0 0.2 collective-permute-done.3
  37.2 20.6 %all-gather.5.cloned.1.call-done = bf16[4096,256]{1,0:T(8,128)(2,1)} async-done(((bf16[256,256]{1,0:T(8,128)(2,1)}), bf16[4096,256]{1,0:T(8,128)(2,1)}) %all-gather.5.cloned.1.call-update) | async-done | bytes 2097168 | tf_op jit(solution)/shard_map/all_gather | solution.py:74
  57.8 2.3 %fusion.16 = bf16[256,256]{1,0:T(8,128)(2,1)S(1)} fusion(bf16[256,4096]{1,0:T(8,128)(2,1)S(1)} %copy-done, bf16[4096,256]{1,0:T(8,128)(2,1)} %all-gather.5.cloned.1.call-done), kind=kOutput, calls=%fused_computation.24 | convolution fusion | flops 536936448 | bytes 4325376 | tf_op jit(solution)/shard_map/dot_general | solution.py:78
  60.1 10.6 %all-gather = bf16[1024,256]{1,0:T(8,128)(2,1)} all-gather(bf16[256,256]{1,0:T(8,128)(2,1)S(1)} %fusion.16), channel_id=2, replica_groups=mesh['cy'=8,'cx'=4,'fsdp'=16] {'cx'}, dimensions={0}, use_global_device_ids=true | all-gather | bytes 655360 | tf_op jit(solution)/shard_map/all_gather | solution.py:81
  70.8 0.0 all-gather.7.cloned.1.call-update
  70.8 3.0 %collective-permute-start.4 = (bf16[256,512]{1,0:T(8,128)(2,1)S(1)}, bf16[256,512]{1,0:T(8,128)(2,1)S(1)}, u32[]{:S(2)}, u32[]{:S(2)}) collective-permute-start(bf16[256,512]{1,0:T(8,128)(2,1)S(1)} %collective-permute-done.1), channel_id=1, source_target_pairs={{0,2},{1,3},{2,4},{3,5},{4,6},{5,7},{6,8},{7,9},{8,10},{9,11},{10,... | collective-permute-start | bytes 786440 | tf_op jit(solution)/shard_map/ppermute | solution.py:36
  73.8 5.3 %collective-permute-done.4 = bf16[256,512]{1,0:T(8,128)(2,1)S(1)} collective-permute-done((bf16[256,512]{1,0:T(8,128)(2,1)S(1)}, bf16[256,512]{1,0:T(8,128)(2,1)S(1)}, u32[]{:S(2)}, u32[]{:S(2)}) %collective-permute-start.4) | collective-permute-done | bytes 262176 | tf_op jit(solution)/shard_map/ppermute | solution.py:36
  79.1 1.9 collective-permute-start.5
  81.0 4.6 %collective-permute-start.6 = (bf16[256,512]{1,0:T(8,128)(2,1)S(1)}, bf16[256,512]{1,0:T(8,128)(2,1)S(1)}, u32[]{:S(2)}, u32[]{:S(2)}) collective-permute-start(bf16[256,512]{1,0:T(8,128)(2,1)S(1)} %collective-permute-done.3), channel_id=1, source_target_pairs={{0,14},{1,15},{2,0},{3,1},{4,2},{5,3},{6,4},{7,5},{8,6},{9,7},{10,... | collective-permute-start | bytes 786440 | tf_op jit(solution)/shard_map/ppermute | solution.py:39
  85.6 1.8 collective-permute-done.5
  87.4 0.9 bitcast_dynamic-update-slice_fusion.22
  88.3 0.8 bitcast_dynamic-update-slice_fusion.19
  89.1 0.8 bitcast_dynamic-update-slice_fusion.16
  90.0 0.8 bitcast_dynamic-update-slice_fusion.13
  90.8 0.8 bitcast_dynamic-update-slice_fusion.10
  91.6 0.8 bitcast_dynamic-update-slice_fusion.7
  92.5 0.8 bitcast_dynamic-update-slice_fusion.4
  93.3 0.7 copy-done.4
  94.0 0.8 bitcast_dynamic-update-slice_fusion.1
  94.9 7.6 %collective-permute-start.7 = (bf16[8,256,512]{2,1,0:T(8,128)(2,1)}, bf16[8,256,512]{2,1,0:T(8,128)(2,1)}, u32[]{:S(2)}, u32[]{:S(2)}) collective-permute-start(bf16[8,256,512]{2,1,0:T(8,128)(2,1)} %get-tuple-element.17), channel_id=1, source_target_pairs={{0,1},{1,0},{2,3},{3,2},{4,5},{5,4},{6,7},{7,6},{8,9},{9,8},{10,11... | collective-permute-start | bytes 6291464 | tf_op jit(solution)/shard_map/ppermute | solution.py:42
  102.5 1.7 bitcast_dynamic-update-slice_fusion.23
  104.2 1.7 bitcast_dynamic-update-slice_fusion.20
  105.9 0.7 bitcast_dynamic-update-slice_fusion.17
  106.6 0.7 bitcast_dynamic-update-slice_fusion.14
  107.3 0.7 bitcast_dynamic-update-slice_fusion.11
  108.0 0.7 bitcast_dynamic-update-slice_fusion.8
  108.7 0.7 bitcast_dynamic-update-slice_fusion.5
  109.5 1.7 bitcast_dynamic-update-slice_fusion.2
  111.2 4.5 %select_bitcast_fusion.1 = (bf16[8,1,256,512]{3,2,1,0:T(8,128)(2,1)S(1)}, bf16[8,1,256,512]{3,2,1,0:T(8,128)(2,1)S(1)}) fusion(pred[]{:T(512)S(6)} %eq.15, bf16[16,256,512]{2,1,0:T(8,128)(2,1)} %bitcast_dynamic-update-slice_fusion.2, s32[]{:T(128)S(6)} %select_n.115, bf16[8,256,512]{2,1,0:T(8,128)(2,1)} %collective-permute-done.7), kind=kLoop, calls=%fused_computation.14 | loop fusion | flops 4194304 | bytes 8388613 | tf_op jit(solution)/shard_map/stack | solution.py:54
  115.7 0.4 pad_maximum_fusion
  116.1 0.0 copy-start.1
  116.1 1.3 convolution_convert_fusion.1
  117.5 0.7 gather_fusion
  118.2 11.0 %all-gather.7.cloned.1.call-done = bf16[32,256,256]{2,1,0:T(8,128)(2,1)} async-done(((bf16[4,256,256]{2,1,0:T(8,128)(2,1)}), bf16[32,256,256]{2,1,0:T(8,128)(2,1)}) %all-gather.7.cloned.1.call-update) | async-done | bytes 4194320 | tf_op jit(solution)/shard_map/all_gather | solution.py:82
  129.2 4.6 %copy.32 = bf16[4,8,256,256]{3,1,2,0:T(8,128)(2,1)S(1)} copy(bf16[4,8,256,256]{3,2,1,0:T(8,128)(2,1)} %bitcast.91) | data formatting | bytes 8388608
  133.8 0.8 convolution_convert_fusion
  134.5 1.8 copy.33
  136.3 8.1 %all-to-all-start = ((bf16[16,256,256]{2,1,0:T(8,128)(2,1)}), bf16[16,256,256]{2,1,0:T(8,128)(2,1)}, u32[]{:S(2)}, u32[]{:S(2)}) async-start(bf16[16,256,256]{2,1,0:T(8,128)(2,1)} %bitcast.90), calls=%async_computation | async-start | bytes 4194304 | tf_op jit(solution)/shard_map/all_to_all | solution.py:102
  144.4 0.1 fusion.19
  144.5 3.5 %collective-permute-start.8 = (bf16[256,256]{1,0:T(8,128)(2,1)S(1)}, bf16[256,256]{1,0:T(8,128)(2,1)S(1)}, u32[]{:S(2)}, u32[]{:S(2)}) collective-permute-start(bf16[256,256]{1,0:T(8,128)(2,1)S(1)} %fusion.16), channel_id=1, source_target_pairs={{0,1},{1,2},{2,3},{3,4},{4,5},{5,6},{6,7},{7,8},{8,9},{9,10},{10,1... | collective-permute-start | bytes 393224 | tf_op jit(solution)/shard_map/ppermute | solution.py:12
  148.1 0.1 constant_dynamic-slice_fusion.1
  148.2 0.6 fusion.43
  152.8 38.8 %collective-permute-done.8 = bf16[256,256]{1,0:T(8,128)(2,1)S(1)} collective-permute-done((bf16[256,256]{1,0:T(8,128)(2,1)S(1)}, bf16[256,256]{1,0:T(8,128)(2,1)S(1)}, u32[]{:S(2)}, u32[]{:S(2)}) %collective-permute-start.8) | collective-permute-done | bytes 131104 | tf_op jit(solution)/shard_map/ppermute | solution.py:12
  191.6 1.8 convolution_bitcast_fusion.2
  193.4 1.4 add_add_fusion
  194.8 1.1 constant_dynamic-slice_fusion
  195.9 6.0 %collective-permute-start.9 = (bf16[512,256]{1,0:T(8,128)(2,1)S(1)}, bf16[512,256]{1,0:T(8,128)(2,1)S(1)}, u32[]{:S(2)}, u32[]{:S(2)}) collective-permute-start(bf16[512,256]{1,0:T(8,128)(2,1)S(1)} %bitcast.97), channel_id=1, source_target_pairs={{0,1},{1,0},{2,3},{3,2},{4,5},{5,4},{6,7},{7,6},{8,9},{9,8},{10,11... | collective-permute-start | bytes 786440 | tf_op jit(solution)/shard_map/ppermute | solution.py:61
  201.9 0.4 convolution_bitcast_fusion.1
  202.3 0.5 collective-permute-done.9
  202.9 0.4 convolution_bitcast_fusion
  203.3 0.8 fusion.18
  204.1 1.4 fusion.1
  205.5 1.6 fusion.13
  207.0 0.8 copy.25
  (26 shorter events, 0.1 us)
Async XLA Ops:
  6.5 51.3 %copy-start = (bf16[256,4096]{1,0:T(8,128)(2,1)S(1)}, bf16[256,4096]{1,0:T(8,128)(2,1)}, u32[]{:S(2)}) copy-start(bf16[256,4096]{1,0:T(8,128)(2,1)} %param.5) | copy-start | bytes 6291460
  6.5 51.3 %all-gather.5.cloned.1.call-start = ((), (), s32[]{:S(2)}) async-start(), calls=%async_computation.1 | async-start | bytes 2228224 | tf_op jit(solution)/shard_map/all_gather | solution.py:74
  8.3 82.6 %copy-start.3 = (bf16[256,512]{1,0:T(8,128)(2,1)S(1)}, bf16[256,512]{1,0:T(8,128)(2,1)}, u32[]{:S(2)}) copy-start(bf16[256,512]{1,0:T(8,128)(2,1)} %param.6) | copy-start | bytes 786436
  8.3 120.9 %all-gather.7.cloned.1.call-start = ((), (), s32[]{:S(2)}) async-start(), calls=%async_computation.2 | async-start | bytes 4718592 | tf_op jit(solution)/shard_map/all_gather | solution.py:82
  8.3 17.0 %collective-permute-start = (bf16[256,512]{1,0:T(8,128)(2,1)}, bf16[256,512]{1,0:T(8,128)(2,1)S(1)}, u32[]{:S(2)}, u32[]{:S(2)}) collective-permute-start(bf16[256,512]{1,0:T(8,128)(2,1)} %param.6), channel_id=1, source_target_pairs={{0,2},{1,3},{2,4},{3,5},{4,6},{5,7},{6,8},{7,9},{8,10},{9,11},{10,... | collective-permute-start | bytes 786440 | tf_op jit(solution)/shard_map/ppermute | solution.py:36
  12.5 14.8 %collective-permute-start.2 = (bf16[256,512]{1,0:T(8,128)(2,1)}, bf16[256,512]{1,0:T(8,128)(2,1)S(1)}, u32[]{:S(2)}, u32[]{:S(2)}) collective-permute-start(bf16[256,512]{1,0:T(8,128)(2,1)} %param.6), channel_id=1, source_target_pairs={{0,14},{1,15},{2,0},{3,1},{4,2},{5,3},{6,4},{7,5},{8,6},{9,7},{10,... | collective-permute-start | bytes 786440 | tf_op jit(solution)/shard_map/ppermute | solution.py:39
  25.4 11.7 %collective-permute-start.1 = (bf16[256,512]{1,0:T(8,128)(2,1)S(1)}, bf16[256,512]{1,0:T(8,128)(2,1)S(1)}, u32[]{:S(2)}, u32[]{:S(2)}) collective-permute-start(bf16[256,512]{1,0:T(8,128)(2,1)S(1)} %collective-permute-done), channel_id=1, source_target_pairs={{0,2},{1,3},{2,4},{3,5},{4,6},{5,7},{6,8},{7,9},{8,10},{9,11},{10,... | collective-permute-start | bytes 786440 | tf_op jit(solution)/shard_map/ppermute | solution.py:36
  27.3 9.9 %collective-permute-start.3 = (bf16[256,512]{1,0:T(8,128)(2,1)S(1)}, bf16[256,512]{1,0:T(8,128)(2,1)S(1)}, u32[]{:S(2)}, u32[]{:S(2)}) collective-permute-start(bf16[256,512]{1,0:T(8,128)(2,1)S(1)} %collective-permute-done.2), channel_id=1, source_target_pairs={{0,14},{1,15},{2,0},{3,1},{4,2},{5,3},{6,4},{7,5},{8,6},{9,7},{10,... | collective-permute-start | bytes 786440 | tf_op jit(solution)/shard_map/ppermute | solution.py:39
  70.8 8.3 %collective-permute-start.4 = (bf16[256,512]{1,0:T(8,128)(2,1)S(1)}, bf16[256,512]{1,0:T(8,128)(2,1)S(1)}, u32[]{:S(2)}, u32[]{:S(2)}) collective-permute-start(bf16[256,512]{1,0:T(8,128)(2,1)S(1)} %collective-permute-done.1), channel_id=1, source_target_pairs={{0,2},{1,3},{2,4},{3,5},{4,6},{5,7},{6,8},{7,9},{8,10},{9,11},{10,... | collective-permute-start | bytes 786440 | tf_op jit(solution)/shard_map/ppermute | solution.py:36
  79.1 15.8 %copy-start.5 = (bf16[256,512]{1,0:T(8,128)(2,1)}, bf16[256,512]{1,0:T(8,128)(2,1)S(1)}, u32[]{:S(2)}) copy-start(bf16[256,512]{1,0:T(8,128)(2,1)S(1)} %collective-permute-done.4) | copy-start | bytes 786436
  79.1 8.3 %collective-permute-start.5 = (bf16[256,512]{1,0:T(8,128)(2,1)S(1)}, bf16[256,512]{1,0:T(8,128)(2,1)S(1)}, u32[]{:S(2)}, u32[]{:S(2)}) collective-permute-start(bf16[256,512]{1,0:T(8,128)(2,1)S(1)} %collective-permute-done.4), channel_id=1, source_target_pairs={{0,2},{1,3},{2,4},{3,5},{4,6},{5,7},{6,8},{7,9},{8,10},{9,11},{10,... | collective-permute-start | bytes 786440 | tf_op jit(solution)/shard_map/ppermute | solution.py:36
  81.0 12.3 %collective-permute-start.6 = (bf16[256,512]{1,0:T(8,128)(2,1)S(1)}, bf16[256,512]{1,0:T(8,128)(2,1)S(1)}, u32[]{:S(2)}, u32[]{:S(2)}) collective-permute-start(bf16[256,512]{1,0:T(8,128)(2,1)S(1)} %collective-permute-done.3), channel_id=1, source_target_pairs={{0,14},{1,15},{2,0},{3,1},{4,2},{5,3},{6,4},{7,5},{8,6},{9,7},{10,... | collective-permute-start | bytes 786440 | tf_op jit(solution)/shard_map/ppermute | solution.py:39
  87.4 7.4 %copy-start.6 = (bf16[256,512]{1,0:T(8,128)(2,1)}, bf16[256,512]{1,0:T(8,128)(2,1)S(1)}, u32[]{:S(2)}) copy-start(bf16[256,512]{1,0:T(8,128)(2,1)S(1)} %collective-permute-done.5) | copy-start | bytes 786436
  93.3 0.7 copy-start.4
  94.9 16.3 %collective-permute-start.7 = (bf16[8,256,512]{2,1,0:T(8,128)(2,1)}, bf16[8,256,512]{2,1,0:T(8,128)(2,1)}, u32[]{:S(2)}, u32[]{:S(2)}) collective-permute-start(bf16[8,256,512]{2,1,0:T(8,128)(2,1)} %get-tuple-element.17), channel_id=1, source_target_pairs={{0,1},{1,0},{2,3},{3,2},{4,5},{5,4},{6,7},{7,6},{8,9},{9,8},{10,11... | collective-permute-start | bytes 6291464 | tf_op jit(solution)/shard_map/ppermute | solution.py:42
  116.1 1.3 copy-start.1
  136.3 58.5 %all-to-all-start = ((bf16[16,256,256]{2,1,0:T(8,128)(2,1)}), bf16[16,256,256]{2,1,0:T(8,128)(2,1)}, u32[]{:S(2)}, u32[]{:S(2)}) async-start(bf16[16,256,256]{2,1,0:T(8,128)(2,1)} %bitcast.90), calls=%async_computation | async-start | bytes 4194304 | tf_op jit(solution)/shard_map/all_to_all | solution.py:102
  144.5 47.0 %collective-permute-start.8 = (bf16[256,256]{1,0:T(8,128)(2,1)S(1)}, bf16[256,256]{1,0:T(8,128)(2,1)S(1)}, u32[]{:S(2)}, u32[]{:S(2)}) collective-permute-start(bf16[256,256]{1,0:T(8,128)(2,1)S(1)} %fusion.16), channel_id=1, source_target_pairs={{0,1},{1,2},{2,3},{3,4},{4,5},{5,6},{6,7},{7,8},{8,9},{9,10},{10,1... | collective-permute-start | bytes 393224 | tf_op jit(solution)/shard_map/ppermute | solution.py:12
  194.8 8.5 %copy-start.2 = (f32[4,256,512]{1,2,0:T(8,128)S(1)}, f32[4,256,512]{1,2,0:T(8,128)}, u32[]{:S(2)}) copy-start(f32[4,256,512]{1,2,0:T(8,128)} %convolution_bitcast_fusion.2) | copy-start | bytes 6291460
  195.9 6.9 %collective-permute-start.9 = (bf16[512,256]{1,0:T(8,128)(2,1)S(1)}, bf16[512,256]{1,0:T(8,128)(2,1)S(1)}, u32[]{:S(2)}, u32[]{:S(2)}) collective-permute-start(bf16[512,256]{1,0:T(8,128)(2,1)S(1)} %bitcast.97), channel_id=1, source_target_pairs={{0,1},{1,0},{2,3},{3,2},{4,5},{5,4},{6,7},{7,6},{8,9},{9,8},{10,11... | collective-permute-start | bytes 786440 | tf_op jit(solution)/shard_map/ppermute | solution.py:61
Sparse Core Ops, SparseCore 0:
  9.5 48.2 all-gather.4
  70.9 58.2 all-gather.6

commit v6 on v5

--- a/solution.py
+++ b/solution.py
@@ -78,11 +78,12 @@
     kv_f32 = jnp.dot(tokens, kv_weight, preferred_element_type=jnp.float32)
     key_value = kv_f32.astype(jnp.bfloat16)
 
+    before_pair = from_behind(key_value, ("cy", "cx", "fsdp"), 1)
     along_x = lax.all_gather(key_value[None], "cx", axis=0, tiled=True)
+    along_x, before_pair = lax.optimization_barrier((along_x, before_pair))
     candidates = lax.all_gather(along_x[None], "cy", axis=0, tiled=True).reshape(
         (-1,) + key_value.shape
     )
-    before_pair = from_behind(key_value, ("cy", "cx", "fsdp"), 1)
     own_block = jnp.concatenate([before_pair, key_value], axis=0)
 
     queries = jnp.dot(tokens, q_weight, preferred_element_type=jnp.float32)

time: 215 us -> 214 us (level)
  starting transfers between devices: 53.9 us -> 46.2 us
  waiting for transfers between devices: 87.7 us -> 91.6 us
    all_to_all x1, waiting for transfers between devices: 0.01 us -> 41.4 us  [per_device(): lax.all_to_all(outgoing, 'fsdp', split_axis=0, concat_axis=0, tiled=True)]
    ppermute x1, waiting for transfers between devices: 38.8 us -> 0.01 us  [from_behind(): return lax.ppermute(array, axis, pairs)]
    ppermute x1, starting transfers between devices: 5.96 us -> 2.42 us  [swap_partner(): return lax.ppermute(array, axis, pairs)]
    ppermute x4, waiting for transfers between devices: 16.6 us -> 19.6 us  [ring_gather_rows(): ahead = lax.ppermute(ahead, axis, shift_pairs(2))]
    ppermute x1, starting transfers between devices: 7.59 us -> 4.8 us  [ring_gather_rows(): other = lax.ppermute(mine, axis, [(i, i ^ 1) for i in range(peers)])]
    unnamed x30 -> x34, local copies, waits for them, and re-layouts: 19.9 us -> 20.7 us
  transfers between devices with their start and end apart: 13 -> 13, of which waited for: 9 -> 9; matrix products, arithmetic and copies ran while one was open for 12% -> 13% of each run, Pallas kernels for 0% -> 0%
where the time goes in v6:
time: 214 us; the launch traced here: 213 us
  waiting for transfers between devices  91.6 us (43%)
  starting transfers between devices  46.2 us (22%)
  local copies, waits for them, and re-layouts  26.5 us (12%)
  between operations  17.4 us (8%)
  blocking collectives  12.2 us (6%)
  other arithmetic  10.4 us (5%)
  matrix products  8.56 us (4%)
    all_to_all x1, waiting for transfers between devices, per_device(): lax.all_to_all(outgoing, 'fsdp', split_axis=0, concat_axis=0, tiled=True)  41.4 us
    unnamed x34, local copies, waits for them, and re-layouts  20.7 us
    all_gather x1, waiting for transfers between devices, per_device(): lax.all_gather(jnp.concatenate([key_weight, value_weight], axis=1), 'fsdp...  20.6 us
    ppermute x4, waiting for transfers between devices, ring_gather_rows(): ahead = lax.ppermute(ahead, axis, shift_pairs(2))  19.6 us
    ppermute x3, starting transfers between devices, ring_gather_rows(): behind = lax.ppermute(behind, axis, shift_pairs(-2))  17.7 us
    all_gather x1, blocking collectives, per_device(): along_x = lax.all_gather(key_value[None], 'cx', axis=0, tiled=True)  12.2 us
    ppermute x4, starting transfers between devices, ring_gather_rows(): ahead = lax.ppermute(ahead, axis, shift_pairs(2))  10 us
    all_gather x1, waiting for transfers between devices, per_device(): lax.all_gather(along_x[None], 'cy', axis=0, tiled=True)  9.27 us
  transfers between devices with their start and end apart: 13, of which 9 were waited for; matrix products, arithmetic and copies ran while one was open for 13% of the time, Pallas kernels for 0%

profile of v6, /device:TPU:7, one launch (start us, length us, event | category | flops | bytes accessed | tf_op | source)
XLA Modules:
  0.0 212.8 jit_solution(1383026823380620197)
XLA Ops:
  6.5 1.7 pad_maximum_fusion.2
  8.2 0.0 all-gather.5.cloned.1.call-update
  8.3 0.0 copy-start.3
  8.3 0.0 all-gather.7.cloned.1.call-start
  8.3 4.1 %collective-permute-start = (bf16[256,512]{1,0:T(8,128)(2,1)}, bf16[256,512]{1,0:T(8,128)(2,1)S(1)}, u32[]{:S(2)}, u32[]{:S(2)}) collective-permute-start(bf16[256,512]{1,0:T(8,128)(2,1)} %param.6), channel_id=1, source_target_pairs={{0,2},{1,3},{2,4},{3,5},{4,6},{5,7},{6,8},{7,9},{8,10},{9,11},{10,... | collective-permute-start | bytes 786440 | tf_op jit(solution)/shard_map/ppermute | solution.py:36
  12.5 8.6 %collective-permute-start.2 = (bf16[256,512]{1,0:T(8,128)(2,1)}, bf16[256,512]{1,0:T(8,128)(2,1)S(1)}, u32[]{:S(2)}, u32[]{:S(2)}) collective-permute-start(bf16[256,512]{1,0:T(8,128)(2,1)} %param.6), channel_id=1, source_target_pairs={{0,14},{1,15},{2,0},{3,1},{4,2},{5,3},{6,4},{7,5},{8,6},{9,7},{10,... | collective-permute-start | bytes 786440 | tf_op jit(solution)/shard_map/ppermute | solution.py:39
  21.1 4.3 %collective-permute-done = bf16[256,512]{1,0:T(8,128)(2,1)S(1)} collective-permute-done((bf16[256,512]{1,0:T(8,128)(2,1)}, bf16[256,512]{1,0:T(8,128)(2,1)S(1)}, u32[]{:S(2)}, u32[]{:S(2)}) %collective-permute-start) | collective-permute-done | bytes 262176 | tf_op jit(solution)/shard_map/ppermute | solution.py:36
  25.4 1.9 collective-permute-start.1
  27.3 4.6 %collective-permute-start.3 = (bf16[256,512]{1,0:T(8,128)(2,1)S(1)}, bf16[256,512]{1,0:T(8,128)(2,1)S(1)}, u32[]{:S(2)}, u32[]{:S(2)}) collective-permute-start(bf16[256,512]{1,0:T(8,128)(2,1)S(1)} %collective-permute-done.2), channel_id=1, source_target_pairs={{0,14},{1,15},{2,0},{3,1},{4,2},{5,3},{6,4},{7,5},{8,6},{9,7},{10,... | collective-permute-start | bytes 786440 | tf_op jit(solution)/shard_map/ppermute | solution.py:39
  31.9 5.2 %collective-permute-done.1 = bf16[256,512]{1,0:T(8,128)(2,1)S(1)} collective-permute-done((bf16[256,512]{1,0:T(8,128)(2,1)S(1)}, bf16[256,512]{1,0:T(8,128)(2,1)S(1)}, u32[]{:S(2)}, u32[]{:S(2)}) %collective-permute-start.1) | collective-permute-done | bytes 262176 | tf_op jit(solution)/shard_map/ppermute | solution.py:36
  37.0 0.2 collective-permute-done.3
  37.2 20.6 %all-gather.5.cloned.1.call-done = bf16[4096,256]{1,0:T(8,128)(2,1)} async-done(((bf16[256,256]{1,0:T(8,128)(2,1)}), bf16[4096,256]{1,0:T(8,128)(2,1)}) %all-gather.5.cloned.1.call-update) | async-done | bytes 2097168 | tf_op jit(solution)/shard_map/all_gather | solution.py:74
  57.8 2.3 %fusion.16 = bf16[256,256]{1,0:T(8,128)(2,1)S(1)} fusion(bf16[256,4096]{1,0:T(8,128)(2,1)S(1)} %copy-done, bf16[4096,256]{1,0:T(8,128)(2,1)} %all-gather.5.cloned.1.call-done), kind=kOutput, calls=%fused_computation.24 | convolution fusion | flops 536936448 | bytes 4325376 | tf_op jit(solution)/shard_map/dot_general | solution.py:78
  60.1 3.2 %collective-permute-start.8 = (bf16[256,256]{1,0:T(8,128)(2,1)S(1)}, bf16[256,256]{1,0:T(8,128)(2,1)S(1)}, u32[]{:S(2)}, u32[]{:S(2)}) collective-permute-start(bf16[256,256]{1,0:T(8,128)(2,1)S(1)} %fusion.16), channel_id=1, source_target_pairs={{0,1},{1,2},{2,3},{3,4},{4,5},{5,6},{6,7},{7,8},{8,9},{9,10},{10,1... | collective-permute-start | bytes 393224 | tf_op jit(solution)/shard_map/ppermute | solution.py:12
  63.3 12.2 %all-gather = bf16[1024,256]{1,0:T(8,128)(2,1)} all-gather(bf16[256,256]{1,0:T(8,128)(2,1)S(1)} %fusion.16), channel_id=2, replica_groups=mesh['cy'=8,'cx'=4,'fsdp'=16] {'cx'}, dimensions={0}, use_global_device_ids=true | all-gather | bytes 655360 | tf_op jit(solution)/shard_map/all_gather | solution.py:82
  75.5 0.6 copy-done.7
  76.2 0.0 all-gather.7.cloned.1.call-update
  76.2 2.1 collective-permute-start.4
  78.3 7.7 %collective-permute-done.4 = bf16[256,512]{1,0:T(8,128)(2,1)S(1)} collective-permute-done((bf16[256,512]{1,0:T(8,128)(2,1)S(1)}, bf16[256,512]{1,0:T(8,128)(2,1)S(1)}, u32[]{:S(2)}, u32[]{:S(2)}) %collective-permute-start.4) | collective-permute-done | bytes 262176 | tf_op jit(solution)/shard_map/ppermute | solution.py:36
  85.9 1.9 collective-permute-start.5
  87.9 4.6 %collective-permute-start.6 = (bf16[256,512]{1,0:T(8,128)(2,1)S(1)}, bf16[256,512]{1,0:T(8,128)(2,1)S(1)}, u32[]{:S(2)}, u32[]{:S(2)}) collective-permute-start(bf16[256,512]{1,0:T(8,128)(2,1)S(1)} %collective-permute-done.3), channel_id=1, source_target_pairs={{0,14},{1,15},{2,0},{3,1},{4,2},{5,3},{6,4},{7,5},{8,6},{9,7},{10,... | collective-permute-start | bytes 786440 | tf_op jit(solution)/shard_map/ppermute | solution.py:39
  92.4 2.4 %collective-permute-done.5 = bf16[256,512]{1,0:T(8,128)(2,1)S(1)} collective-permute-done((bf16[256,512]{1,0:T(8,128)(2,1)S(1)}, bf16[256,512]{1,0:T(8,128)(2,1)S(1)}, u32[]{:S(2)}, u32[]{:S(2)}) %collective-permute-start.5) | collective-permute-done | bytes 262176 | tf_op jit(solution)/shard_map/ppermute | solution.py:36
  94.8 0.9 bitcast_dynamic-update-slice_fusion.22
  95.7 0.8 bitcast_dynamic-update-slice_fusion.19
  96.6 0.9 bitcast_dynamic-update-slice_fusion.16
  97.4 0.8 bitcast_dynamic-update-slice_fusion.13
  98.3 0.8 bitcast_dynamic-update-slice_fusion.10
  99.1 0.8 bitcast_dynamic-update-slice_fusion.7
  100.0 0.9 bitcast_dynamic-update-slice_fusion.4
  100.8 0.7 copy-done.4
  101.5 0.8 bitcast_dynamic-update-slice_fusion.1
  102.4 4.8 %collective-permute-start.7 = (bf16[8,256,512]{2,1,0:T(8,128)(2,1)}, bf16[8,256,512]{2,1,0:T(8,128)(2,1)}, u32[]{:S(2)}, u32[]{:S(2)}) collective-permute-start(bf16[8,256,512]{2,1,0:T(8,128)(2,1)} %get-tuple-element.21), channel_id=1, source_target_pairs={{0,1},{1,0},{2,3},{3,2},{4,5},{5,4},{6,7},{7,6},{8,9},{9,8},{10,11... | collective-permute-start | bytes 6291464 | tf_op jit(solution)/shard_map/ppermute | solution.py:42
  107.2 1.7 bitcast_dynamic-update-slice_fusion.23
  108.9 1.7 bitcast_dynamic-update-slice_fusion.20
  110.6 0.7 bitcast_dynamic-update-slice_fusion.17
  111.3 0.7 bitcast_dynamic-update-slice_fusion.14
  112.0 0.7 bitcast_dynamic-update-slice_fusion.11
  112.7 0.7 bitcast_dynamic-update-slice_fusion.8
  113.5 0.7 bitcast_dynamic-update-slice_fusion.5
  114.2 1.7 bitcast_dynamic-update-slice_fusion.2
  115.9 4.5 %select_bitcast_fusion.1 = (bf16[8,1,256,512]{3,2,1,0:T(8,128)(2,1)S(1)}, bf16[8,1,256,512]{3,2,1,0:T(8,128)(2,1)S(1)}) fusion(pred[]{:T(512)S(6)} %eq.15, bf16[16,256,512]{2,1,0:T(8,128)(2,1)} %bitcast_dynamic-update-slice_fusion.2, s32[]{:T(128)S(6)} %select_n.115, bf16[8,256,512]{2,1,0:T(8,128)(2,1)} %collective-permute-done.7), kind=kLoop, calls=%fused_computation.14 | loop fusion | flops 4194304 | bytes 8388613 | tf_op jit(solution)/shard_map/stack | solution.py:54
  120.4 0.4 pad_maximum_fusion
  120.8 1.3 convolution_convert_fusion.1
  122.1 0.7 gather_fusion
  122.8 9.3 %all-gather.7.cloned.1.call-done = bf16[32,256,256]{2,1,0:T(8,128)(2,1)} async-done(((bf16[4,256,256]{2,1,0:T(8,128)(2,1)}), bf16[32,256,256]{2,1,0:T(8,128)(2,1)}) %all-gather.7.cloned.1.call-update) | async-done | bytes 4194320 | tf_op jit(solution)/shard_map/all_gather | solution.py:84
  132.1 4.6 %copy.32 = bf16[4,8,256,256]{3,1,2,0:T(8,128)(2,1)S(1)} copy(bf16[4,8,256,256]{3,2,1,0:T(8,128)(2,1)} %bitcast.91) | data formatting | bytes 8388608
  136.7 0.8 convolution_convert_fusion
  137.5 1.8 copy.33
  139.3 8.1 %all-to-all-start = ((bf16[16,256,256]{2,1,0:T(8,128)(2,1)}), bf16[16,256,256]{2,1,0:T(8,128)(2,1)}, u32[]{:S(2)}, u32[]{:S(2)}) async-start(bf16[16,256,256]{2,1,0:T(8,128)(2,1)} %bitcast.90), calls=%async_computation | async-start | bytes 4194304 | tf_op jit(solution)/shard_map/all_to_all | solution.py:103
  147.3 0.1 fusion.19
  147.5 0.1 constant_dynamic-slice_fusion.1
  147.6 0.5 fusion.43
  151.8 1.8 convolution_bitcast_fusion.2
  153.6 1.4 add_add_fusion
  155.0 41.4 %all-to-all-done = bf16[16,256,256]{2,1,0:T(8,128)(2,1)} async-done(((bf16[16,256,256]{2,1,0:T(8,128)(2,1)}), bf16[16,256,256]{2,1,0:T(8,128)(2,1)}, u32[]{:S(2)}, u32[]{:S(2)}) %all-to-all-start) | async-done | bytes 2097184 | tf_op jit(solution)/shard_map/all_to_all | solution.py:103
  196.4 1.1 constant_dynamic-slice_fusion
  197.5 2.4 %collective-permute-start.9 = (bf16[512,256]{1,0:T(8,128)(2,1)S(1)}, bf16[512,256]{1,0:T(8,128)(2,1)S(1)}, u32[]{:S(2)}, u32[]{:S(2)}) collective-permute-start(bf16[512,256]{1,0:T(8,128)(2,1)S(1)} %bitcast.97), channel_id=1, source_target_pairs={{0,1},{1,0},{2,3},{3,2},{4,5},{5,4},{6,7},{7,6},{8,9},{9,8},{10,11... | collective-permute-start | bytes 786440 | tf_op jit(solution)/shard_map/ppermute | solution.py:61
  200.0 0.4 convolution_bitcast_fusion.1
  200.4 0.6 collective-permute-done.9
  200.9 0.4 convolution_bitcast_fusion
  201.4 0.8 fusion.18
  202.1 1.4 fusion.1
  203.6 1.6 fusion.13
  205.1 0.8 copy.25
  (30 shorter events, 0.1 us)
Async XLA Ops:
  6.5 51.3 %copy-start = (bf16[256,4096]{1,0:T(8,128)(2,1)S(1)}, bf16[256,4096]{1,0:T(8,128)(2,1)}, u32[]{:S(2)}) copy-start(bf16[256,4096]{1,0:T(8,128)(2,1)} %param.5) | copy-start | bytes 6291460
  6.5 51.3 %all-gather.5.cloned.1.call-start = ((), (), s32[]{:S(2)}) async-start(), calls=%async_computation.1 | async-start | bytes 2228224 | tf_op jit(solution)/shard_map/all_gather | solution.py:74
  8.3 90.0 %copy-start.3 = (bf16[256,512]{1,0:T(8,128)(2,1)S(1)}, bf16[256,512]{1,0:T(8,128)(2,1)}, u32[]{:S(2)}) copy-start(bf16[256,512]{1,0:T(8,128)(2,1)} %param.6) | copy-start | bytes 786436
  8.3 123.9 %all-gather.7.cloned.1.call-start = ((), (), s32[]{:S(2)}) async-start(), calls=%async_computation.2 | async-start | bytes 4718592 | tf_op jit(solution)/shard_map/all_gather | solution.py:84
  8.3 17.0 %collective-permute-start = (bf16[256,512]{1,0:T(8,128)(2,1)}, bf16[256,512]{1,0:T(8,128)(2,1)S(1)}, u32[]{:S(2)}, u32[]{:S(2)}) collective-permute-start(bf16[256,512]{1,0:T(8,128)(2,1)} %param.6), channel_id=1, source_target_pairs={{0,2},{1,3},{2,4},{3,5},{4,6},{5,7},{6,8},{7,9},{8,10},{9,11},{10,... | collective-permute-start | bytes 786440 | tf_op jit(solution)/shard_map/ppermute | solution.py:36
  12.5 14.8 %collective-permute-start.2 = (bf16[256,512]{1,0:T(8,128)(2,1)}, bf16[256,512]{1,0:T(8,128)(2,1)S(1)}, u32[]{:S(2)}, u32[]{:S(2)}) collective-permute-start(bf16[256,512]{1,0:T(8,128)(2,1)} %param.6), channel_id=1, source_target_pairs={{0,14},{1,15},{2,0},{3,1},{4,2},{5,3},{6,4},{7,5},{8,6},{9,7},{10,... | collective-permute-start | bytes 786440 | tf_op jit(solution)/shard_map/ppermute | solution.py:39
  25.4 11.7 %collective-permute-start.1 = (bf16[256,512]{1,0:T(8,128)(2,1)S(1)}, bf16[256,512]{1,0:T(8,128)(2,1)S(1)}, u32[]{:S(2)}, u32[]{:S(2)}) collective-permute-start(bf16[256,512]{1,0:T(8,128)(2,1)S(1)} %collective-permute-done), channel_id=1, source_target_pairs={{0,2},{1,3},{2,4},{3,5},{4,6},{5,7},{6,8},{7,9},{8,10},{9,11},{10,... | collective-permute-start | bytes 786440 | tf_op jit(solution)/shard_map/ppermute | solution.py:36
  27.3 9.9 %collective-permute-start.3 = (bf16[256,512]{1,0:T(8,128)(2,1)S(1)}, bf16[256,512]{1,0:T(8,128)(2,1)S(1)}, u32[]{:S(2)}, u32[]{:S(2)}) collective-permute-start(bf16[256,512]{1,0:T(8,128)(2,1)S(1)} %collective-permute-done.2), channel_id=1, source_target_pairs={{0,14},{1,15},{2,0},{3,1},{4,2},{5,3},{6,4},{7,5},{8,6},{9,7},{10,... | collective-permute-start | bytes 786440 | tf_op jit(solution)/shard_map/ppermute | solution.py:39
  60.1 15.4 %collective-permute-start.8 = (bf16[256,256]{1,0:T(8,128)(2,1)S(1)}, bf16[256,256]{1,0:T(8,128)(2,1)S(1)}, u32[]{:S(2)}, u32[]{:S(2)}) collective-permute-start(bf16[256,256]{1,0:T(8,128)(2,1)S(1)} %fusion.16), channel_id=1, source_target_pairs={{0,1},{1,2},{2,3},{3,4},{4,5},{5,6},{6,7},{7,8},{8,9},{9,10},{10,1... | collective-permute-start | bytes 393224 | tf_op jit(solution)/shard_map/ppermute | solution.py:12
  75.5 0.6 copy-start.7
  76.2 9.7 %collective-permute-start.4 = (bf16[256,512]{1,0:T(8,128)(2,1)S(1)}, bf16[256,512]{1,0:T(8,128)(2,1)S(1)}, u32[]{:S(2)}, u32[]{:S(2)}) collective-permute-start(bf16[256,512]{1,0:T(8,128)(2,1)S(1)} %collective-permute-done.1), channel_id=1, source_target_pairs={{0,2},{1,3},{2,4},{3,5},{4,6},{5,7},{6,8},{7,9},{8,10},{9,11},{10,... | collective-permute-start | bytes 786440 | tf_op jit(solution)/shard_map/ppermute | solution.py:36
  85.9 16.4 %copy-start.5 = (bf16[256,512]{1,0:T(8,128)(2,1)}, bf16[256,512]{1,0:T(8,128)(2,1)S(1)}, u32[]{:S(2)}) copy-start(bf16[256,512]{1,0:T(8,128)(2,1)S(1)} %collective-permute-done.4) | copy-start | bytes 786436
  85.9 8.9 %collective-permute-start.5 = (bf16[256,512]{1,0:T(8,128)(2,1)S(1)}, bf16[256,512]{1,0:T(8,128)(2,1)S(1)}, u32[]{:S(2)}, u32[]{:S(2)}) collective-permute-start(bf16[256,512]{1,0:T(8,128)(2,1)S(1)} %collective-permute-done.4), channel_id=1, source_target_pairs={{0,2},{1,3},{2,4},{3,5},{4,6},{5,7},{6,8},{7,9},{8,10},{9,11},{10,... | collective-permute-start | bytes 786440 | tf_op jit(solution)/shard_map/ppermute | solution.py:36
  87.9 13.0 %collective-permute-start.6 = (bf16[256,512]{1,0:T(8,128)(2,1)S(1)}, bf16[256,512]{1,0:T(8,128)(2,1)S(1)}, u32[]{:S(2)}, u32[]{:S(2)}) collective-permute-start(bf16[256,512]{1,0:T(8,128)(2,1)S(1)} %collective-permute-done.3), channel_id=1, source_target_pairs={{0,14},{1,15},{2,0},{3,1},{4,2},{5,3},{6,4},{7,5},{8,6},{9,7},{10,... | collective-permute-start | bytes 786440 | tf_op jit(solution)/shard_map/ppermute | solution.py:39
  94.8 7.5 %copy-start.6 = (bf16[256,512]{1,0:T(8,128)(2,1)}, bf16[256,512]{1,0:T(8,128)(2,1)S(1)}, u32[]{:S(2)}) copy-start(bf16[256,512]{1,0:T(8,128)(2,1)S(1)} %collective-permute-done.5) | copy-start | bytes 786436
  100.8 0.7 copy-start.4
  102.4 13.5 %collective-permute-start.7 = (bf16[8,256,512]{2,1,0:T(8,128)(2,1)}, bf16[8,256,512]{2,1,0:T(8,128)(2,1)}, u32[]{:S(2)}, u32[]{:S(2)}) collective-permute-start(bf16[8,256,512]{2,1,0:T(8,128)(2,1)} %get-tuple-element.21), channel_id=1, source_target_pairs={{0,1},{1,0},{2,3},{3,2},{4,5},{5,4},{6,7},{7,6},{8,9},{9,8},{10,11... | collective-permute-start | bytes 6291464 | tf_op jit(solution)/shard_map/ppermute | solution.py:42
  120.8 1.3 copy-start.1
  137.5 14.3 %copy-start.8 = (bf16[256,256]{1,0:T(8,128)(2,1)S(1)}, bf16[256,256]{1,0:T(8,128)(2,1)}, u32[]{:S(2)}) copy-start(bf16[256,256]{1,0:T(8,128)(2,1)} %copy-done.7) | copy-start | bytes 393220
  139.3 57.1 %all-to-all-start = ((bf16[16,256,256]{2,1,0:T(8,128)(2,1)}), bf16[16,256,256]{2,1,0:T(8,128)(2,1)}, u32[]{:S(2)}, u32[]{:S(2)}) async-start(bf16[16,256,256]{2,1,0:T(8,128)(2,1)} %bitcast.90), calls=%async_computation | async-start | bytes 4194304 | tf_op jit(solution)/shard_map/all_to_all | solution.py:103
  196.4 5.0 %copy-start.2 = (f32[4,256,512]{1,2,0:T(8,128)S(1)}, f32[4,256,512]{1,2,0:T(8,128)}, u32[]{:S(2)}) copy-start(f32[4,256,512]{1,2,0:T(8,128)} %convolution_bitcast_fusion.2) | copy-start | bytes 6291460
  197.5 3.4 %collective-permute-start.9 = (bf16[512,256]{1,0:T(8,128)(2,1)S(1)}, bf16[512,256]{1,0:T(8,128)(2,1)S(1)}, u32[]{:S(2)}, u32[]{:S(2)}) collective-permute-start(bf16[512,256]{1,0:T(8,128)(2,1)S(1)} %bitcast.97), channel_id=1, source_target_pairs={{0,1},{1,0},{2,3},{3,2},{4,5},{5,4},{6,7},{7,6},{8,9},{9,8},{10,11... | collective-permute-start | bytes 786440 | tf_op jit(solution)/shard_map/ppermute | solution.py:61
Sparse Core Ops, SparseCore 0:
  9.5 48.2 all-gather.4
  76.3 55.7 all-gather.6

commit v7 on v5

--- a/solution.py
+++ b/solution.py
@@ -92,13 +92,7 @@
 
     dest_block = group_index * blocks_group + jnp.arange(lane_count, dtype=jnp.int32) // 2
     dest_pick = chosen[dest_block, jnp.arange(lane_count, dtype=jnp.int32) % 2]
-    sources = candidates.shape[0]
-    pick_hot = (
-        (dest_pick // blocks_group)[:, None] == jnp.arange(sources, dtype=jnp.int32)[None, :]
-    ).astype(candidates.dtype)
-    outgoing = jnp.dot(
-        pick_hot, candidates.reshape(sources, -1), preferred_element_type=jnp.float32
-    ).astype(candidates.dtype).reshape((lane_count,) + candidates.shape[1:])
+    outgoing = jnp.take(candidates, dest_pick // blocks_group, axis=0, mode="clip")
     incoming = lax.all_to_all(outgoing, "fsdp", split_axis=0, concat_axis=0, tiled=True)
 
     mine = lax.dynamic_index_in_dim(chosen, my_block, 0, keepdims=False)

time: 215 us -> 212 us (0.986)
  local copies, waits for them, and re-layouts: 25.8 us -> 23.6 us
    unnamed x30 -> x28, local copies, waits for them, and re-layouts: 19.9 us -> 13.6 us
    gather x0 -> x1, local copies, waits for them, and re-layouts: none -> 4.23 us  [per_device(): jnp.take(candidates, dest_pick // blocks_group, axis=0, mode='clip')]
  transfers between devices with their start and end apart: 13 -> 13, of which waited for: 9 -> 9; matrix products, arithmetic and copies ran while one was open for 12% -> 13% of each run, Pallas kernels for 0% -> 0%
where the time goes in v7:
time: 212 us
  waiting for transfers between devices  88.3 us (42%)
  starting transfers between devices  53.7 us (25%)
  local copies, waits for them, and re-layouts  23.6 us (11%)
  between operations  17.4 us (8%)
  blocking collectives  10.6 us (5%)
  other arithmetic  10.4 us (5%)
  matrix products  7.73 us (4%)
    ppermute x1, waiting for transfers between devices, from_behind(): return lax.ppermute(array, axis, pairs)  39.2 us
    all_gather x1, waiting for transfers between devices, per_device(): lax.all_gather(jnp.concatenate([key_weight, value_weight], axis=1), 'fsdp...  20.6 us
    ppermute x3, starting transfers between devices, ring_gather_rows(): behind = lax.ppermute(behind, axis, shift_pairs(-2))  17.7 us
    ppermute x4, waiting for transfers between devices, ring_gather_rows(): ahead = lax.ppermute(ahead, axis, shift_pairs(2))  16.6 us
    unnamed x28, local copies, waits for them, and re-layouts  13.6 us
    all_gather x1, waiting for transfers between devices, per_device(): lax.all_gather(along_x[None], 'cy', axis=0, tiled=True)  11 us
    ppermute x4, starting transfers between devices, ring_gather_rows(): ahead = lax.ppermute(ahead, axis, shift_pairs(2))  11 us
    all_gather x1, blocking collectives, per_device(): along_x = lax.all_gather(key_value[None], 'cx', axis=0, tiled=True)  10.6 us
  transfers between devices with their start and end apart: 13, of which 9 were waited for; matrix products, arithmetic and copies ran while one was open for 13% of the time, Pallas kernels for 0%

profile of v7, /device:TPU:7, one launch (start us, length us, event | category | flops | bytes accessed | tf_op | source)
XLA Modules:
  0.0 211.8 jit_solution(5109586770303646003)
XLA Ops:
  6.5 1.7 pad_maximum_fusion.2
  8.2 0.0 all-gather.5.cloned.1.call-update
  8.3 0.0 copy-start.3
  8.3 0.0 all-gather.7.cloned.1.call-start
  8.3 4.1 %collective-permute-start = (bf16[256,512]{1,0:T(8,128)(2,1)}, bf16[256,512]{1,0:T(8,128)(2,1)S(1)}, u32[]{:S(2)}, u32[]{:S(2)}) collective-permute-start(bf16[256,512]{1,0:T(8,128)(2,1)} %param.6), channel_id=1, source_target_pairs={{0,2},{1,3},{2,4},{3,5},{4,6},{5,7},{6,8},{7,9},{8,10},{9,11},{10,... | collective-permute-start | bytes 786440 | tf_op jit(solution)/shard_map/ppermute | solution.py:36
  12.5 8.6 %collective-permute-start.2 = (bf16[256,512]{1,0:T(8,128)(2,1)}, bf16[256,512]{1,0:T(8,128)(2,1)S(1)}, u32[]{:S(2)}, u32[]{:S(2)}) collective-permute-start(bf16[256,512]{1,0:T(8,128)(2,1)} %param.6), channel_id=1, source_target_pairs={{0,14},{1,15},{2,0},{3,1},{4,2},{5,3},{6,4},{7,5},{8,6},{9,7},{10,... | collective-permute-start | bytes 786440 | tf_op jit(solution)/shard_map/ppermute | solution.py:39
  21.1 4.3 %collective-permute-done = bf16[256,512]{1,0:T(8,128)(2,1)S(1)} collective-permute-done((bf16[256,512]{1,0:T(8,128)(2,1)}, bf16[256,512]{1,0:T(8,128)(2,1)S(1)}, u32[]{:S(2)}, u32[]{:S(2)}) %collective-permute-start) | collective-permute-done | bytes 262176 | tf_op jit(solution)/shard_map/ppermute | solution.py:36
  25.4 1.9 collective-permute-start.1
  27.3 0.0 collective-permute-done.2
  27.3 4.6 %collective-permute-start.3 = (bf16[256,512]{1,0:T(8,128)(2,1)S(1)}, bf16[256,512]{1,0:T(8,128)(2,1)S(1)}, u32[]{:S(2)}, u32[]{:S(2)}) collective-permute-start(bf16[256,512]{1,0:T(8,128)(2,1)S(1)} %collective-permute-done.2), channel_id=1, source_target_pairs={{0,14},{1,15},{2,0},{3,1},{4,2},{5,3},{6,4},{7,5},{8,6},{9,7},{10,... | collective-permute-start | bytes 786440 | tf_op jit(solution)/shard_map/ppermute | solution.py:39
  31.9 5.2 %collective-permute-done.1 = bf16[256,512]{1,0:T(8,128)(2,1)S(1)} collective-permute-done((bf16[256,512]{1,0:T(8,128)(2,1)S(1)}, bf16[256,512]{1,0:T(8,128)(2,1)S(1)}, u32[]{:S(2)}, u32[]{:S(2)}) %collective-permute-start.1) | collective-permute-done | bytes 262176 | tf_op jit(solution)/shard_map/ppermute | solution.py:36
  37.0 0.2 collective-permute-done.3
  37.2 20.6 %all-gather.5.cloned.1.call-done = bf16[4096,256]{1,0:T(8,128)(2,1)} async-done(((bf16[256,256]{1,0:T(8,128)(2,1)}), bf16[4096,256]{1,0:T(8,128)(2,1)}) %all-gather.5.cloned.1.call-update) | async-done | bytes 2097168 | tf_op jit(solution)/shard_map/all_gather | solution.py:74
  57.8 2.3 %fusion.16 = bf16[256,256]{1,0:T(8,128)(2,1)S(1)} fusion(bf16[256,4096]{1,0:T(8,128)(2,1)S(1)} %copy-done, bf16[4096,256]{1,0:T(8,128)(2,1)} %all-gather.5.cloned.1.call-done), kind=kOutput, calls=%fused_computation.24 | convolution fusion | flops 536936448 | bytes 4325376 | tf_op jit(solution)/shard_map/dot_general | solution.py:78
  60.1 10.6 %all-gather = bf16[1024,256]{1,0:T(8,128)(2,1)} all-gather(bf16[256,256]{1,0:T(8,128)(2,1)S(1)} %fusion.16), channel_id=2, replica_groups=mesh['cy'=8,'cx'=4,'fsdp'=16] {'cx'}, dimensions={0}, use_global_device_ids=true | all-gather | bytes 655360 | tf_op jit(solution)/shard_map/all_gather | solution.py:81
  70.8 0.0 all-gather.7.cloned.1.call-update
  70.8 3.0 %collective-permute-start.4 = (bf16[256,512]{1,0:T(8,128)(2,1)S(1)}, bf16[256,512]{1,0:T(8,128)(2,1)S(1)}, u32[]{:S(2)}, u32[]{:S(2)}) collective-permute-start(bf16[256,512]{1,0:T(8,128)(2,1)S(1)} %collective-permute-done.1), channel_id=1, source_target_pairs={{0,2},{1,3},{2,4},{3,5},{4,6},{5,7},{6,8},{7,9},{8,10},{9,11},{10,... | collective-permute-start | bytes 786440 | tf_op jit(solution)/shard_map/ppermute | solution.py:36
  73.8 5.3 %collective-permute-done.4 = bf16[256,512]{1,0:T(8,128)(2,1)S(1)} collective-permute-done((bf16[256,512]{1,0:T(8,128)(2,1)S(1)}, bf16[256,512]{1,0:T(8,128)(2,1)S(1)}, u32[]{:S(2)}, u32[]{:S(2)}) %collective-permute-start.4) | collective-permute-done | bytes 262176 | tf_op jit(solution)/shard_map/ppermute | solution.py:36
  79.1 1.9 collective-permute-start.5
  81.0 4.6 %collective-permute-start.6 = (bf16[256,512]{1,0:T(8,128)(2,1)S(1)}, bf16[256,512]{1,0:T(8,128)(2,1)S(1)}, u32[]{:S(2)}, u32[]{:S(2)}) collective-permute-start(bf16[256,512]{1,0:T(8,128)(2,1)S(1)} %collective-permute-done.3), channel_id=1, source_target_pairs={{0,14},{1,15},{2,0},{3,1},{4,2},{5,3},{6,4},{7,5},{8,6},{9,7},{10,... | collective-permute-start | bytes 786440 | tf_op jit(solution)/shard_map/ppermute | solution.py:39
  85.6 1.8 collective-permute-done.5
  87.4 0.9 bitcast_dynamic-update-slice_fusion.22
  88.3 0.8 bitcast_dynamic-update-slice_fusion.19
  89.1 0.8 bitcast_dynamic-update-slice_fusion.16
  90.0 0.8 bitcast_dynamic-update-slice_fusion.13
  90.8 0.8 bitcast_dynamic-update-slice_fusion.10
  91.6 0.8 bitcast_dynamic-update-slice_fusion.7
  92.5 0.8 bitcast_dynamic-update-slice_fusion.4
  93.3 0.0 collective-permute-done.6
  93.3 0.7 copy-done.4
  94.0 0.8 bitcast_dynamic-update-slice_fusion.1
  94.9 7.6 %collective-permute-start.7 = (bf16[8,256,512]{2,1,0:T(8,128)(2,1)}, bf16[8,256,512]{2,1,0:T(8,128)(2,1)}, u32[]{:S(2)}, u32[]{:S(2)}) collective-permute-start(bf16[8,256,512]{2,1,0:T(8,128)(2,1)} %get-tuple-element.17), channel_id=1, source_target_pairs={{0,1},{1,0},{2,3},{3,2},{4,5},{5,4},{6,7},{7,6},{8,9},{9,8},{10,11... | collective-permute-start | bytes 6291464 | tf_op jit(solution)/shard_map/ppermute | solution.py:42
  102.5 1.7 bitcast_dynamic-update-slice_fusion.23
  104.2 1.7 bitcast_dynamic-update-slice_fusion.20
  105.9 0.7 bitcast_dynamic-update-slice_fusion.17
  106.6 0.7 bitcast_dynamic-update-slice_fusion.14
  107.3 0.7 bitcast_dynamic-update-slice_fusion.11
  108.0 0.7 bitcast_dynamic-update-slice_fusion.8
  108.7 0.7 bitcast_dynamic-update-slice_fusion.5
  109.5 1.7 bitcast_dynamic-update-slice_fusion.2
  111.2 4.5 %select_bitcast_fusion.1 = (bf16[8,1,256,512]{3,2,1,0:T(8,128)(2,1)S(1)}, bf16[8,1,256,512]{3,2,1,0:T(8,128)(2,1)S(1)}) fusion(pred[]{:T(512)S(6)} %eq.14, bf16[16,256,512]{2,1,0:T(8,128)(2,1)} %bitcast_dynamic-update-slice_fusion.2, s32[]{:T(128)S(6)} %select_n.118, bf16[8,256,512]{2,1,0:T(8,128)(2,1)} %collective-permute-done.7), kind=kLoop, calls=%fused_computation.14 | loop fusion | flops 4194304 | bytes 8388613 | tf_op jit(solution)/shard_map/stack | solution.py:54
  115.7 0.4 pad_maximum_fusion
  116.1 0.0 copy-start.1
  116.1 1.3 convolution_convert_fusion
  117.4 0.7 gather_fusion
  118.2 11.0 %all-gather.7.cloned.1.call-done = bf16[32,256,256]{2,1,0:T(8,128)(2,1)} async-done(((bf16[4,256,256]{2,1,0:T(8,128)(2,1)}), bf16[32,256,256]{2,1,0:T(8,128)(2,1)}) %all-gather.7.cloned.1.call-update) | async-done | bytes 4194320 | tf_op jit(solution)/shard_map/all_gather | solution.py:82
  129.2 4.2 %gather_fusion.1 = bf16[16,256,256]{2,1,0:T(8,128)(2,1)} fusion(bf16[32,256,256]{2,1,0:T(8,128)(2,1)} %all-gather.7.cloned.1.call-done, s32[1024]{0:T(1024)S(1)} %pad_clamp_fusion), kind=kCustom, calls=%fused_computation.1 | custom fusion | bytes 4194368 | tf_op jit(solution)/shard_map/jit(_take)/gather | solution.py:95
  133.4 8.1 %all-to-all-start = ((bf16[16,256,256]{2,1,0:T(8,128)(2,1)}), bf16[16,256,256]{2,1,0:T(8,128)(2,1)}, u32[]{:S(2)}, u32[]{:S(2)}) async-start(bf16[16,256,256]{2,1,0:T(8,128)(2,1)} %gather_fusion.1), calls=%async_computation | async-start | bytes 4194304 | tf_op jit(solution)/shard_map/all_to_all | solution.py:96
  141.5 0.1 fusion.19
  141.6 3.5 %collective-permute-start.8 = (bf16[256,256]{1,0:T(8,128)(2,1)S(1)}, bf16[256,256]{1,0:T(8,128)(2,1)S(1)}, u32[]{:S(2)}, u32[]{:S(2)}) collective-permute-start(bf16[256,256]{1,0:T(8,128)(2,1)S(1)} %fusion.16), channel_id=1, source_target_pairs={{0,1},{1,2},{2,3},{3,4},{4,5},{5,6},{6,7},{7,8},{8,9},{9,10},{10,1... | collective-permute-start | bytes 393224 | tf_op jit(solution)/shard_map/ppermute | solution.py:12
  145.2 0.1 constant_dynamic-slice_fusion.1
  145.3 0.5 fusion.43
  149.5 39.2 %collective-permute-done.8 = bf16[256,256]{1,0:T(8,128)(2,1)S(1)} collective-permute-done((bf16[256,256]{1,0:T(8,128)(2,1)S(1)}, bf16[256,256]{1,0:T(8,128)(2,1)S(1)}, u32[]{:S(2)}, u32[]{:S(2)}) %collective-permute-start.8) | collective-permute-done | bytes 131104 | tf_op jit(solution)/shard_map/ppermute | solution.py:12
  188.7 1.7 convolution_bitcast_fusion.2
  190.4 1.4 add_add_fusion
  191.8 1.1 constant_dynamic-slice_fusion
  193.0 5.8 %collective-permute-start.9 = (bf16[512,256]{1,0:T(8,128)(2,1)S(1)}, bf16[512,256]{1,0:T(8,128)(2,1)S(1)}, u32[]{:S(2)}, u32[]{:S(2)}) collective-permute-start(bf16[512,256]{1,0:T(8,128)(2,1)S(1)} %bitcast.100), channel_id=1, source_target_pairs={{0,1},{1,0},{2,3},{3,2},{4,5},{5,4},{6,7},{7,6},{8,9},{9,8},{10,11... | collective-permute-start | bytes 786440 | tf_op jit(solution)/shard_map/ppermute | solution.py:61
  198.8 0.4 convolution_bitcast_fusion.1
  199.2 0.7 collective-permute-done.9
  199.9 0.4 convolution_bitcast_fusion
  200.3 0.8 fusion.18
  201.1 1.4 fusion.1
  202.5 1.6 fusion.13
  204.1 0.8 copy.25
  (25 shorter events, 0.1 us)
Async XLA Ops:
  6.5 51.3 %copy-start = (bf16[256,4096]{1,0:T(8,128)(2,1)S(1)}, bf16[256,4096]{1,0:T(8,128)(2,1)}, u32[]{:S(2)}) copy-start(bf16[256,4096]{1,0:T(8,128)(2,1)} %param.5) | copy-start | bytes 6291460
  6.5 51.3 %all-gather.5.cloned.1.call-start = ((), (), s32[]{:S(2)}) async-start(), calls=%async_computation.1 | async-start | bytes 2228224 | tf_op jit(solution)/shard_map/all_gather | solution.py:74
  8.3 82.6 %copy-start.3 = (bf16[256,512]{1,0:T(8,128)(2,1)S(1)}, bf16[256,512]{1,0:T(8,128)(2,1)}, u32[]{:S(2)}) copy-start(bf16[256,512]{1,0:T(8,128)(2,1)} %param.6) | copy-start | bytes 786436
  8.3 120.9 %all-gather.7.cloned.1.call-start = ((), (), s32[]{:S(2)}) async-start(), calls=%async_computation.2 | async-start | bytes 4718592 | tf_op jit(solution)/shard_map/all_gather | solution.py:82
  8.3 17.0 %collective-permute-start = (bf16[256,512]{1,0:T(8,128)(2,1)}, bf16[256,512]{1,0:T(8,128)(2,1)S(1)}, u32[]{:S(2)}, u32[]{:S(2)}) collective-permute-start(bf16[256,512]{1,0:T(8,128)(2,1)} %param.6), channel_id=1, source_target_pairs={{0,2},{1,3},{2,4},{3,5},{4,6},{5,7},{6,8},{7,9},{8,10},{9,11},{10,... | collective-permute-start | bytes 786440 | tf_op jit(solution)/shard_map/ppermute | solution.py:36
  12.5 14.8 %collective-permute-start.2 = (bf16[256,512]{1,0:T(8,128)(2,1)}, bf16[256,512]{1,0:T(8,128)(2,1)S(1)}, u32[]{:S(2)}, u32[]{:S(2)}) collective-permute-start(bf16[256,512]{1,0:T(8,128)(2,1)} %param.6), channel_id=1, source_target_pairs={{0,14},{1,15},{2,0},{3,1},{4,2},{5,3},{6,4},{7,5},{8,6},{9,7},{10,... | collective-permute-start | bytes 786440 | tf_op jit(solution)/shard_map/ppermute | solution.py:39
  25.4 11.7 %collective-permute-start.1 = (bf16[256,512]{1,0:T(8,128)(2,1)S(1)}, bf16[256,512]{1,0:T(8,128)(2,1)S(1)}, u32[]{:S(2)}, u32[]{:S(2)}) collective-permute-start(bf16[256,512]{1,0:T(8,128)(2,1)S(1)} %collective-permute-done), channel_id=1, source_target_pairs={{0,2},{1,3},{2,4},{3,5},{4,6},{5,7},{6,8},{7,9},{8,10},{9,11},{10,... | collective-permute-start | bytes 786440 | tf_op jit(solution)/shard_map/ppermute | solution.py:36
  27.3 9.9 %collective-permute-start.3 = (bf16[256,512]{1,0:T(8,128)(2,1)S(1)}, bf16[256,512]{1,0:T(8,128)(2,1)S(1)}, u32[]{:S(2)}, u32[]{:S(2)}) collective-permute-start(bf16[256,512]{1,0:T(8,128)(2,1)S(1)} %collective-permute-done.2), channel_id=1, source_target_pairs={{0,14},{1,15},{2,0},{3,1},{4,2},{5,3},{6,4},{7,5},{8,6},{9,7},{10,... | collective-permute-start | bytes 786440 | tf_op jit(solution)/shard_map/ppermute | solution.py:39
  70.8 8.3 %collective-permute-start.4 = (bf16[256,512]{1,0:T(8,128)(2,1)S(1)}, bf16[256,512]{1,0:T(8,128)(2,1)S(1)}, u32[]{:S(2)}, u32[]{:S(2)}) collective-permute-start(bf16[256,512]{1,0:T(8,128)(2,1)S(1)} %collective-permute-done.1), channel_id=1, source_target_pairs={{0,2},{1,3},{2,4},{3,5},{4,6},{5,7},{6,8},{7,9},{8,10},{9,11},{10,... | collective-permute-start | bytes 786440 | tf_op jit(solution)/shard_map/ppermute | solution.py:36
  79.1 15.8 %copy-start.5 = (bf16[256,512]{1,0:T(8,128)(2,1)}, bf16[256,512]{1,0:T(8,128)(2,1)S(1)}, u32[]{:S(2)}) copy-start(bf16[256,512]{1,0:T(8,128)(2,1)S(1)} %collective-permute-done.4) | copy-start | bytes 786436
  79.1 8.3 %collective-permute-start.5 = (bf16[256,512]{1,0:T(8,128)(2,1)S(1)}, bf16[256,512]{1,0:T(8,128)(2,1)S(1)}, u32[]{:S(2)}, u32[]{:S(2)}) collective-permute-start(bf16[256,512]{1,0:T(8,128)(2,1)S(1)} %collective-permute-done.4), channel_id=1, source_target_pairs={{0,2},{1,3},{2,4},{3,5},{4,6},{5,7},{6,8},{7,9},{8,10},{9,11},{10,... | collective-permute-start | bytes 786440 | tf_op jit(solution)/shard_map/ppermute | solution.py:36
  81.0 12.3 %collective-permute-start.6 = (bf16[256,512]{1,0:T(8,128)(2,1)S(1)}, bf16[256,512]{1,0:T(8,128)(2,1)S(1)}, u32[]{:S(2)}, u32[]{:S(2)}) collective-permute-start(bf16[256,512]{1,0:T(8,128)(2,1)S(1)} %collective-permute-done.3), channel_id=1, source_target_pairs={{0,14},{1,15},{2,0},{3,1},{4,2},{5,3},{6,4},{7,5},{8,6},{9,7},{10,... | collective-permute-start | bytes 786440 | tf_op jit(solution)/shard_map/ppermute | solution.py:39
  87.4 7.4 %copy-start.6 = (bf16[256,512]{1,0:T(8,128)(2,1)}, bf16[256,512]{1,0:T(8,128)(2,1)S(1)}, u32[]{:S(2)}) copy-start(bf16[256,512]{1,0:T(8,128)(2,1)S(1)} %collective-permute-done.5) | copy-start | bytes 786436
  93.3 0.7 copy-start.4
  94.9 16.3 %collective-permute-start.7 = (bf16[8,256,512]{2,1,0:T(8,128)(2,1)}, bf16[8,256,512]{2,1,0:T(8,128)(2,1)}, u32[]{:S(2)}, u32[]{:S(2)}) collective-permute-start(bf16[8,256,512]{2,1,0:T(8,128)(2,1)} %get-tuple-element.17), channel_id=1, source_target_pairs={{0,1},{1,0},{2,3},{3,2},{4,5},{5,4},{6,7},{7,6},{8,9},{9,8},{10,11... | collective-permute-start | bytes 6291464 | tf_op jit(solution)/shard_map/ppermute | solution.py:42
  116.1 1.3 copy-start.1
  133.4 58.4 %all-to-all-start = ((bf16[16,256,256]{2,1,0:T(8,128)(2,1)}), bf16[16,256,256]{2,1,0:T(8,128)(2,1)}, u32[]{:S(2)}, u32[]{:S(2)}) async-start(bf16[16,256,256]{2,1,0:T(8,128)(2,1)} %gather_fusion.1), calls=%async_computation | async-start | bytes 4194304 | tf_op jit(solution)/shard_map/all_to_all | solution.py:96
  141.6 47.0 %collective-permute-start.8 = (bf16[256,256]{1,0:T(8,128)(2,1)S(1)}, bf16[256,256]{1,0:T(8,128)(2,1)S(1)}, u32[]{:S(2)}, u32[]{:S(2)}) collective-permute-start(bf16[256,256]{1,0:T(8,128)(2,1)S(1)} %fusion.16), channel_id=1, source_target_pairs={{0,1},{1,2},{2,3},{3,4},{4,5},{5,6},{6,7},{7,8},{8,9},{9,10},{10,1... | collective-permute-start | bytes 393224 | tf_op jit(solution)/shard_map/ppermute | solution.py:12
  191.8 8.5 %copy-start.2 = (f32[4,256,512]{1,2,0:T(8,128)S(1)}, f32[4,256,512]{1,2,0:T(8,128)}, u32[]{:S(2)}) copy-start(f32[4,256,512]{1,2,0:T(8,128)} %convolution_bitcast_fusion.2) | copy-start | bytes 6291460
  193.0 6.9 %collective-permute-start.9 = (bf16[512,256]{1,0:T(8,128)(2,1)S(1)}, bf16[512,256]{1,0:T(8,128)(2,1)S(1)}, u32[]{:S(2)}, u32[]{:S(2)}) collective-permute-start(bf16[512,256]{1,0:T(8,128)(2,1)S(1)} %bitcast.100), channel_id=1, source_target_pairs={{0,1},{1,0},{2,3},{3,2},{4,5},{5,4},{6,7},{7,6},{8,9},{9,8},{10,11... | collective-permute-start | bytes 786440 | tf_op jit(solution)/shard_map/ppermute | solution.py:61
Sparse Core Ops, SparseCore 0:
  9.5 48.2 all-gather.4
  70.9 58.2 all-gather.6

commit v8 on v7

--- a/solution.py
+++ b/solution.py
@@ -55,6 +55,18 @@
     return full.reshape((peers * array.shape[0],) + array.shape[1:]), tied
 
 
+def shift_gather(array, axis):
+    peers = lax.axis_size(axis)
+    parts = [array] + [
+        lax.ppermute(array, axis, [(i, (i - by) % peers) for i in range(peers)])
+        for by in range(1, peers)
+    ]
+    stacked = jnp.stack(parts, axis=0)
+    doubled = jnp.concatenate([stacked, stacked], axis=0)
+    me = lax.axis_index(axis)
+    return lax.dynamic_slice_in_dim(doubled, peers - me, peers, 0)
+
+
 def swap_partner(array, axis):
     peers = lax.axis_size(axis)
     pairs = [(i, i ^ 1) for i in range(peers)]
@@ -78,7 +90,7 @@
     kv_f32 = jnp.dot(tokens, kv_weight, preferred_element_type=jnp.float32)
     key_value = kv_f32.astype(jnp.bfloat16)
 
-    along_x = lax.all_gather(key_value[None], "cx", axis=0, tiled=True)
+    along_x = shift_gather(key_value, "cx")
     candidates = lax.all_gather(along_x[None], "cy", axis=0, tiled=True).reshape(
         (-1,) + key_value.shape
     )

time: 212 us -> 220 us (1.038)
  blocking collectives: 10.6 us -> 0 us
  local copies, waits for them, and re-layouts: 23.6 us -> 32.1 us
  starting transfers between devices: 53.7 us -> 59.6 us
  waiting for transfers between devices: 88.3 us -> 91.2 us
    all_gather x1 -> x0, blocking collectives: 10.6 us -> none  [per_device(): along_x = lax.all_gather(key_value[None], 'cx', axis=0, tiled=True)]
    ppermute x0 -> x3, starting transfers between devices: none -> 9.07 us  [shift_gather(): lax.ppermute(array, axis, [(i, (i - by) % peers) for i in range(peers)])]
    unnamed x28 -> x34, local copies, waits for them, and re-layouts: 13.6 us -> 19.5 us
    ppermute x1, starting transfers between devices: 7.59 us -> 4.93 us  [ring_gather_rows(): other = lax.ppermute(mine, axis, [(i, i ^ 1) for i in range(peers)])]
  transfers between devices with their start and end apart: 13 -> 16, of which waited for: 9 -> 10; matrix products, arithmetic and copies ran while one was open for 13% -> 13% of each run, Pallas kernels for 0% -> 0%
where the time goes in v8:
time: 220 us; the launch traced here: 219 us
  waiting for transfers between devices  91.2 us (41%)
  starting transfers between devices  59.6 us (27%)
  local copies, waits for them, and re-layouts  32.1 us (15%)
  between operations  17.4 us (8%)
  other arithmetic  10.4 us (5%)
  matrix products  8.41 us (4%)
    ppermute x1, waiting for transfers between devices, from_behind(): return lax.ppermute(array, axis, pairs)  39.2 us
    all_gather x1, waiting for transfers between devices, per_device(): lax.all_gather(jnp.concatenate([key_weight, value_weight], axis=1), 'fsdp...  20.8 us
    unnamed x34, local copies, waits for them, and re-layouts  19.5 us
    ppermute x4, waiting for transfers between devices, ring_gather_rows(): ahead = lax.ppermute(ahead, axis, shift_pairs(2))  18.3 us
    ppermute x3, starting transfers between devices, ring_gather_rows(): behind = lax.ppermute(behind, axis, shift_pairs(-2))  17.7 us
    ppermute x4, starting transfers between devices, ring_gather_rows(): ahead = lax.ppermute(ahead, axis, shift_pairs(2))  10.4 us
    all_gather x1, waiting for transfers between devices, per_device(): lax.all_gather(along_x[None], 'cy', axis=0, tiled=True)  9.71 us
    ppermute x3, starting transfers between devices, shift_gather(): lax.ppermute(array, axis, [(i, (i - by) % peers) for i in range(peers)])  9.07 us
  transfers between devices with their start and end apart: 16, of which 10 were waited for; matrix products, arithmetic and copies ran while one was open for 13% of the time, Pallas kernels for 0%

profile of v8, /device:TPU:7, one launch (start us, length us, event | category | flops | bytes accessed | tf_op | source)
XLA Modules:
  0.0 219.1 jit_solution(12064365229611809715)
XLA Ops:
  6.5 1.7 pad_maximum_fusion.2
  8.3 4.0 %collective-permute-start = (bf16[256,512]{1,0:T(8,128)(2,1)}, bf16[256,512]{1,0:T(8,128)(2,1)S(1)}, u32[]{:S(2)}, u32[]{:S(2)}) collective-permute-start(bf16[256,512]{1,0:T(8,128)(2,1)} %param.6), channel_id=1, source_target_pairs={{0,2},{1,3},{2,4},{3,5},{4,6},{5,7},{6,8},{7,9},{8,10},{9,11},{10,... | collective-permute-start | bytes 786440 | tf_op jit(solution)/shard_map/ppermute | solution.py:36
  12.3 8.6 %collective-permute-start.2 = (bf16[256,512]{1,0:T(8,128)(2,1)}, bf16[256,512]{1,0:T(8,128)(2,1)S(1)}, u32[]{:S(2)}, u32[]{:S(2)}) collective-permute-start(bf16[256,512]{1,0:T(8,128)(2,1)} %param.6), channel_id=1, source_target_pairs={{0,14},{1,15},{2,0},{3,1},{4,2},{5,3},{6,4},{7,5},{8,6},{9,7},{10,... | collective-permute-start | bytes 786440 | tf_op jit(solution)/shard_map/ppermute | solution.py:39
  20.9 4.3 %collective-permute-done = bf16[256,512]{1,0:T(8,128)(2,1)S(1)} collective-permute-done((bf16[256,512]{1,0:T(8,128)(2,1)}, bf16[256,512]{1,0:T(8,128)(2,1)S(1)}, u32[]{:S(2)}, u32[]{:S(2)}) %collective-permute-start) | collective-permute-done | bytes 262176 | tf_op jit(solution)/shard_map/ppermute | solution.py:36
  25.2 1.9 collective-permute-start.1
  27.1 4.6 %collective-permute-start.3 = (bf16[256,512]{1,0:T(8,128)(2,1)S(1)}, bf16[256,512]{1,0:T(8,128)(2,1)S(1)}, u32[]{:S(2)}, u32[]{:S(2)}) collective-permute-start(bf16[256,512]{1,0:T(8,128)(2,1)S(1)} %collective-permute-done.2), channel_id=1, source_target_pairs={{0,14},{1,15},{2,0},{3,1},{4,2},{5,3},{6,4},{7,5},{8,6},{9,7},{10,... | collective-permute-start | bytes 786440 | tf_op jit(solution)/shard_map/ppermute | solution.py:39
  31.7 4.7 %collective-permute-done.1 = bf16[256,512]{1,0:T(8,128)(2,1)S(1)} collective-permute-done((bf16[256,512]{1,0:T(8,128)(2,1)S(1)}, bf16[256,512]{1,0:T(8,128)(2,1)S(1)}, u32[]{:S(2)}, u32[]{:S(2)}) %collective-permute-start.1) | collective-permute-done | bytes 262176 | tf_op jit(solution)/shard_map/ppermute | solution.py:36
  36.4 0.6 collective-permute-done.3
  37.1 20.8 %all-gather.4.cloned.1.call-done = bf16[4096,256]{1,0:T(8,128)(2,1)} async-done(((bf16[256,256]{1,0:T(8,128)(2,1)}), bf16[4096,256]{1,0:T(8,128)(2,1)}) %all-gather.4.cloned.1.call-update) | async-done | bytes 2097168 | tf_op jit(solution)/shard_map/all_gather | solution.py:86
  57.9 2.9 %bitcast_dynamic-update-slice_fusion.24 = (bf16[8,256,256]{2,1,0:T(8,128)(2,1)}, bf16[256,256]{0,1:T(8,128)(2,1)S(1)}) fusion(bf16[256,4096]{1,0:T(8,128)(2,1)S(1)} %copy-done, bf16[4096,256]{1,0:T(8,128)(2,1)} %all-gather.4.cloned.1.call-done), kind=kOutput, calls=%fused_computation.65 | convolution fusion | flops 536936448 | bytes 4456448 | tf_op jit(solution)/shard_map/dot_general | solution.py:90
  60.8 2.6 %collective-permute-start.9 = (bf16[256,256]{1,0:T(8,128)(2,1)S(1)}, bf16[256,256]{1,0:T(8,128)(2,1)}, u32[]{:S(2)}, u32[]{:S(2)}) collective-permute-start(bf16[256,256]{1,0:T(8,128)(2,1)S(1)} %bitcast.113), channel_id=1, source_target_pairs={{0,48},{16,0},{32,16},{48,32},{1,49},{17,1},{33,17},{49,33},{2,50}... | collective-permute-start | bytes 393224 | tf_op jit(solution)/shard_map/ppermute | solution.py:61
  63.4 2.8 %collective-permute-start.10 = (bf16[256,256]{1,0:T(8,128)(2,1)S(1)}, bf16[256,256]{1,0:T(8,128)(2,1)S(1)}, u32[]{:S(2)}, u32[]{:S(2)}) collective-permute-start(bf16[256,256]{1,0:T(8,128)(2,1)S(1)} %bitcast.114), channel_id=1, source_target_pairs={{0,32},{16,48},{32,0},{48,16},{1,33},{17,49},{33,1},{49,17},{2,34}... | collective-permute-start | bytes 393224 | tf_op jit(solution)/shard_map/ppermute | solution.py:61
  66.2 3.7 %collective-permute-start.11 = (bf16[256,256]{1,0:T(8,128)(2,1)S(1)}, bf16[256,256]{1,0:T(8,128)(2,1)S(1)}, u32[]{:S(2)}, u32[]{:S(2)}) collective-permute-start(bf16[256,256]{1,0:T(8,128)(2,1)S(1)} %bitcast.115), channel_id=1, source_target_pairs={{0,16},{16,32},{32,48},{48,0},{1,17},{17,33},{33,49},{49,1},{2,18}... | collective-permute-start | bytes 393224 | tf_op jit(solution)/shard_map/ppermute | solution.py:61
  69.9 1.6 bitcast_dynamic-update-slice_fusion.30
  71.5 0.7 bitcast_dynamic-update-slice_fusion.28
  72.2 1.8 collective-permute-done.11
  74.0 0.7 bitcast_dynamic-update-slice_fusion.26
  74.6 0.7 bitcast_dynamic-update-slice_fusion.25
  75.3 1.6 bitcast_dynamic-update-slice_fusion.31
  76.9 0.7 bitcast_dynamic-update-slice_fusion.29
  77.5 0.6 bitcast_dynamic-update-slice_fusion.27
  78.2 1.9 constant_dynamic-slice_fusion.1
  80.1 2.6 %collective-permute-start.4 = (bf16[256,512]{1,0:T(8,128)(2,1)S(1)}, bf16[256,512]{1,0:T(8,128)(2,1)S(1)}, u32[]{:S(2)}, u32[]{:S(2)}) collective-permute-start(bf16[256,512]{1,0:T(8,128)(2,1)S(1)} %collective-permute-done.1), channel_id=1, source_target_pairs={{0,2},{1,3},{2,4},{3,5},{4,6},{5,7},{6,8},{7,9},{8,10},{9,11},{10,... | collective-permute-start | bytes 786440 | tf_op jit(solution)/shard_map/ppermute | solution.py:36
  82.7 7.0 %collective-permute-done.4 = bf16[256,512]{1,0:T(8,128)(2,1)S(1)} collective-permute-done((bf16[256,512]{1,0:T(8,128)(2,1)S(1)}, bf16[256,512]{1,0:T(8,128)(2,1)S(1)}, u32[]{:S(2)}, u32[]{:S(2)}) %collective-permute-start.4) | collective-permute-done | bytes 262176 | tf_op jit(solution)/shard_map/ppermute | solution.py:36
  89.7 1.9 collective-permute-start.5
  91.6 4.6 %collective-permute-start.6 = (bf16[256,512]{1,0:T(8,128)(2,1)S(1)}, bf16[256,512]{1,0:T(8,128)(2,1)S(1)}, u32[]{:S(2)}, u32[]{:S(2)}) collective-permute-start(bf16[256,512]{1,0:T(8,128)(2,1)S(1)} %collective-permute-done.3), channel_id=1, source_target_pairs={{0,14},{1,15},{2,0},{3,1},{4,2},{5,3},{6,4},{7,5},{8,6},{9,7},{10,... | collective-permute-start | bytes 786440 | tf_op jit(solution)/shard_map/ppermute | solution.py:39
  96.2 2.3 %collective-permute-done.5 = bf16[256,512]{1,0:T(8,128)(2,1)S(1)} collective-permute-done((bf16[256,512]{1,0:T(8,128)(2,1)S(1)}, bf16[256,512]{1,0:T(8,128)(2,1)S(1)}, u32[]{:S(2)}, u32[]{:S(2)}) %collective-permute-start.5) | collective-permute-done | bytes 262176 | tf_op jit(solution)/shard_map/ppermute | solution.py:36
  98.5 0.9 bitcast_dynamic-update-slice_fusion.22
  99.4 0.8 bitcast_dynamic-update-slice_fusion.19
  100.2 0.9 bitcast_dynamic-update-slice_fusion.16
  101.1 0.9 bitcast_dynamic-update-slice_fusion.13
  101.9 0.8 bitcast_dynamic-update-slice_fusion.10
  102.8 0.8 bitcast_dynamic-update-slice_fusion.7
  103.6 0.9 bitcast_dynamic-update-slice_fusion.4
  104.5 0.7 copy-done.4
  105.2 0.8 bitcast_dynamic-update-slice_fusion.1
  106.0 4.9 %collective-permute-start.7 = (bf16[8,256,512]{2,1,0:T(8,128)(2,1)}, bf16[8,256,512]{2,1,0:T(8,128)(2,1)}, u32[]{:S(2)}, u32[]{:S(2)}) collective-permute-start(bf16[8,256,512]{2,1,0:T(8,128)(2,1)} %get-tuple-element.17), channel_id=1, source_target_pairs={{0,1},{1,0},{2,3},{3,2},{4,5},{5,4},{6,7},{7,6},{8,9},{9,8},{10,11... | collective-permute-start | bytes 6291464 | tf_op jit(solution)/shard_map/ppermute | solution.py:42
  111.0 1.7 bitcast_dynamic-update-slice_fusion.23
  112.7 1.7 bitcast_dynamic-update-slice_fusion.20
  114.4 0.7 bitcast_dynamic-update-slice_fusion.17
  115.1 0.7 bitcast_dynamic-update-slice_fusion.14
  115.8 0.7 bitcast_dynamic-update-slice_fusion.11
  116.6 0.7 bitcast_dynamic-update-slice_fusion.8
  117.3 0.7 bitcast_dynamic-update-slice_fusion.5
  118.0 1.7 bitcast_dynamic-update-slice_fusion.2
  119.7 4.6 %select_bitcast_fusion.1 = (bf16[8,1,256,512]{3,2,1,0:T(8,128)(2,1)S(1)}, bf16[8,1,256,512]{3,2,1,0:T(8,128)(2,1)S(1)}) fusion(pred[]{:T(512)S(6)} %eq.14, bf16[16,256,512]{2,1,0:T(8,128)(2,1)} %bitcast_dynamic-update-slice_fusion.2, s32[]{:T(128)S(6)} %select_n.121, bf16[8,256,512]{2,1,0:T(8,128)(2,1)} %collective-permute-done.7), kind=kLoop, calls=%fused_computation.14 | loop fusion | flops 4194304 | bytes 8388613 | tf_op jit(solution)/shard_map/stack | solution.py:54
  124.7 1.3 convolution_convert_fusion
  126.0 0.7 gather_fusion
  126.7 9.7 %all-gather.6.cloned.1.call-done = bf16[32,256,256]{2,1,0:T(8,128)(2,1)} async-done(((bf16[4,256,256]{2,1,0:T(8,128)(2,1)}), bf16[32,256,256]{2,1,0:T(8,128)(2,1)}) %all-gather.6.cloned.1.call-update) | async-done | bytes 4194320 | tf_op jit(solution)/shard_map/all_gather | solution.py:94
  136.5 4.2 %gather_fusion.1 = bf16[16,256,256]{2,1,0:T(8,128)(2,1)} fusion(bf16[32,256,256]{2,1,0:T(8,128)(2,1)} %all-gather.6.cloned.1.call-done, s32[1024]{0:T(1024)S(1)} %pad_clamp_fusion), kind=kCustom, calls=%fused_computation.1 | custom fusion | bytes 4194368 | tf_op jit(solution)/shard_map/jit(_take)/gather | solution.py:107
  140.7 8.1 %all-to-all-start = ((bf16[16,256,256]{2,1,0:T(8,128)(2,1)}), bf16[16,256,256]{2,1,0:T(8,128)(2,1)}, u32[]{:S(2)}, u32[]{:S(2)}) async-start(bf16[16,256,256]{2,1,0:T(8,128)(2,1)} %gather_fusion.1), calls=%async_computation | async-start | bytes 4194304 | tf_op jit(solution)/shard_map/all_to_all | solution.py:108
  148.9 3.5 %collective-permute-start.8 = (bf16[256,256]{1,0:T(8,128)(2,1)S(1)}, bf16[256,256]{1,0:T(8,128)(2,1)S(1)}, u32[]{:S(2)}, u32[]{:S(2)}) collective-permute-start(bf16[256,256]{1,0:T(8,128)(2,1)S(1)} %bitcast.116), channel_id=1, source_target_pairs={{0,1},{1,2},{2,3},{3,4},{4,5},{5,6},{6,7},{7,8},{8,9},{9,10},{10,1... | collective-permute-start | bytes 393224 | tf_op jit(solution)/shard_map/ppermute | solution.py:12
  152.6 0.5 fusion.42
  156.8 39.2 %collective-permute-done.8 = bf16[256,256]{1,0:T(8,128)(2,1)S(1)} collective-permute-done((bf16[256,256]{1,0:T(8,128)(2,1)S(1)}, bf16[256,256]{1,0:T(8,128)(2,1)S(1)}, u32[]{:S(2)}, u32[]{:S(2)}) %collective-permute-start.8) | collective-permute-done | bytes 131104 | tf_op jit(solution)/shard_map/ppermute | solution.py:12
  196.0 1.7 convolution_bitcast_fusion.2
  197.7 1.4 add_add_fusion
  199.2 1.1 constant_dynamic-slice_fusion
  200.3 5.8 %collective-permute-start.12 = (bf16[512,256]{1,0:T(8,128)(2,1)S(1)}, bf16[512,256]{1,0:T(8,128)(2,1)S(1)}, u32[]{:S(2)}, u32[]{:S(2)}) collective-permute-start(bf16[512,256]{1,0:T(8,128)(2,1)S(1)} %bitcast.110), channel_id=1, source_target_pairs={{0,1},{1,0},{2,3},{3,2},{4,5},{5,4},{6,7},{7,6},{8,9},{9,8},{10,11... | collective-permute-start | bytes 786440 | tf_op jit(solution)/shard_map/ppermute | solution.py:73
  206.1 0.4 convolution_bitcast_fusion.1
  206.5 0.7 collective-permute-done.12
  207.6 0.8 fusion.17
  208.4 1.4 fusion.1
  209.8 1.6 fusion.13
  211.4 0.8 copy.25
  (38 shorter events, 1.2 us)
Async XLA Ops:
  6.5 51.3 %copy-start = (bf16[256,4096]{1,0:T(8,128)(2,1)S(1)}, bf16[256,4096]{1,0:T(8,128)(2,1)}, u32[]{:S(2)}) copy-start(bf16[256,4096]{1,0:T(8,128)(2,1)} %param.5) | copy-start | bytes 6291460
  6.5 51.3 %all-gather.4.cloned.1.call-start = ((), (), s32[]{:S(2)}) async-start(), calls=%async_computation.1 | async-start | bytes 2228224 | tf_op jit(solution)/shard_map/all_gather | solution.py:86
  8.3 128.2 %all-gather.6.cloned.1.call-start = ((), (), s32[]{:S(2)}) async-start(), calls=%async_computation.2 | async-start | bytes 4718592 | tf_op jit(solution)/shard_map/all_gather | solution.py:94
  8.3 16.9 %collective-permute-start = (bf16[256,512]{1,0:T(8,128)(2,1)}, bf16[256,512]{1,0:T(8,128)(2,1)S(1)}, u32[]{:S(2)}, u32[]{:S(2)}) collective-permute-start(bf16[256,512]{1,0:T(8,128)(2,1)} %param.6), channel_id=1, source_target_pairs={{0,2},{1,3},{2,4},{3,5},{4,6},{5,7},{6,8},{7,9},{8,10},{9,11},{10,... | collective-permute-start | bytes 786440 | tf_op jit(solution)/shard_map/ppermute | solution.py:36
  12.3 14.8 %collective-permute-start.2 = (bf16[256,512]{1,0:T(8,128)(2,1)}, bf16[256,512]{1,0:T(8,128)(2,1)S(1)}, u32[]{:S(2)}, u32[]{:S(2)}) collective-permute-start(bf16[256,512]{1,0:T(8,128)(2,1)} %param.6), channel_id=1, source_target_pairs={{0,14},{1,15},{2,0},{3,1},{4,2},{5,3},{6,4},{7,5},{8,6},{9,7},{10,... | collective-permute-start | bytes 786440 | tf_op jit(solution)/shard_map/ppermute | solution.py:39
  25.2 11.2 %collective-permute-start.1 = (bf16[256,512]{1,0:T(8,128)(2,1)S(1)}, bf16[256,512]{1,0:T(8,128)(2,1)S(1)}, u32[]{:S(2)}, u32[]{:S(2)}) collective-permute-start(bf16[256,512]{1,0:T(8,128)(2,1)S(1)} %collective-permute-done), channel_id=1, source_target_pairs={{0,2},{1,3},{2,4},{3,5},{4,6},{5,7},{6,8},{7,9},{8,10},{9,11},{10,... | collective-permute-start | bytes 786440 | tf_op jit(solution)/shard_map/ppermute | solution.py:36
  27.1 9.9 %collective-permute-start.3 = (bf16[256,512]{1,0:T(8,128)(2,1)S(1)}, bf16[256,512]{1,0:T(8,128)(2,1)S(1)}, u32[]{:S(2)}, u32[]{:S(2)}) collective-permute-start(bf16[256,512]{1,0:T(8,128)(2,1)S(1)} %collective-permute-done.2), channel_id=1, source_target_pairs={{0,14},{1,15},{2,0},{3,1},{4,2},{5,3},{6,4},{7,5},{8,6},{9,7},{10,... | collective-permute-start | bytes 786440 | tf_op jit(solution)/shard_map/ppermute | solution.py:39
  60.8 41.1 %copy-start.3 = (bf16[256,512]{1,0:T(8,128)(2,1)S(1)}, bf16[256,512]{1,0:T(8,128)(2,1)}, u32[]{:S(2)}) copy-start(bf16[256,512]{1,0:T(8,128)(2,1)} %param.6) | copy-start | bytes 786436
  60.8 9.1 %collective-permute-start.9 = (bf16[256,256]{1,0:T(8,128)(2,1)S(1)}, bf16[256,256]{1,0:T(8,128)(2,1)}, u32[]{:S(2)}, u32[]{:S(2)}) collective-permute-start(bf16[256,256]{1,0:T(8,128)(2,1)S(1)} %bitcast.113), channel_id=1, source_target_pairs={{0,48},{16,0},{32,16},{48,32},{1,49},{17,1},{33,17},{49,33},{2,50}... | collective-permute-start | bytes 393224 | tf_op jit(solution)/shard_map/ppermute | solution.py:61
  63.4 8.1 %collective-permute-start.10 = (bf16[256,256]{1,0:T(8,128)(2,1)S(1)}, bf16[256,256]{1,0:T(8,128)(2,1)S(1)}, u32[]{:S(2)}, u32[]{:S(2)}) collective-permute-start(bf16[256,256]{1,0:T(8,128)(2,1)S(1)} %bitcast.114), channel_id=1, source_target_pairs={{0,32},{16,48},{32,0},{48,16},{1,33},{17,49},{33,1},{49,17},{2,34}... | collective-permute-start | bytes 393224 | tf_op jit(solution)/shard_map/ppermute | solution.py:61
  66.2 7.8 %collective-permute-start.11 = (bf16[256,256]{1,0:T(8,128)(2,1)S(1)}, bf16[256,256]{1,0:T(8,128)(2,1)S(1)}, u32[]{:S(2)}, u32[]{:S(2)}) collective-permute-start(bf16[256,256]{1,0:T(8,128)(2,1)S(1)} %bitcast.115), channel_id=1, source_target_pairs={{0,16},{16,32},{32,48},{48,0},{1,17},{17,33},{33,49},{49,1},{2,18}... | collective-permute-start | bytes 393224 | tf_op jit(solution)/shard_map/ppermute | solution.py:61
  80.1 9.6 %collective-permute-start.4 = (bf16[256,512]{1,0:T(8,128)(2,1)S(1)}, bf16[256,512]{1,0:T(8,128)(2,1)S(1)}, u32[]{:S(2)}, u32[]{:S(2)}) collective-permute-start(bf16[256,512]{1,0:T(8,128)(2,1)S(1)} %collective-permute-done.1), channel_id=1, source_target_pairs={{0,2},{1,3},{2,4},{3,5},{4,6},{5,7},{6,8},{7,9},{8,10},{9,11},{10,... | collective-permute-start | bytes 786440 | tf_op jit(solution)/shard_map/ppermute | solution.py:36
  89.7 16.3 %copy-start.5 = (bf16[256,512]{1,0:T(8,128)(2,1)}, bf16[256,512]{1,0:T(8,128)(2,1)S(1)}, u32[]{:S(2)}) copy-start(bf16[256,512]{1,0:T(8,128)(2,1)S(1)} %collective-permute-done.4) | copy-start | bytes 786436
  89.7 8.8 %collective-permute-start.5 = (bf16[256,512]{1,0:T(8,128)(2,1)S(1)}, bf16[256,512]{1,0:T(8,128)(2,1)S(1)}, u32[]{:S(2)}, u32[]{:S(2)}) collective-permute-start(bf16[256,512]{1,0:T(8,128)(2,1)S(1)} %collective-permute-done.4), channel_id=1, source_target_pairs={{0,2},{1,3},{2,4},{3,5},{4,6},{5,7},{6,8},{7,9},{8,10},{9,11},{10,... | collective-permute-start | bytes 786440 | tf_op jit(solution)/shard_map/ppermute | solution.py:36
  91.6 12.8 %collective-permute-start.6 = (bf16[256,512]{1,0:T(8,128)(2,1)S(1)}, bf16[256,512]{1,0:T(8,128)(2,1)S(1)}, u32[]{:S(2)}, u32[]{:S(2)}) collective-permute-start(bf16[256,512]{1,0:T(8,128)(2,1)S(1)} %collective-permute-done.3), channel_id=1, source_target_pairs={{0,14},{1,15},{2,0},{3,1},{4,2},{5,3},{6,4},{7,5},{8,6},{9,7},{10,... | collective-permute-start | bytes 786440 | tf_op jit(solution)/shard_map/ppermute | solution.py:39
  98.5 7.5 %copy-start.6 = (bf16[256,512]{1,0:T(8,128)(2,1)}, bf16[256,512]{1,0:T(8,128)(2,1)S(1)}, u32[]{:S(2)}) copy-start(bf16[256,512]{1,0:T(8,128)(2,1)S(1)} %collective-permute-done.5) | copy-start | bytes 786436
  104.5 0.7 copy-start.4
  106.0 13.7 %collective-permute-start.7 = (bf16[8,256,512]{2,1,0:T(8,128)(2,1)}, bf16[8,256,512]{2,1,0:T(8,128)(2,1)}, u32[]{:S(2)}, u32[]{:S(2)}) collective-permute-start(bf16[8,256,512]{2,1,0:T(8,128)(2,1)} %get-tuple-element.17), channel_id=1, source_target_pairs={{0,1},{1,0},{2,3},{3,2},{4,5},{5,4},{6,7},{7,6},{8,9},{9,8},{10,11... | collective-permute-start | bytes 6291464 | tf_op jit(solution)/shard_map/ppermute | solution.py:42
  124.7 1.3 copy-start.1
  140.7 58.4 %all-to-all-start = ((bf16[16,256,256]{2,1,0:T(8,128)(2,1)}), bf16[16,256,256]{2,1,0:T(8,128)(2,1)}, u32[]{:S(2)}, u32[]{:S(2)}) async-start(bf16[16,256,256]{2,1,0:T(8,128)(2,1)} %gather_fusion.1), calls=%async_computation | async-start | bytes 4194304 | tf_op jit(solution)/shard_map/all_to_all | solution.py:108
  148.9 47.0 %collective-permute-start.8 = (bf16[256,256]{1,0:T(8,128)(2,1)S(1)}, bf16[256,256]{1,0:T(8,128)(2,1)S(1)}, u32[]{:S(2)}, u32[]{:S(2)}) collective-permute-start(bf16[256,256]{1,0:T(8,128)(2,1)S(1)} %bitcast.116), channel_id=1, source_target_pairs={{0,1},{1,2},{2,3},{3,4},{4,5},{5,6},{6,7},{7,8},{8,9},{9,10},{10,1... | collective-permute-start | bytes 393224 | tf_op jit(solution)/shard_map/ppermute | solution.py:12
  199.1 8.5 %copy-start.2 = (f32[4,256,512]{1,2,0:T(8,128)S(1)}, f32[4,256,512]{1,2,0:T(8,128)}, u32[]{:S(2)}) copy-start(f32[4,256,512]{1,2,0:T(8,128)} %convolution_bitcast_fusion.2) | copy-start | bytes 6291460
  200.3 6.9 %collective-permute-start.12 = (bf16[512,256]{1,0:T(8,128)(2,1)S(1)}, bf16[512,256]{1,0:T(8,128)(2,1)S(1)}, u32[]{:S(2)}, u32[]{:S(2)}) collective-permute-start(bf16[512,256]{1,0:T(8,128)(2,1)S(1)} %bitcast.110), channel_id=1, source_target_pairs={{0,1},{1,0},{2,3},{3,2},{4,5},{5,4},{6,7},{7,6},{8,9},{9,8},{10,11... | collective-permute-start | bytes 786440 | tf_op jit(solution)/shard_map/ppermute | solution.py:73
Sparse Core Ops, SparseCore 0:
  9.5 48.3 all-gather.3
  80.2 56.1 all-gather.5

commit v9 on v7

--- a/solution.py
+++ b/solution.py
@@ -72,11 +72,11 @@
     global_index = group_index * lane_count + lane_index
 
     kv_weight = lax.all_gather(
-        jnp.concatenate([key_weight, value_weight], axis=1), "fsdp", axis=0, tiled=True
+        jnp.stack([key_weight, value_weight], axis=0), "fsdp", axis=1, tiled=True
     )
     q_weight, kv_weight = ring_gather_rows(query_weight, "fsdp", 2, kv_weight)
-    kv_f32 = jnp.dot(tokens, kv_weight, preferred_element_type=jnp.float32)
-    key_value = kv_f32.astype(jnp.bfloat16)
+    kv_f32 = jnp.einsum("td,kdc->tkc", tokens, kv_weight, preferred_element_type=jnp.float32)
+    key_value = kv_f32.astype(jnp.bfloat16).reshape(token_rows, 2 * head_width)
 
     along_x = lax.all_gather(key_value[None], "cx", axis=0, tiled=True)
     candidates = lax.all_gather(along_x[None], "cy", axis=0, tiled=True).reshape(
@@ -141,16 +141,13 @@
     highest = jnp.max(scores, axis=2, keepdims=True)
     probs = jnp.exp(scores - highest)
     denominator = jnp.sum(probs, axis=2, keepdims=True)
-    mixed = (
-        jnp.einsum(
-            "hqk,kd->hqd",
-            probs.astype(jnp.bfloat16),
-            value_rows,
-            preferred_element_type=jnp.float32,
-        )
-        / denominator
-    )
-    return jnp.transpose(mixed, (1, 0, 2)).reshape(token_rows, -1).astype(jnp.bfloat16)
+    mixed = jnp.einsum(
+        "hqk,kd->qhd",
+        probs.astype(jnp.bfloat16),
+        value_rows,
+        preferred_element_type=jnp.float32,
+    ) / jnp.transpose(denominator, (1, 0, 2))
+    return mixed.reshape(token_rows, -1).astype(jnp.bfloat16)
 
 
 def split_ctx(mesh):

time: 212 us -> 219 us (1.033)
  waiting for transfers between devices: 88.3 us -> 92.4 us
    ppermute x1, waiting for transfers between devices: 39.2 us -> 43.4 us  [from_behind(): return lax.ppermute(array, axis, pairs)]
    unnamed x28 -> x30, local copies, waits for them, and re-layouts: 13.6 us -> 13.7 us
  transfers between devices with their start and end apart: 13 -> 13, of which waited for: 9 -> 9; matrix products, arithmetic and copies ran while one was open for 13% -> 12% of each run, Pallas kernels for 0% -> 0%
where the time goes in v9:
time: 219 us; the launch traced here: 218 us
  waiting for transfers between devices  92.4 us (42%)
  starting transfers between devices  53.5 us (24%)
  local copies, waits for them, and re-layouts  25 us (11%)
  between operations  17.8 us (8%)
  blocking collectives  10.6 us (5%)
  other arithmetic  10.4 us (5%)
  matrix products  8.6 us (4%)
    ppermute x1, waiting for transfers between devices, from_behind(): return lax.ppermute(array, axis, pairs)  43.4 us
    all_gather x1, waiting for transfers between devices, per_device(): lax.all_gather(jnp.stack([key_weight, value_weight], axis=0), 'fsdp', axi...  20.8 us
    ppermute x3, starting transfers between devices, ring_gather_rows(): behind = lax.ppermute(behind, axis, shift_pairs(-2))  17.7 us
    ppermute x4, waiting for transfers between devices, ring_gather_rows(): ahead = lax.ppermute(ahead, axis, shift_pairs(2))  16.2 us
    unnamed x30, local copies, waits for them, and re-layouts  13.7 us
    ppermute x4, starting transfers between devices, ring_gather_rows(): ahead = lax.ppermute(ahead, axis, shift_pairs(2))  10.7 us
    all_gather x1, blocking collectives, per_device(): along_x = lax.all_gather(key_value[None], 'cx', axis=0, tiled=True)  10.6 us
    all_gather x1, waiting for transfers between devices, per_device(): lax.all_gather(along_x[None], 'cy', axis=0, tiled=True)  10.5 us
  transfers between devices with their start and end apart: 13, of which 9 were waited for; matrix products, arithmetic and copies ran while one was open for 12% of the time, Pallas kernels for 0%

profile of v9, /device:TPU:7, one launch (start us, length us, event | category | flops | bytes accessed | tf_op | source)
XLA Modules:
  0.0 218.3 jit_solution(11033897927935394350)
XLA Ops:
  6.5 1.7 pad_maximum_fusion.2
  8.2 0.0 all-gather.4.cloned.1.call-update
  8.3 0.0 all-gather.6.cloned.1.call-start
  8.3 4.0 %collective-permute-start = (bf16[256,512]{1,0:T(8,128)(2,1)}, bf16[256,512]{1,0:T(8,128)(2,1)S(1)}, u32[]{:S(2)}, u32[]{:S(2)}) collective-permute-start(bf16[256,512]{1,0:T(8,128)(2,1)} %param.6), channel_id=1, source_target_pairs={{0,2},{1,3},{2,4},{3,5},{4,6},{5,7},{6,8},{7,9},{8,10},{9,11},{10,... | collective-permute-start | bytes 786440 | tf_op jit(solution)/shard_map/ppermute | solution.py:36
  12.3 8.6 %collective-permute-start.2 = (bf16[256,512]{1,0:T(8,128)(2,1)}, bf16[256,512]{1,0:T(8,128)(2,1)S(1)}, u32[]{:S(2)}, u32[]{:S(2)}) collective-permute-start(bf16[256,512]{1,0:T(8,128)(2,1)} %param.6), channel_id=1, source_target_pairs={{0,14},{1,15},{2,0},{3,1},{4,2},{5,3},{6,4},{7,5},{8,6},{9,7},{10,... | collective-permute-start | bytes 786440 | tf_op jit(solution)/shard_map/ppermute | solution.py:39
  20.9 4.3 %collective-permute-done = bf16[256,512]{1,0:T(8,128)(2,1)S(1)} collective-permute-done((bf16[256,512]{1,0:T(8,128)(2,1)}, bf16[256,512]{1,0:T(8,128)(2,1)S(1)}, u32[]{:S(2)}, u32[]{:S(2)}) %collective-permute-start) | collective-permute-done | bytes 262176 | tf_op jit(solution)/shard_map/ppermute | solution.py:36
  25.2 1.9 collective-permute-start.1
  27.1 0.0 collective-permute-done.2
  27.1 4.6 %collective-permute-start.3 = (bf16[256,512]{1,0:T(8,128)(2,1)S(1)}, bf16[256,512]{1,0:T(8,128)(2,1)S(1)}, u32[]{:S(2)}, u32[]{:S(2)}) collective-permute-start(bf16[256,512]{1,0:T(8,128)(2,1)S(1)} %collective-permute-done.2), channel_id=1, source_target_pairs={{0,14},{1,15},{2,0},{3,1},{4,2},{5,3},{6,4},{7,5},{8,6},{9,7},{10,... | collective-permute-start | bytes 786440 | tf_op jit(solution)/shard_map/ppermute | solution.py:39
  31.7 4.7 %collective-permute-done.1 = bf16[256,512]{1,0:T(8,128)(2,1)S(1)} collective-permute-done((bf16[256,512]{1,0:T(8,128)(2,1)S(1)}, bf16[256,512]{1,0:T(8,128)(2,1)S(1)}, u32[]{:S(2)}, u32[]{:S(2)}) %collective-permute-start.1) | collective-permute-done | bytes 262176 | tf_op jit(solution)/shard_map/ppermute | solution.py:36
  36.4 0.8 collective-permute-done.3
  37.1 20.8 %all-gather.4.cloned.1.call-done = bf16[2,4096,128]{2,1,0:T(8,128)(2,1)} async-done(((bf16[2,256,128]{2,1,0:T(8,128)(2,1)}), bf16[2,4096,128]{2,1,0:T(8,128)(2,1)}) %all-gather.4.cloned.1.call-update) | async-done | bytes 2097168 | tf_op jit(solution)/shard_map/all_gather | solution.py:74
  57.9 3.0 %fusion.18 = bf16[2,128,256]{2,1,0:T(8,128)(2,1)} fusion(bf16[2,4096,128]{2,1,0:T(8,128)(2,1)} %all-gather.4.cloned.1.call-done, bf16[256,4096]{1,0:T(8,128)(2,1)S(1)} %copy-done), kind=kOutput, calls=%fused_computation.25 | convolution fusion | flops 536936448 | bytes 4325376 | tf_op jit(solution)/shard_map/td,kdc->tkc/dot_general | solution.py:78
  60.9 1.0 copy.30
  62.0 10.6 %all_gather.10 = bf16[4,256,256]{2,1,0:T(8,128)(2,1)} all-gather(bf16[1,256,256]{2,1,0:T(8,128)(2,1)S(1)} %copy.30), channel_id=1, replica_groups=mesh['cy'=8,'cx'=4,'fsdp'=16] {'cx'}, dimensions={0}, use_global_device_ids=true | all-gather | bytes 655360 | tf_op jit(solution)/shard_map/all_gather | solution.py:81
  72.6 0.0 all-gather.6.cloned.1.call-update
  72.6 2.9 %collective-permute-start.5 = (bf16[256,512]{1,0:T(8,128)(2,1)S(1)}, bf16[256,512]{1,0:T(8,128)(2,1)S(1)}, u32[]{:S(2)}, u32[]{:S(2)}) collective-permute-start(bf16[256,512]{1,0:T(8,128)(2,1)S(1)} %collective-permute-done.1), channel_id=1, source_target_pairs={{0,2},{1,3},{2,4},{3,5},{4,6},{5,7},{6,8},{7,9},{8,10},{9,11},{10,... | collective-permute-start | bytes 786440 | tf_op jit(solution)/shard_map/ppermute | solution.py:36
  75.6 5.4 %collective-permute-done.5 = bf16[256,512]{1,0:T(8,128)(2,1)S(1)} collective-permute-done((bf16[256,512]{1,0:T(8,128)(2,1)S(1)}, bf16[256,512]{1,0:T(8,128)(2,1)S(1)}, u32[]{:S(2)}, u32[]{:S(2)}) %collective-permute-start.5) | collective-permute-done | bytes 262176 | tf_op jit(solution)/shard_map/ppermute | solution.py:36
  81.0 1.9 collective-permute-start.6
  82.9 4.6 %collective-permute-start.7 = (bf16[256,512]{1,0:T(8,128)(2,1)S(1)}, bf16[256,512]{1,0:T(8,128)(2,1)S(1)}, u32[]{:S(2)}, u32[]{:S(2)}) collective-permute-start(bf16[256,512]{1,0:T(8,128)(2,1)S(1)} %collective-permute-done.3), channel_id=1, source_target_pairs={{0,14},{1,15},{2,0},{3,1},{4,2},{5,3},{6,4},{7,5},{8,6},{9,7},{10,... | collective-permute-start | bytes 786440 | tf_op jit(solution)/shard_map/ppermute | solution.py:39
  87.5 1.8 collective-permute-done.6
  89.3 0.9 bitcast_dynamic-update-slice_fusion.22
  90.2 0.9 bitcast_dynamic-update-slice_fusion.19
  91.0 0.8 bitcast_dynamic-update-slice_fusion.16
  91.9 0.8 bitcast_dynamic-update-slice_fusion.13
  92.7 0.8 bitcast_dynamic-update-slice_fusion.10
  93.6 0.8 bitcast_dynamic-update-slice_fusion.7
  94.4 0.9 bitcast_dynamic-update-slice_fusion.4
  95.3 0.7 copy-done.4
  96.0 0.8 bitcast_dynamic-update-slice_fusion.1
  96.8 7.6 %collective-permute-start.8 = (bf16[8,256,512]{2,1,0:T(8,128)(2,1)}, bf16[8,256,512]{2,1,0:T(8,128)(2,1)}, u32[]{:S(2)}, u32[]{:S(2)}) collective-permute-start(bf16[8,256,512]{2,1,0:T(8,128)(2,1)} %get-tuple-element.17), channel_id=1, source_target_pairs={{0,1},{1,0},{2,3},{3,2},{4,5},{5,4},{6,7},{7,6},{8,9},{9,8},{10,11... | collective-permute-start | bytes 6291464 | tf_op jit(solution)/shard_map/ppermute | solution.py:42
  104.5 1.7 bitcast_dynamic-update-slice_fusion.23
  106.2 1.7 bitcast_dynamic-update-slice_fusion.20
  107.9 0.7 bitcast_dynamic-update-slice_fusion.17
  108.6 0.7 bitcast_dynamic-update-slice_fusion.14
  109.4 0.7 bitcast_dynamic-update-slice_fusion.11
  110.1 0.7 bitcast_dynamic-update-slice_fusion.8
  110.8 0.7 bitcast_dynamic-update-slice_fusion.5
  111.5 1.7 bitcast_dynamic-update-slice_fusion.2
  113.2 4.5 %select_bitcast_fusion.1 = (bf16[8,1,256,512]{3,2,1,0:T(8,128)(2,1)S(1)}, bf16[8,1,256,512]{3,2,1,0:T(8,128)(2,1)S(1)}) fusion(pred[]{:T(512)S(6)} %eq.14, bf16[16,256,512]{2,1,0:T(8,128)(2,1)} %bitcast_dynamic-update-slice_fusion.2, s32[]{:T(128)S(6)} %select_n.118, bf16[8,256,512]{2,1,0:T(8,128)(2,1)} %collective-permute-done.8), kind=kLoop, calls=%fused_computation.16 | loop fusion | flops 4194304 | bytes 8388613 | tf_op jit(solution)/shard_map/stack | solution.py:54
  117.8 0.4 pad_maximum_fusion
  118.2 0.0 copy-start.1
  118.2 1.3 convolution_convert_fusion
  119.5 0.7 gather_fusion
  120.2 10.5 %all-gather.6.cloned.1.call-done = bf16[32,256,256]{2,1,0:T(8,128)(2,1)} async-done(((bf16[4,256,256]{2,1,0:T(8,128)(2,1)}), bf16[32,256,256]{2,1,0:T(8,128)(2,1)}) %all-gather.6.cloned.1.call-update) | async-done | bytes 4194320 | tf_op jit(solution)/shard_map/all_gather | solution.py:82
  130.8 4.2 %gather_fusion.1 = bf16[16,256,256]{2,1,0:T(8,128)(2,1)} fusion(bf16[32,256,256]{2,1,0:T(8,128)(2,1)} %all-gather.6.cloned.1.call-done, s32[1024]{0:T(1024)S(1)} %pad_clamp_fusion), kind=kCustom, calls=%fused_computation.1 | custom fusion | bytes 4194368 | tf_op jit(solution)/shard_map/jit(_take)/gather | solution.py:95
  135.0 8.1 %all-to-all-start = ((bf16[16,256,256]{2,1,0:T(8,128)(2,1)}), bf16[16,256,256]{2,1,0:T(8,128)(2,1)}, u32[]{:S(2)}, u32[]{:S(2)}) async-start(bf16[16,256,256]{2,1,0:T(8,128)(2,1)} %gather_fusion.1), calls=%async_computation | async-start | bytes 4194304 | tf_op jit(solution)/shard_map/all_to_all | solution.py:96
  143.1 0.1 copy.28
  143.2 3.5 %collective-permute-start.4 = (bf16[256,256]{1,0:T(8,128)(2,1)S(1)}, bf16[256,256]{1,0:T(8,128)(2,1)S(1)}, u32[]{:S(2)}, u32[]{:S(2)}) collective-permute-start(bf16[256,256]{1,0:T(8,128)(2,1)S(1)} %copy.28), channel_id=1, source_target_pairs={{0,1},{1,2},{2,3},{3,4},{4,5},{5,6},{6,7},{7,8},{8,9},{9,10},{10,1... | collective-permute-start | bytes 393224 | tf_op jit(solution)/shard_map/ppermute | solution.py:12
  146.7 0.1 fusion.23
  146.9 43.4 %collective-permute-done.4 = bf16[256,256]{1,0:T(8,128)(2,1)S(1)} collective-permute-done((bf16[256,256]{1,0:T(8,128)(2,1)S(1)}, bf16[256,256]{1,0:T(8,128)(2,1)S(1)}, u32[]{:S(2)}, u32[]{:S(2)}) %collective-permute-start.4) | collective-permute-done | bytes 131104 | tf_op jit(solution)/shard_map/ppermute | solution.py:12
  190.3 0.1 constant_dynamic-slice_fusion.1
  190.3 0.6 fusion.45
  195.0 1.7 convolution_bitcast_fusion.2
  196.8 1.4 add_add_fusion
  198.2 1.1 constant_dynamic-slice_fusion
  199.3 5.8 %collective-permute-start.9 = (bf16[512,256]{1,0:T(8,128)(2,1)S(1)}, bf16[512,256]{1,0:T(8,128)(2,1)S(1)}, u32[]{:S(2)}, u32[]{:S(2)}) collective-permute-start(bf16[512,256]{1,0:T(8,128)(2,1)S(1)} %bitcast.111), channel_id=1, source_target_pairs={{0,1},{1,0},{2,3},{3,2},{4,5},{5,4},{6,7},{7,6},{8,9},{9,8},{10,11... | collective-permute-start | bytes 786440 | tf_op jit(solution)/shard_map/ppermute | solution.py:61
  205.1 0.4 convolution_bitcast_fusion.1
  205.6 0.7 collective-permute-done.9
  206.3 0.4 convolution_bitcast_fusion
  206.7 0.8 fusion.22
  207.5 1.4 fusion.1
  208.9 1.7 fusion.15
  210.6 0.8 copy.37
  (30 shorter events, 0.1 us)
Async XLA Ops:
  6.5 51.4 %copy-start = (bf16[256,4096]{1,0:T(8,128)(2,1)S(1)}, bf16[256,4096]{1,0:T(8,128)(2,1)}, u32[]{:S(2)}) copy-start(bf16[256,4096]{1,0:T(8,128)(2,1)} %param.5) | copy-start | bytes 6291460
  6.5 51.4 %all-gather.4.cloned.1.call-start = ((), (), s32[]{:S(2)}) async-start(), calls=%async_computation.1 | async-start | bytes 2228224 | tf_op jit(solution)/shard_map/all_gather | solution.py:74
  8.3 122.5 %all-gather.6.cloned.1.call-start = ((), (), s32[]{:S(2)}) async-start(), calls=%async_computation.2 | async-start | bytes 4718592 | tf_op jit(solution)/shard_map/all_gather | solution.py:82
  8.3 16.9 %collective-permute-start = (bf16[256,512]{1,0:T(8,128)(2,1)}, bf16[256,512]{1,0:T(8,128)(2,1)S(1)}, u32[]{:S(2)}, u32[]{:S(2)}) collective-permute-start(bf16[256,512]{1,0:T(8,128)(2,1)} %param.6), channel_id=1, source_target_pairs={{0,2},{1,3},{2,4},{3,5},{4,6},{5,7},{6,8},{7,9},{8,10},{9,11},{10,... | collective-permute-start | bytes 786440 | tf_op jit(solution)/shard_map/ppermute | solution.py:36
  12.3 14.8 %collective-permute-start.2 = (bf16[256,512]{1,0:T(8,128)(2,1)}, bf16[256,512]{1,0:T(8,128)(2,1)S(1)}, u32[]{:S(2)}, u32[]{:S(2)}) collective-permute-start(bf16[256,512]{1,0:T(8,128)(2,1)} %param.6), channel_id=1, source_target_pairs={{0,14},{1,15},{2,0},{3,1},{4,2},{5,3},{6,4},{7,5},{8,6},{9,7},{10,... | collective-permute-start | bytes 786440 | tf_op jit(solution)/shard_map/ppermute | solution.py:39
  25.2 11.2 %collective-permute-start.1 = (bf16[256,512]{1,0:T(8,128)(2,1)S(1)}, bf16[256,512]{1,0:T(8,128)(2,1)S(1)}, u32[]{:S(2)}, u32[]{:S(2)}) collective-permute-start(bf16[256,512]{1,0:T(8,128)(2,1)S(1)} %collective-permute-done), channel_id=1, source_target_pairs={{0,2},{1,3},{2,4},{3,5},{4,6},{5,7},{6,8},{7,9},{8,10},{9,11},{10,... | collective-permute-start | bytes 786440 | tf_op jit(solution)/shard_map/ppermute | solution.py:36
  27.1 10.0 %collective-permute-start.3 = (bf16[256,512]{1,0:T(8,128)(2,1)S(1)}, bf16[256,512]{1,0:T(8,128)(2,1)S(1)}, u32[]{:S(2)}, u32[]{:S(2)}) collective-permute-start(bf16[256,512]{1,0:T(8,128)(2,1)S(1)} %collective-permute-done.2), channel_id=1, source_target_pairs={{0,14},{1,15},{2,0},{3,1},{4,2},{5,3},{6,4},{7,5},{8,6},{9,7},{10,... | collective-permute-start | bytes 786440 | tf_op jit(solution)/shard_map/ppermute | solution.py:39
  60.9 31.8 %copy-start.3 = (bf16[256,512]{1,0:T(8,128)(2,1)S(1)}, bf16[256,512]{1,0:T(8,128)(2,1)}, u32[]{:S(2)}) copy-start(bf16[256,512]{1,0:T(8,128)(2,1)} %param.6) | copy-start | bytes 786436
  72.6 8.3 %collective-permute-start.5 = (bf16[256,512]{1,0:T(8,128)(2,1)S(1)}, bf16[256,512]{1,0:T(8,128)(2,1)S(1)}, u32[]{:S(2)}, u32[]{:S(2)}) collective-permute-start(bf16[256,512]{1,0:T(8,128)(2,1)S(1)} %collective-permute-done.1), channel_id=1, source_target_pairs={{0,2},{1,3},{2,4},{3,5},{4,6},{5,7},{6,8},{7,9},{8,10},{9,11},{10,... | collective-permute-start | bytes 786440 | tf_op jit(solution)/shard_map/ppermute | solution.py:36
  81.0 15.8 %copy-start.5 = (bf16[256,512]{1,0:T(8,128)(2,1)}, bf16[256,512]{1,0:T(8,128)(2,1)S(1)}, u32[]{:S(2)}) copy-start(bf16[256,512]{1,0:T(8,128)(2,1)S(1)} %collective-permute-done.5) | copy-start | bytes 786436
  81.0 8.3 %collective-permute-start.6 = (bf16[256,512]{1,0:T(8,128)(2,1)S(1)}, bf16[256,512]{1,0:T(8,128)(2,1)S(1)}, u32[]{:S(2)}, u32[]{:S(2)}) collective-permute-start(bf16[256,512]{1,0:T(8,128)(2,1)S(1)} %collective-permute-done.5), channel_id=1, source_target_pairs={{0,2},{1,3},{2,4},{3,5},{4,6},{5,7},{6,8},{7,9},{8,10},{9,11},{10,... | collective-permute-start | bytes 786440 | tf_op jit(solution)/shard_map/ppermute | solution.py:36
  82.9 12.4 %collective-permute-start.7 = (bf16[256,512]{1,0:T(8,128)(2,1)S(1)}, bf16[256,512]{1,0:T(8,128)(2,1)S(1)}, u32[]{:S(2)}, u32[]{:S(2)}) collective-permute-start(bf16[256,512]{1,0:T(8,128)(2,1)S(1)} %collective-permute-done.3), channel_id=1, source_target_pairs={{0,14},{1,15},{2,0},{3,1},{4,2},{5,3},{6,4},{7,5},{8,6},{9,7},{10,... | collective-permute-start | bytes 786440 | tf_op jit(solution)/shard_map/ppermute | solution.py:39
  89.3 7.5 %copy-start.6 = (bf16[256,512]{1,0:T(8,128)(2,1)}, bf16[256,512]{1,0:T(8,128)(2,1)S(1)}, u32[]{:S(2)}) copy-start(bf16[256,512]{1,0:T(8,128)(2,1)S(1)} %collective-permute-done.6) | copy-start | bytes 786436
  95.3 0.7 copy-start.4
  96.8 16.4 %collective-permute-start.8 = (bf16[8,256,512]{2,1,0:T(8,128)(2,1)}, bf16[8,256,512]{2,1,0:T(8,128)(2,1)}, u32[]{:S(2)}, u32[]{:S(2)}) collective-permute-start(bf16[8,256,512]{2,1,0:T(8,128)(2,1)} %get-tuple-element.17), channel_id=1, source_target_pairs={{0,1},{1,0},{2,3},{3,2},{4,5},{5,4},{6,7},{7,6},{8,9},{9,8},{10,11... | collective-permute-start | bytes 6291464 | tf_op jit(solution)/shard_map/ppermute | solution.py:42
  118.2 1.3 copy-start.1
  120.2 22.9 %copy-start.7 = (bf16[2,128,256]{2,1,0:T(8,128)(2,1)S(1)}, bf16[2,128,256]{2,1,0:T(8,128)(2,1)}, u32[]{:S(2)}) copy-start(bf16[2,128,256]{2,1,0:T(8,128)(2,1)} %fusion.18) | copy-start | bytes 393220
  135.0 63.2 %all-to-all-start = ((bf16[16,256,256]{2,1,0:T(8,128)(2,1)}), bf16[16,256,256]{2,1,0:T(8,128)(2,1)}, u32[]{:S(2)}, u32[]{:S(2)}) async-start(bf16[16,256,256]{2,1,0:T(8,128)(2,1)} %gather_fusion.1), calls=%async_computation | async-start | bytes 4194304 | tf_op jit(solution)/shard_map/all_to_all | solution.py:96
  143.2 47.1 %collective-permute-start.4 = (bf16[256,256]{1,0:T(8,128)(2,1)S(1)}, bf16[256,256]{1,0:T(8,128)(2,1)S(1)}, u32[]{:S(2)}, u32[]{:S(2)}) collective-permute-start(bf16[256,256]{1,0:T(8,128)(2,1)S(1)} %copy.28), channel_id=1, source_target_pairs={{0,1},{1,2},{2,3},{3,4},{4,5},{5,6},{6,7},{7,8},{8,9},{9,10},{10,1... | collective-permute-start | bytes 393224 | tf_op jit(solution)/shard_map/ppermute | solution.py:12
  198.2 8.5 %copy-start.2 = (f32[4,256,512]{1,2,0:T(8,128)S(1)}, f32[4,256,512]{1,2,0:T(8,128)}, u32[]{:S(2)}) copy-start(f32[4,256,512]{1,2,0:T(8,128)} %convolution_bitcast_fusion.2) | copy-start | bytes 6291460
  199.3 6.9 %collective-permute-start.9 = (bf16[512,256]{1,0:T(8,128)(2,1)S(1)}, bf16[512,256]{1,0:T(8,128)(2,1)S(1)}, u32[]{:S(2)}, u32[]{:S(2)}) collective-permute-start(bf16[512,256]{1,0:T(8,128)(2,1)S(1)} %bitcast.111), channel_id=1, source_target_pairs={{0,1},{1,0},{2,3},{3,2},{4,5},{5,4},{6,7},{7,6},{8,9},{9,8},{10,11... | collective-permute-start | bytes 786440 | tf_op jit(solution)/shard_map/ppermute | solution.py:61
Sparse Core Ops, SparseCore 0:
  9.5 48.3 all-gather.3
  72.8 57.9 all-gather.5

commit v10 on v7

--- a/solution.py
+++ b/solution.py
@@ -91,18 +91,21 @@
     queries, chosen = lax.optimization_barrier((queries, chosen))
 
     dest_block = group_index * blocks_group + jnp.arange(lane_count, dtype=jnp.int32) // 2
-    dest_pick = chosen[dest_block, jnp.arange(lane_count, dtype=jnp.int32) % 2]
+    dest_pick = chosen[dest_block]
     outgoing = jnp.take(candidates, dest_pick // blocks_group, axis=0, mode="clip")
     incoming = lax.all_to_all(outgoing, "fsdp", split_axis=0, concat_axis=0, tiled=True)
 
     mine = lax.dynamic_index_in_dim(chosen, my_block, 0, keepdims=False)
-    my_choice = lane_index % 2
-    my_pick = jnp.where(my_choice == 0, mine[0], mine[1])
-    place = my_pick % blocks_group * 2
-    block_mine = lax.dynamic_slice_in_dim(incoming, place, 2, 0).reshape(
-        2 * token_rows, 2 * head_width
-    )
-    block_partner = swap_partner(block_mine, "fsdp")
+
+    def assemble(which):
+        place = mine[which] % blocks_group * 2
+        return lax.dynamic_slice_in_dim(incoming[:, which], place, 2, 0).reshape(
+            2 * token_rows, 2 * head_width
+        )
+
+    block_mine = assemble(0)
+    block_partner = assemble(1)
+    my_choice = 0
 
     scale = head_width ** (-0.5)
     scores = jnp.concatenate(

time: 212 us -> 257 us (1.21); the launches traced: 212 us -> 253 us
  waiting for transfers between devices: 88.3 us -> 145 us
  local copies, waits for them, and re-layouts: 23.6 us -> 15 us
  starting transfers between devices: 53.7 us -> 47.9 us
  other arithmetic: 10.4 us -> 6.73 us
  between operations: 17.4 us -> 20.3 us
    ppermute x1, waiting for transfers between devices: 39.2 us -> 81.3 us  [from_behind(): return lax.ppermute(array, axis, pairs)]
    all_gather x1, waiting for transfers between devices: 11 us -> 24.1 us  [per_device(): lax.all_gather(along_x[None], 'cy', axis=0, tiled=True)]
    unnamed x28 -> x22, local copies, waits for them, and re-layouts: 13.6 us -> 4.85 us
    ppermute x1 -> x0, starting transfers between devices: 5.79 us -> none  [swap_partner(): return lax.ppermute(array, axis, pairs)]
    another operation x2, other arithmetic: 4.93 us -> 1.31 us  [ring_gather_rows(): full = jnp.stack([first, second], axis=1)]
    slice x1 -> x2, local copies, waits for them, and re-layouts: 0.52 us -> 3.09 us  [the longest x1 2.51 us: assemble(): incoming[:, which]]
  transfers between devices with their start and end apart: 13 -> 12, of which waited for: 9 -> 9; matrix products, arithmetic and copies ran while one was open for 13% -> 5% of each run, Pallas kernels for 0% -> 0%
where the time goes in v10:
time: 257 us; the launch traced here: 253 us
  waiting for transfers between devices  145 us (56%)
  starting transfers between devices  47.9 us (19%)
  between operations  20.3 us (8%)
  local copies, waits for them, and re-layouts  15 us (6%)
  blocking collectives  10.6 us (4%)
  matrix products  7.82 us (3%)
  other arithmetic  6.73 us (3%)
    ppermute x1, waiting for transfers between devices, from_behind(): return lax.ppermute(array, axis, pairs)  81.3 us
    all_gather x1, waiting for transfers between devices, per_device(): lax.all_gather(along_x[None], 'cy', axis=0, tiled=True)  24.1 us
    all_gather x1, waiting for transfers between devices, per_device(): lax.all_gather(jnp.concatenate([key_weight, value_weight], axis=1), 'fsdp...  20.6 us
    ppermute x3, starting transfers between devices, ring_gather_rows(): behind = lax.ppermute(behind, axis, shift_pairs(-2))  17.7 us
    ppermute x4, waiting for transfers between devices, ring_gather_rows(): ahead = lax.ppermute(ahead, axis, shift_pairs(2))  17 us
    ppermute x4, starting transfers between devices, ring_gather_rows(): ahead = lax.ppermute(ahead, axis, shift_pairs(2))  11 us
    all_gather x1, blocking collectives, per_device(): along_x = lax.all_gather(key_value[None], 'cx', axis=0, tiled=True)  10.6 us
    all_to_all x1, starting transfers between devices, per_device(): lax.all_to_all(outgoing, 'fsdp', split_axis=0, concat_axis=0, tiled=True)  8.07 us
  transfers between devices with their start and end apart: 12, of which 9 were waited for; matrix products, arithmetic and copies ran while one was open for 5% of the time, Pallas kernels for 0%

profile of v10, /device:TPU:7, one launch (start us, length us, event | category | flops | bytes accessed | tf_op | source)
XLA Modules:
  0.0 253.2 jit_solution(1089264497294242232)
XLA Ops:
  6.5 0.0 copy-start
  6.5 0.0 all-gather.5.cloned.1.call-start
  6.5 1.7 pad_maximum_fusion.2
  8.2 0.0 all-gather.5.cloned.1.call-update
  8.3 0.0 copy-start.2
  8.3 0.0 all-gather.7.cloned.1.call-start
  8.3 4.1 %collective-permute-start = (bf16[256,512]{1,0:T(8,128)(2,1)}, bf16[256,512]{1,0:T(8,128)(2,1)S(1)}, u32[]{:S(2)}, u32[]{:S(2)}) collective-permute-start(bf16[256,512]{1,0:T(8,128)(2,1)} %param.6), channel_id=1, source_target_pairs={{0,2},{1,3},{2,4},{3,5},{4,6},{5,7},{6,8},{7,9},{8,10},{9,11},{10,... | collective-permute-start | bytes 786440 | tf_op jit(solution)/shard_map/ppermute | solution.py:36
  12.5 8.6 %collective-permute-start.2 = (bf16[256,512]{1,0:T(8,128)(2,1)}, bf16[256,512]{1,0:T(8,128)(2,1)S(1)}, u32[]{:S(2)}, u32[]{:S(2)}) collective-permute-start(bf16[256,512]{1,0:T(8,128)(2,1)} %param.6), channel_id=1, source_target_pairs={{0,14},{1,15},{2,0},{3,1},{4,2},{5,3},{6,4},{7,5},{8,6},{9,7},{10,... | collective-permute-start | bytes 786440 | tf_op jit(solution)/shard_map/ppermute | solution.py:39
  21.1 4.3 %collective-permute-done = bf16[256,512]{1,0:T(8,128)(2,1)S(1)} collective-permute-done((bf16[256,512]{1,0:T(8,128)(2,1)}, bf16[256,512]{1,0:T(8,128)(2,1)S(1)}, u32[]{:S(2)}, u32[]{:S(2)}) %collective-permute-start) | collective-permute-done | bytes 262176 | tf_op jit(solution)/shard_map/ppermute | solution.py:36
  25.4 1.9 collective-permute-start.1
  27.3 0.0 collective-permute-done.2
  27.3 4.6 %collective-permute-start.3 = (bf16[256,512]{1,0:T(8,128)(2,1)S(1)}, bf16[256,512]{1,0:T(8,128)(2,1)S(1)}, u32[]{:S(2)}, u32[]{:S(2)}) collective-permute-start(bf16[256,512]{1,0:T(8,128)(2,1)S(1)} %collective-permute-done.2), channel_id=1, source_target_pairs={{0,14},{1,15},{2,0},{3,1},{4,2},{5,3},{6,4},{7,5},{8,6},{9,7},{10,... | collective-permute-start | bytes 786440 | tf_op jit(solution)/shard_map/ppermute | solution.py:39
  31.9 5.2 %collective-permute-done.1 = bf16[256,512]{1,0:T(8,128)(2,1)S(1)} collective-permute-done((bf16[256,512]{1,0:T(8,128)(2,1)S(1)}, bf16[256,512]{1,0:T(8,128)(2,1)S(1)}, u32[]{:S(2)}, u32[]{:S(2)}) %collective-permute-start.1) | collective-permute-done | bytes 262176 | tf_op jit(solution)/shard_map/ppermute | solution.py:36
  37.0 0.2 collective-permute-done.3
  37.2 20.6 %all-gather.5.cloned.1.call-done = bf16[4096,256]{1,0:T(8,128)(2,1)} async-done(((bf16[256,256]{1,0:T(8,128)(2,1)}), bf16[4096,256]{1,0:T(8,128)(2,1)}) %all-gather.5.cloned.1.call-update) | async-done | bytes 2097168 | tf_op jit(solution)/shard_map/all_gather | solution.py:74
  57.8 0.0 copy-done
  57.8 2.3 fusion.16
  60.1 10.6 %all-gather = bf16[1024,256]{1,0:T(8,128)(2,1)} all-gather(bf16[256,256]{1,0:T(8,128)(2,1)S(1)} %fusion.16), channel_id=2, replica_groups=mesh['cy'=8,'cx'=4,'fsdp'=16] {'cx'}, dimensions={0}, use_global_device_ids=true | all-gather | bytes 655360 | tf_op jit(solution)/shard_map/all_gather | solution.py:81
  70.8 0.0 all-gather.7.cloned.1.call-update
  70.8 3.0 %collective-permute-start.4 = (bf16[256,512]{1,0:T(8,128)(2,1)S(1)}, bf16[256,512]{1,0:T(8,128)(2,1)}, u32[]{:S(2)}, u32[]{:S(2)}) collective-permute-start(bf16[256,512]{1,0:T(8,128)(2,1)S(1)} %collective-permute-done.1), channel_id=1, source_target_pairs={{0,2},{1,3},{2,4},{3,5},{4,6},{5,7},{6,8},{7,9},{8,10},{9,11},{10,... | collective-permute-start | bytes 786440 | tf_op jit(solution)/shard_map/ppermute | solution.py:36
  73.8 5.4 %collective-permute-done.4 = bf16[256,512]{1,0:T(8,128)(2,1)} collective-permute-done((bf16[256,512]{1,0:T(8,128)(2,1)S(1)}, bf16[256,512]{1,0:T(8,128)(2,1)}, u32[]{:S(2)}, u32[]{:S(2)}) %collective-permute-start.4) | collective-permute-done | bytes 262176 | tf_op jit(solution)/shard_map/ppermute | solution.py:36
  79.2 1.9 collective-permute-start.5
  81.2 4.6 %collective-permute-start.6 = (bf16[256,512]{1,0:T(8,128)(2,1)S(1)}, bf16[256,512]{1,0:T(8,128)(2,1)S(1)}, u32[]{:S(2)}, u32[]{:S(2)}) collective-permute-start(bf16[256,512]{1,0:T(8,128)(2,1)S(1)} %collective-permute-done.3), channel_id=1, source_target_pairs={{0,14},{1,15},{2,0},{3,1},{4,2},{5,3},{6,4},{7,5},{8,6},{9,7},{10,... | collective-permute-start | bytes 786440 | tf_op jit(solution)/shard_map/ppermute | solution.py:39
  85.8 2.1 collective-permute-done.5
  87.8 1.0 bitcast_dynamic-update-slice_fusion.22
  88.8 1.0 bitcast_dynamic-update-slice_fusion.19
  89.9 0.0 copy-done.2
  90.1 0.0 collective-permute-done.6
  90.1 7.6 %collective-permute-start.7 = (bf16[8,256,512]{2,1,0:T(8,128)(2,1)S(1)}, bf16[8,256,512]{2,1,0:T(8,128)(2,1)S(1)}, u32[]{:S(2)}, u32[]{:S(2)}) collective-permute-start(bf16[8,256,512]{2,1,0:T(8,128)(2,1)S(1)} %get-tuple-element.19), channel_id=1, source_target_pairs={{0,1},{1,0},{2,3},{3,2},{4,5},{5,4},{6,7},{7,6},{8,9},{9,8},{10,11... | collective-permute-start | bytes 6291464 | tf_op jit(solution)/shard_map/ppermute | solution.py:42
  97.7 1.0 bitcast_dynamic-update-slice_fusion.23
  98.7 1.0 bitcast_dynamic-update-slice_fusion.20
  99.9 1.6 collective-permute-done.7
  101.5 0.9 select_bitcast_fusion.1
  102.4 0.4 pad_maximum_fusion
  102.8 0.0 copy-start.3
  102.8 1.3 convolution_convert_fusion
  104.1 0.0 copy-done.3
  104.1 0.1 copy.29
  104.3 0.6 gather_fusion
  104.8 0.1 copy.30
  104.9 0.1 copy.31
  105.0 0.1 reshape.150
  105.1 24.1 %all-gather.7.cloned.1.call-done = bf16[32,256,256]{2,1,0:T(8,128)(2,1)} async-done(((bf16[4,256,256]{2,1,0:T(8,128)(2,1)}), bf16[32,256,256]{2,1,0:T(8,128)(2,1)}) %all-gather.7.cloned.1.call-update) | async-done | bytes 4194320 | tf_op jit(solution)/shard_map/all_gather | solution.py:82
  129.2 5.0 %gather_fusion.1 = bf16[32,256,256]{2,1,0:T(8,128)(2,1)} fusion(bf16[32,256,256]{2,1,0:T(8,128)(2,1)} %all-gather.7.cloned.1.call-done, s32[1024]{0:T(1024)S(1)} %pad_clamp_fusion), kind=kCustom, calls=%fused_computation.1 | custom fusion | bytes 8388736 | tf_op jit(solution)/shard_map/jit(_take)/gather | solution.py:95
  134.2 8.1 %all-to-all-start = ((bf16[16,2,256,256]{3,2,1,0:T(8,128)(2,1)}), bf16[16,2,256,256]{3,2,1,0:T(8,128)(2,1)}, u32[]{:S(2)}, u32[]{:S(2)}) async-start(bf16[16,2,256,256]{3,2,1,0:T(8,128)(2,1)} %bitcast.95), calls=%async_computation | async-start | bytes 8388608 | tf_op jit(solution)/shard_map/all_to_all | solution.py:96
  142.3 0.1 fusion.19
  142.4 3.5 %collective-permute-start.8 = (bf16[256,256]{1,0:T(8,128)(2,1)S(1)}, bf16[256,256]{1,0:T(8,128)(2,1)S(1)}, u32[]{:S(2)}, u32[]{:S(2)}) collective-permute-start(bf16[256,256]{1,0:T(8,128)(2,1)S(1)} %fusion.16), channel_id=1, source_target_pairs={{0,1},{1,2},{2,3},{3,4},{4,5},{5,6},{6,7},{7,8},{8,9},{9,10},{10,1... | collective-permute-start | bytes 393224 | tf_op jit(solution)/shard_map/ppermute | solution.py:12
  146.0 0.1 constant_dynamic-slice_fusion.2
  146.0 0.6 fusion.38
  153.1 81.3 %collective-permute-done.8 = bf16[256,256]{1,0:T(8,128)(2,1)S(1)} collective-permute-done((bf16[256,256]{1,0:T(8,128)(2,1)S(1)}, bf16[256,256]{1,0:T(8,128)(2,1)S(1)}, u32[]{:S(2)}, u32[]{:S(2)}) %collective-permute-start.8) | collective-permute-done | bytes 131104 | tf_op jit(solution)/shard_map/ppermute | solution.py:12
  234.5 1.8 convolution_bitcast_fusion.2
  236.3 1.4 add_add_fusion
  237.7 0.0 all-to-all-done
  237.7 2.5 fusion.37
  240.2 0.0 copy-start.1
  240.3 0.4 convolution_bitcast_fusion.1
  240.7 0.4 convolution_bitcast_fusion
  241.2 0.6 copy-done.1
  241.8 0.7 fusion.18
  242.6 1.4 fusion.1
  244.0 1.6 fusion.13
  245.6 0.8 copy.36
  (25 shorter events, 0.5 us)
Async XLA Ops:
  6.5 51.3 %copy-start = (bf16[256,4096]{1,0:T(8,128)(2,1)S(1)}, bf16[256,4096]{1,0:T(8,128)(2,1)}, u32[]{:S(2)}) copy-start(bf16[256,4096]{1,0:T(8,128)(2,1)} %param.5) | copy-start | bytes 6291460
  6.5 51.3 %all-gather.5.cloned.1.call-start = ((), (), s32[]{:S(2)}) async-start(), calls=%async_computation.1 | async-start | bytes 2228224 | tf_op jit(solution)/shard_map/all_gather | solution.py:74
  8.3 81.7 %copy-start.2 = (bf16[256,512]{1,0:T(8,128)(2,1)S(1)}, bf16[256,512]{1,0:T(8,128)(2,1)}, u32[]{:S(2)}) copy-start(bf16[256,512]{1,0:T(8,128)(2,1)} %param.6) | copy-start | bytes 786436
  8.3 120.9 %all-gather.7.cloned.1.call-start = ((), (), s32[]{:S(2)}) async-start(), calls=%async_computation.2 | async-start | bytes 4718592 | tf_op jit(solution)/shard_map/all_gather | solution.py:82
  8.3 17.0 %collective-permute-start = (bf16[256,512]{1,0:T(8,128)(2,1)}, bf16[256,512]{1,0:T(8,128)(2,1)S(1)}, u32[]{:S(2)}, u32[]{:S(2)}) collective-permute-start(bf16[256,512]{1,0:T(8,128)(2,1)} %param.6), channel_id=1, source_target_pairs={{0,2},{1,3},{2,4},{3,5},{4,6},{5,7},{6,8},{7,9},{8,10},{9,11},{10,... | collective-permute-start | bytes 786440 | tf_op jit(solution)/shard_map/ppermute | solution.py:36
  12.5 14.8 %collective-permute-start.2 = (bf16[256,512]{1,0:T(8,128)(2,1)}, bf16[256,512]{1,0:T(8,128)(2,1)S(1)}, u32[]{:S(2)}, u32[]{:S(2)}) collective-permute-start(bf16[256,512]{1,0:T(8,128)(2,1)} %param.6), channel_id=1, source_target_pairs={{0,14},{1,15},{2,0},{3,1},{4,2},{5,3},{6,4},{7,5},{8,6},{9,7},{10,... | collective-permute-start | bytes 786440 | tf_op jit(solution)/shard_map/ppermute | solution.py:39
  25.4 11.7 %collective-permute-start.1 = (bf16[256,512]{1,0:T(8,128)(2,1)S(1)}, bf16[256,512]{1,0:T(8,128)(2,1)S(1)}, u32[]{:S(2)}, u32[]{:S(2)}) collective-permute-start(bf16[256,512]{1,0:T(8,128)(2,1)S(1)} %collective-permute-done), channel_id=1, source_target_pairs={{0,2},{1,3},{2,4},{3,5},{4,6},{5,7},{6,8},{7,9},{8,10},{9,11},{10,... | collective-permute-start | bytes 786440 | tf_op jit(solution)/shard_map/ppermute | solution.py:36
  27.3 9.9 %collective-permute-start.3 = (bf16[256,512]{1,0:T(8,128)(2,1)S(1)}, bf16[256,512]{1,0:T(8,128)(2,1)S(1)}, u32[]{:S(2)}, u32[]{:S(2)}) collective-permute-start(bf16[256,512]{1,0:T(8,128)(2,1)S(1)} %collective-permute-done.2), channel_id=1, source_target_pairs={{0,14},{1,15},{2,0},{3,1},{4,2},{5,3},{6,4},{7,5},{8,6},{9,7},{10,... | collective-permute-start | bytes 786440 | tf_op jit(solution)/shard_map/ppermute | solution.py:39
  70.8 8.4 %collective-permute-start.4 = (bf16[256,512]{1,0:T(8,128)(2,1)S(1)}, bf16[256,512]{1,0:T(8,128)(2,1)}, u32[]{:S(2)}, u32[]{:S(2)}) collective-permute-start(bf16[256,512]{1,0:T(8,128)(2,1)S(1)} %collective-permute-done.1), channel_id=1, source_target_pairs={{0,2},{1,3},{2,4},{3,5},{4,6},{5,7},{6,8},{7,9},{8,10},{9,11},{10,... | collective-permute-start | bytes 786440 | tf_op jit(solution)/shard_map/ppermute | solution.py:36
  79.2 8.6 %collective-permute-start.5 = (bf16[256,512]{1,0:T(8,128)(2,1)}, bf16[256,512]{1,0:T(8,128)(2,1)}, u32[]{:S(2)}, u32[]{:S(2)}) collective-permute-start(bf16[256,512]{1,0:T(8,128)(2,1)} %collective-permute-done.4), channel_id=1, source_target_pairs={{0,2},{1,3},{2,4},{3,5},{4,6},{5,7},{6,8},{7,9},{8,10},{9,11},{10,... | collective-permute-start | bytes 786440 | tf_op jit(solution)/shard_map/ppermute | solution.py:36
  81.2 8.9 %collective-permute-start.6 = (bf16[256,512]{1,0:T(8,128)(2,1)S(1)}, bf16[256,512]{1,0:T(8,128)(2,1)S(1)}, u32[]{:S(2)}, u32[]{:S(2)}) collective-permute-start(bf16[256,512]{1,0:T(8,128)(2,1)S(1)} %collective-permute-done.3), channel_id=1, source_target_pairs={{0,14},{1,15},{2,0},{3,1},{4,2},{5,3},{6,4},{7,5},{8,6},{9,7},{10,... | collective-permute-start | bytes 786440 | tf_op jit(solution)/shard_map/ppermute | solution.py:39
  90.1 11.4 %collective-permute-start.7 = (bf16[8,256,512]{2,1,0:T(8,128)(2,1)S(1)}, bf16[8,256,512]{2,1,0:T(8,128)(2,1)S(1)}, u32[]{:S(2)}, u32[]{:S(2)}) collective-permute-start(bf16[8,256,512]{2,1,0:T(8,128)(2,1)S(1)} %get-tuple-element.19), channel_id=1, source_target_pairs={{0,1},{1,0},{2,3},{3,2},{4,5},{5,4},{6,7},{7,6},{8,9},{9,8},{10,11... | collective-permute-start | bytes 6291464 | tf_op jit(solution)/shard_map/ppermute | solution.py:42
  102.8 1.3 copy-start.3
  134.2 103.5 %all-to-all-start = ((bf16[16,2,256,256]{3,2,1,0:T(8,128)(2,1)}), bf16[16,2,256,256]{3,2,1,0:T(8,128)(2,1)}, u32[]{:S(2)}, u32[]{:S(2)}) async-start(bf16[16,2,256,256]{3,2,1,0:T(8,128)(2,1)} %bitcast.95), calls=%async_computation | async-start | bytes 8388608 | tf_op jit(solution)/shard_map/all_to_all | solution.py:96
  142.4 92.1 %collective-permute-start.8 = (bf16[256,256]{1,0:T(8,128)(2,1)S(1)}, bf16[256,256]{1,0:T(8,128)(2,1)S(1)}, u32[]{:S(2)}, u32[]{:S(2)}) collective-permute-start(bf16[256,256]{1,0:T(8,128)(2,1)S(1)} %fusion.16), channel_id=1, source_target_pairs={{0,1},{1,2},{2,3},{3,4},{4,5},{5,6},{6,7},{7,8},{8,9},{9,10},{10,1... | collective-permute-start | bytes 393224 | tf_op jit(solution)/shard_map/ppermute | solution.py:12
  240.2 1.6 copy-start.1
Sparse Core Ops, SparseCore 0:
  9.5 48.2 all-gather.4
  70.9 58.2 all-gather.6

commit v11 on v7

--- a/solution.py
+++ b/solution.py
@@ -93,6 +93,8 @@
     dest_block = group_index * blocks_group + jnp.arange(lane_count, dtype=jnp.int32) // 2
     dest_pick = chosen[dest_block, jnp.arange(lane_count, dtype=jnp.int32) % 2]
     outgoing = jnp.take(candidates, dest_pick // blocks_group, axis=0, mode="clip")
+    needed = dest_pick % blocks_group == lane_index // 2
+    outgoing = jnp.where(needed[:, None, None], outgoing, jnp.zeros_like(outgoing))
     incoming = lax.all_to_all(outgoing, "fsdp", split_axis=0, concat_axis=0, tiled=True)
 
     mine = lax.dynamic_index_in_dim(chosen, my_block, 0, keepdims=False)

time: 212 us -> 216 us (1.019)
  other arithmetic: 10.4 us -> 13.5 us
    select_n x0 -> x1, other arithmetic: none -> 3.16 us  [per_device(): jnp.where(needed[:, None, None], outgoing, jnp.zeros_like(outgoing))]
  transfers between devices with their start and end apart: 13 -> 13, of which waited for: 9 -> 9; matrix products, arithmetic and copies ran while one was open for 13% -> 12% of each run, Pallas kernels for 0% -> 0%
where the time goes in v11:
time: 216 us; the launch traced here: 215 us
  waiting for transfers between devices  88.3 us (41%)
  starting transfers between devices  53.7 us (25%)
  local copies, waits for them, and re-layouts  23.6 us (11%)
  between operations  17.4 us (8%)
  other arithmetic  13.5 us (6%)
  blocking collectives  10.6 us (5%)
  matrix products  7.73 us (4%)
    ppermute x1, waiting for transfers between devices, from_behind(): return lax.ppermute(array, axis, pairs)  39.2 us
    all_gather x1, waiting for transfers between devices, per_device(): lax.all_gather(jnp.concatenate([key_weight, value_weight], axis=1), 'fsdp...  20.6 us
    ppermute x3, starting transfers between devices, ring_gather_rows(): behind = lax.ppermute(behind, axis, shift_pairs(-2))  17.7 us
    ppermute x4, waiting for transfers between devices, ring_gather_rows(): ahead = lax.ppermute(ahead, axis, shift_pairs(2))  16.6 us
    unnamed x28, local copies, waits for them, and re-layouts  13.6 us
    all_gather x1, waiting for transfers between devices, per_device(): lax.all_gather(along_x[None], 'cy', axis=0, tiled=True)  11 us
    ppermute x4, starting transfers between devices, ring_gather_rows(): ahead = lax.ppermute(ahead, axis, shift_pairs(2))  11 us
    all_gather x1, blocking collectives, per_device(): along_x = lax.all_gather(key_value[None], 'cx', axis=0, tiled=True)  10.6 us
  transfers between devices with their start and end apart: 13, of which 9 were waited for; matrix products, arithmetic and copies ran while one was open for 12% of the time, Pallas kernels for 0%

profile of v11, /device:TPU:7, one launch (start us, length us, event | category | flops | bytes accessed | tf_op | source)
XLA Modules:
  0.0 214.9 jit_solution(5920880322382169400)
XLA Ops:
  6.5 1.7 pad_maximum_fusion.2
  8.2 0.0 all-gather.5.cloned.1.call-update
  8.3 0.0 copy-start.3
  8.3 0.0 all-gather.7.cloned.1.call-start
  8.3 4.1 %collective-permute-start = (bf16[256,512]{1,0:T(8,128)(2,1)}, bf16[256,512]{1,0:T(8,128)(2,1)S(1)}, u32[]{:S(2)}, u32[]{:S(2)}) collective-permute-start(bf16[256,512]{1,0:T(8,128)(2,1)} %param.6), channel_id=1, source_target_pairs={{0,2},{1,3},{2,4},{3,5},{4,6},{5,7},{6,8},{7,9},{8,10},{9,11},{10,... | collective-permute-start | bytes 786440 | tf_op jit(solution)/shard_map/ppermute | solution.py:36
  12.5 8.6 %collective-permute-start.2 = (bf16[256,512]{1,0:T(8,128)(2,1)}, bf16[256,512]{1,0:T(8,128)(2,1)S(1)}, u32[]{:S(2)}, u32[]{:S(2)}) collective-permute-start(bf16[256,512]{1,0:T(8,128)(2,1)} %param.6), channel_id=1, source_target_pairs={{0,14},{1,15},{2,0},{3,1},{4,2},{5,3},{6,4},{7,5},{8,6},{9,7},{10,... | collective-permute-start | bytes 786440 | tf_op jit(solution)/shard_map/ppermute | solution.py:39
  21.1 4.3 %collective-permute-done = bf16[256,512]{1,0:T(8,128)(2,1)S(1)} collective-permute-done((bf16[256,512]{1,0:T(8,128)(2,1)}, bf16[256,512]{1,0:T(8,128)(2,1)S(1)}, u32[]{:S(2)}, u32[]{:S(2)}) %collective-permute-start) | collective-permute-done | bytes 262176 | tf_op jit(solution)/shard_map/ppermute | solution.py:36
  25.4 1.9 collective-permute-start.1
  27.3 4.6 %collective-permute-start.3 = (bf16[256,512]{1,0:T(8,128)(2,1)S(1)}, bf16[256,512]{1,0:T(8,128)(2,1)S(1)}, u32[]{:S(2)}, u32[]{:S(2)}) collective-permute-start(bf16[256,512]{1,0:T(8,128)(2,1)S(1)} %collective-permute-done.2), channel_id=1, source_target_pairs={{0,14},{1,15},{2,0},{3,1},{4,2},{5,3},{6,4},{7,5},{8,6},{9,7},{10,... | collective-permute-start | bytes 786440 | tf_op jit(solution)/shard_map/ppermute | solution.py:39
  31.9 5.2 %collective-permute-done.1 = bf16[256,512]{1,0:T(8,128)(2,1)S(1)} collective-permute-done((bf16[256,512]{1,0:T(8,128)(2,1)S(1)}, bf16[256,512]{1,0:T(8,128)(2,1)S(1)}, u32[]{:S(2)}, u32[]{:S(2)}) %collective-permute-start.1) | collective-permute-done | bytes 262176 | tf_op jit(solution)/shard_map/ppermute | solution.py:36
  37.0 0.2 collective-permute-done.3
  37.2 20.6 %all-gather.5.cloned.1.call-done = bf16[4096,256]{1,0:T(8,128)(2,1)} async-done(((bf16[256,256]{1,0:T(8,128)(2,1)}), bf16[4096,256]{1,0:T(8,128)(2,1)}) %all-gather.5.cloned.1.call-update) | async-done | bytes 2097168 | tf_op jit(solution)/shard_map/all_gather | solution.py:74
  57.8 2.3 %fusion.16 = bf16[256,256]{1,0:T(8,128)(2,1)S(1)} fusion(bf16[256,4096]{1,0:T(8,128)(2,1)S(1)} %copy-done, bf16[4096,256]{1,0:T(8,128)(2,1)} %all-gather.5.cloned.1.call-done), kind=kOutput, calls=%fused_computation.25 | convolution fusion | flops 536936448 | bytes 4325376 | tf_op jit(solution)/shard_map/dot_general | solution.py:78
  60.1 10.6 %all-gather = bf16[1024,256]{1,0:T(8,128)(2,1)} all-gather(bf16[256,256]{1,0:T(8,128)(2,1)S(1)} %fusion.16), channel_id=2, replica_groups=mesh['cy'=8,'cx'=4,'fsdp'=16] {'cx'}, dimensions={0}, use_global_device_ids=true | all-gather | bytes 655360 | tf_op jit(solution)/shard_map/all_gather | solution.py:81
  70.8 0.0 all-gather.7.cloned.1.call-update
  70.8 3.0 %collective-permute-start.4 = (bf16[256,512]{1,0:T(8,128)(2,1)S(1)}, bf16[256,512]{1,0:T(8,128)(2,1)S(1)}, u32[]{:S(2)}, u32[]{:S(2)}) collective-permute-start(bf16[256,512]{1,0:T(8,128)(2,1)S(1)} %collective-permute-done.1), channel_id=1, source_target_pairs={{0,2},{1,3},{2,4},{3,5},{4,6},{5,7},{6,8},{7,9},{8,10},{9,11},{10,... | collective-permute-start | bytes 786440 | tf_op jit(solution)/shard_map/ppermute | solution.py:36
  73.8 5.3 %collective-permute-done.4 = bf16[256,512]{1,0:T(8,128)(2,1)S(1)} collective-permute-done((bf16[256,512]{1,0:T(8,128)(2,1)S(1)}, bf16[256,512]{1,0:T(8,128)(2,1)S(1)}, u32[]{:S(2)}, u32[]{:S(2)}) %collective-permute-start.4) | collective-permute-done | bytes 262176 | tf_op jit(solution)/shard_map/ppermute | solution.py:36
  79.1 1.9 collective-permute-start.5
  81.0 4.6 %collective-permute-start.6 = (bf16[256,512]{1,0:T(8,128)(2,1)S(1)}, bf16[256,512]{1,0:T(8,128)(2,1)S(1)}, u32[]{:S(2)}, u32[]{:S(2)}) collective-permute-start(bf16[256,512]{1,0:T(8,128)(2,1)S(1)} %collective-permute-done.3), channel_id=1, source_target_pairs={{0,14},{1,15},{2,0},{3,1},{4,2},{5,3},{6,4},{7,5},{8,6},{9,7},{10,... | collective-permute-start | bytes 786440 | tf_op jit(solution)/shard_map/ppermute | solution.py:39
  85.6 1.8 collective-permute-done.5
  87.4 0.9 bitcast_dynamic-update-slice_fusion.22
  88.3 0.8 bitcast_dynamic-update-slice_fusion.19
  89.1 0.8 bitcast_dynamic-update-slice_fusion.16
  90.0 0.8 bitcast_dynamic-update-slice_fusion.13
  90.8 0.8 bitcast_dynamic-update-slice_fusion.10
  91.6 0.8 bitcast_dynamic-update-slice_fusion.7
  92.5 0.8 bitcast_dynamic-update-slice_fusion.4
  93.3 0.0 collective-permute-done.6
  93.3 0.7 copy-done.4
  94.0 0.8 bitcast_dynamic-update-slice_fusion.1
  94.9 7.6 %collective-permute-start.7 = (bf16[8,256,512]{2,1,0:T(8,128)(2,1)}, bf16[8,256,512]{2,1,0:T(8,128)(2,1)}, u32[]{:S(2)}, u32[]{:S(2)}) collective-permute-start(bf16[8,256,512]{2,1,0:T(8,128)(2,1)} %get-tuple-element.17), channel_id=1, source_target_pairs={{0,1},{1,0},{2,3},{3,2},{4,5},{5,4},{6,7},{7,6},{8,9},{9,8},{10,11... | collective-permute-start | bytes 6291464 | tf_op jit(solution)/shard_map/ppermute | solution.py:42
  102.5 1.7 bitcast_dynamic-update-slice_fusion.23
  104.2 1.7 bitcast_dynamic-update-slice_fusion.20
  105.9 0.7 bitcast_dynamic-update-slice_fusion.17
  106.6 0.7 bitcast_dynamic-update-slice_fusion.14
  107.3 0.7 bitcast_dynamic-update-slice_fusion.11
  108.0 0.7 bitcast_dynamic-update-slice_fusion.8
  108.7 0.7 bitcast_dynamic-update-slice_fusion.5
  109.5 1.7 bitcast_dynamic-update-slice_fusion.2
  111.2 4.5 %select_bitcast_fusion.1 = (bf16[8,1,256,512]{3,2,1,0:T(8,128)(2,1)S(1)}, bf16[8,1,256,512]{3,2,1,0:T(8,128)(2,1)S(1)}) fusion(pred[]{:T(512)S(6)} %eq.25, bf16[16,256,512]{2,1,0:T(8,128)(2,1)} %bitcast_dynamic-update-slice_fusion.2, s32[]{:T(128)S(6)} %select_n.131, bf16[8,256,512]{2,1,0:T(8,128)(2,1)} %collective-permute-done.7), kind=kLoop, calls=%fused_computation.14 | loop fusion | flops 4194304 | bytes 8388613 | tf_op jit(solution)/shard_map/stack | solution.py:54
  115.7 0.4 pad_maximum_fusion
  116.1 0.0 copy-start.1
  116.1 1.3 convolution_convert_fusion
  117.4 0.7 gather_fusion
  118.2 11.0 %all-gather.7.cloned.1.call-done = bf16[32,256,256]{2,1,0:T(8,128)(2,1)} async-done(((bf16[4,256,256]{2,1,0:T(8,128)(2,1)}), bf16[32,256,256]{2,1,0:T(8,128)(2,1)}) %all-gather.7.cloned.1.call-update) | async-done | bytes 4194320 | tf_op jit(solution)/shard_map/all_gather | solution.py:82
  129.2 4.2 %gather_fusion.1 = bf16[16,256,256]{2,1,0:T(8,128)(2,1)} fusion(bf16[32,256,256]{2,1,0:T(8,128)(2,1)} %all-gather.7.cloned.1.call-done, s32[1024]{0:T(1024)S(1)} %pad_clamp_fusion), kind=kCustom, calls=%fused_computation.1 | custom fusion | bytes 4194368 | tf_op jit(solution)/shard_map/jit(_take)/gather | solution.py:95
  133.4 3.2 %broadcast_select_fusion = bf16[16,256,256]{2,1,0:T(8,128)(2,1)} fusion(bf16[16,256,256]{2,1,0:T(8,128)(2,1)} %gather_fusion.1, pred[16]{0:T(512)(128)(4,1)S(1)} %fusion.38), kind=kLoop, calls=%fused_computation.15 | loop fusion | flops 1048576 | bytes 4194320 | tf_op jit(solution)/shard_map/jit(_where)/select_n | solution.py:97
  136.6 8.1 %all-to-all-start = ((bf16[16,256,256]{2,1,0:T(8,128)(2,1)}), bf16[16,256,256]{2,1,0:T(8,128)(2,1)}, u32[]{:S(2)}, u32[]{:S(2)}) async-start(bf16[16,256,256]{2,1,0:T(8,128)(2,1)} %broadcast_select_fusion), calls=%async_computation | async-start | bytes 4194304 | tf_op jit(solution)/shard_map/all_to_all | solution.py:98
  144.6 0.1 fusion.19
  144.8 3.5 %collective-permute-start.8 = (bf16[256,256]{1,0:T(8,128)(2,1)S(1)}, bf16[256,256]{1,0:T(8,128)(2,1)S(1)}, u32[]{:S(2)}, u32[]{:S(2)}) collective-permute-start(bf16[256,256]{1,0:T(8,128)(2,1)S(1)} %fusion.16), channel_id=1, source_target_pairs={{0,1},{1,2},{2,3},{3,4},{4,5},{5,6},{6,7},{7,8},{8,9},{9,10},{10,1... | collective-permute-start | bytes 393224 | tf_op jit(solution)/shard_map/ppermute | solution.py:12
  148.3 0.1 constant_dynamic-slice_fusion.1
  148.4 0.5 fusion.45
  152.7 39.2 %collective-permute-done.8 = bf16[256,256]{1,0:T(8,128)(2,1)S(1)} collective-permute-done((bf16[256,256]{1,0:T(8,128)(2,1)S(1)}, bf16[256,256]{1,0:T(8,128)(2,1)S(1)}, u32[]{:S(2)}, u32[]{:S(2)}) %collective-permute-start.8) | collective-permute-done | bytes 131104 | tf_op jit(solution)/shard_map/ppermute | solution.py:12
  191.8 1.7 convolution_bitcast_fusion.2
  193.6 1.4 add_add_fusion
  195.0 1.1 constant_dynamic-slice_fusion
  196.1 5.8 %collective-permute-start.9 = (bf16[512,256]{1,0:T(8,128)(2,1)S(1)}, bf16[512,256]{1,0:T(8,128)(2,1)S(1)}, u32[]{:S(2)}, u32[]{:S(2)}) collective-permute-start(bf16[512,256]{1,0:T(8,128)(2,1)S(1)} %bitcast.100), channel_id=1, source_target_pairs={{0,1},{1,0},{2,3},{3,2},{4,5},{5,4},{6,7},{7,6},{8,9},{9,8},{10,11... | collective-permute-start | bytes 786440 | tf_op jit(solution)/shard_map/ppermute | solution.py:61
  201.9 0.4 convolution_bitcast_fusion.1
  202.4 0.7 collective-permute-done.9
  203.1 0.4 convolution_bitcast_fusion
  203.5 0.8 fusion.18
  204.3 1.4 fusion.1
  205.7 1.6 fusion.13
  207.3 0.8 copy.25
  (27 shorter events, 0.1 us)
Async XLA Ops:
  6.5 51.3 %copy-start = (bf16[256,4096]{1,0:T(8,128)(2,1)S(1)}, bf16[256,4096]{1,0:T(8,128)(2,1)}, u32[]{:S(2)}) copy-start(bf16[256,4096]{1,0:T(8,128)(2,1)} %param.5) | copy-start | bytes 6291460
  6.5 51.3 %all-gather.5.cloned.1.call-start = ((), (), s32[]{:S(2)}) async-start(), calls=%async_computation.1 | async-start | bytes 2228224 | tf_op jit(solution)/shard_map/all_gather | solution.py:74
  8.3 82.6 %copy-start.3 = (bf16[256,512]{1,0:T(8,128)(2,1)S(1)}, bf16[256,512]{1,0:T(8,128)(2,1)}, u32[]{:S(2)}) copy-start(bf16[256,512]{1,0:T(8,128)(2,1)} %param.6) | copy-start | bytes 786436
  8.3 120.9 %all-gather.7.cloned.1.call-start = ((), (), s32[]{:S(2)}) async-start(), calls=%async_computation.2 | async-start | bytes 4718592 | tf_op jit(solution)/shard_map/all_gather | solution.py:82
  8.3 17.0 %collective-permute-start = (bf16[256,512]{1,0:T(8,128)(2,1)}, bf16[256,512]{1,0:T(8,128)(2,1)S(1)}, u32[]{:S(2)}, u32[]{:S(2)}) collective-permute-start(bf16[256,512]{1,0:T(8,128)(2,1)} %param.6), channel_id=1, source_target_pairs={{0,2},{1,3},{2,4},{3,5},{4,6},{5,7},{6,8},{7,9},{8,10},{9,11},{10,... | collective-permute-start | bytes 786440 | tf_op jit(solution)/shard_map/ppermute | solution.py:36
  12.5 14.8 %collective-permute-start.2 = (bf16[256,512]{1,0:T(8,128)(2,1)}, bf16[256,512]{1,0:T(8,128)(2,1)S(1)}, u32[]{:S(2)}, u32[]{:S(2)}) collective-permute-start(bf16[256,512]{1,0:T(8,128)(2,1)} %param.6), channel_id=1, source_target_pairs={{0,14},{1,15},{2,0},{3,1},{4,2},{5,3},{6,4},{7,5},{8,6},{9,7},{10,... | collective-permute-start | bytes 786440 | tf_op jit(solution)/shard_map/ppermute | solution.py:39
  25.4 11.7 %collective-permute-start.1 = (bf16[256,512]{1,0:T(8,128)(2,1)S(1)}, bf16[256,512]{1,0:T(8,128)(2,1)S(1)}, u32[]{:S(2)}, u32[]{:S(2)}) collective-permute-start(bf16[256,512]{1,0:T(8,128)(2,1)S(1)} %collective-permute-done), channel_id=1, source_target_pairs={{0,2},{1,3},{2,4},{3,5},{4,6},{5,7},{6,8},{7,9},{8,10},{9,11},{10,... | collective-permute-start | bytes 786440 | tf_op jit(solution)/shard_map/ppermute | solution.py:36
  27.3 9.9 %collective-permute-start.3 = (bf16[256,512]{1,0:T(8,128)(2,1)S(1)}, bf16[256,512]{1,0:T(8,128)(2,1)S(1)}, u32[]{:S(2)}, u32[]{:S(2)}) collective-permute-start(bf16[256,512]{1,0:T(8,128)(2,1)S(1)} %collective-permute-done.2), channel_id=1, source_target_pairs={{0,14},{1,15},{2,0},{3,1},{4,2},{5,3},{6,4},{7,5},{8,6},{9,7},{10,... | collective-permute-start | bytes 786440 | tf_op jit(solution)/shard_map/ppermute | solution.py:39
  70.8 8.3 %collective-permute-start.4 = (bf16[256,512]{1,0:T(8,128)(2,1)S(1)}, bf16[256,512]{1,0:T(8,128)(2,1)S(1)}, u32[]{:S(2)}, u32[]{:S(2)}) collective-permute-start(bf16[256,512]{1,0:T(8,128)(2,1)S(1)} %collective-permute-done.1), channel_id=1, source_target_pairs={{0,2},{1,3},{2,4},{3,5},{4,6},{5,7},{6,8},{7,9},{8,10},{9,11},{10,... | collective-permute-start | bytes 786440 | tf_op jit(solution)/shard_map/ppermute | solution.py:36
  79.1 15.8 %copy-start.5 = (bf16[256,512]{1,0:T(8,128)(2,1)}, bf16[256,512]{1,0:T(8,128)(2,1)S(1)}, u32[]{:S(2)}) copy-start(bf16[256,512]{1,0:T(8,128)(2,1)S(1)} %collective-permute-done.4) | copy-start | bytes 786436
  79.1 8.3 %collective-permute-start.5 = (bf16[256,512]{1,0:T(8,128)(2,1)S(1)}, bf16[256,512]{1,0:T(8,128)(2,1)S(1)}, u32[]{:S(2)}, u32[]{:S(2)}) collective-permute-start(bf16[256,512]{1,0:T(8,128)(2,1)S(1)} %collective-permute-done.4), channel_id=1, source_target_pairs={{0,2},{1,3},{2,4},{3,5},{4,6},{5,7},{6,8},{7,9},{8,10},{9,11},{10,... | collective-permute-start | bytes 786440 | tf_op jit(solution)/shard_map/ppermute | solution.py:36
  81.0 12.3 %collective-permute-start.6 = (bf16[256,512]{1,0:T(8,128)(2,1)S(1)}, bf16[256,512]{1,0:T(8,128)(2,1)S(1)}, u32[]{:S(2)}, u32[]{:S(2)}) collective-permute-start(bf16[256,512]{1,0:T(8,128)(2,1)S(1)} %collective-permute-done.3), channel_id=1, source_target_pairs={{0,14},{1,15},{2,0},{3,1},{4,2},{5,3},{6,4},{7,5},{8,6},{9,7},{10,... | collective-permute-start | bytes 786440 | tf_op jit(solution)/shard_map/ppermute | solution.py:39
  87.4 7.4 %copy-start.6 = (bf16[256,512]{1,0:T(8,128)(2,1)}, bf16[256,512]{1,0:T(8,128)(2,1)S(1)}, u32[]{:S(2)}) copy-start(bf16[256,512]{1,0:T(8,128)(2,1)S(1)} %collective-permute-done.5) | copy-start | bytes 786436
  93.3 0.7 copy-start.4
  94.9 16.3 %collective-permute-start.7 = (bf16[8,256,512]{2,1,0:T(8,128)(2,1)}, bf16[8,256,512]{2,1,0:T(8,128)(2,1)}, u32[]{:S(2)}, u32[]{:S(2)}) collective-permute-start(bf16[8,256,512]{2,1,0:T(8,128)(2,1)} %get-tuple-element.17), channel_id=1, source_target_pairs={{0,1},{1,0},{2,3},{3,2},{4,5},{5,4},{6,7},{7,6},{8,9},{9,8},{10,11... | collective-permute-start | bytes 6291464 | tf_op jit(solution)/shard_map/ppermute | solution.py:42
  116.1 1.3 copy-start.1
  136.6 58.4 %all-to-all-start = ((bf16[16,256,256]{2,1,0:T(8,128)(2,1)}), bf16[16,256,256]{2,1,0:T(8,128)(2,1)}, u32[]{:S(2)}, u32[]{:S(2)}) async-start(bf16[16,256,256]{2,1,0:T(8,128)(2,1)} %broadcast_select_fusion), calls=%async_computation | async-start | bytes 4194304 | tf_op jit(solution)/shard_map/all_to_all | solution.py:98
  144.8 47.0 %collective-permute-start.8 = (bf16[256,256]{1,0:T(8,128)(2,1)S(1)}, bf16[256,256]{1,0:T(8,128)(2,1)S(1)}, u32[]{:S(2)}, u32[]{:S(2)}) collective-permute-start(bf16[256,256]{1,0:T(8,128)(2,1)S(1)} %fusion.16), channel_id=1, source_target_pairs={{0,1},{1,2},{2,3},{3,4},{4,5},{5,6},{6,7},{7,8},{8,9},{9,10},{10,1... | collective-permute-start | bytes 393224 | tf_op jit(solution)/shard_map/ppermute | solution.py:12
  195.0 8.5 %copy-start.2 = (f32[4,256,512]{1,2,0:T(8,128)S(1)}, f32[4,256,512]{1,2,0:T(8,128)}, u32[]{:S(2)}) copy-start(f32[4,256,512]{1,2,0:T(8,128)} %convolution_bitcast_fusion.2) | copy-start | bytes 6291460
  196.1 6.9 %collective-permute-start.9 = (bf16[512,256]{1,0:T(8,128)(2,1)S(1)}, bf16[512,256]{1,0:T(8,128)(2,1)S(1)}, u32[]{:S(2)}, u32[]{:S(2)}) collective-permute-start(bf16[512,256]{1,0:T(8,128)(2,1)S(1)} %bitcast.100), channel_id=1, source_target_pairs={{0,1},{1,0},{2,3},{3,2},{4,5},{5,4},{6,7},{7,6},{8,9},{9,8},{10,11... | collective-permute-start | bytes 786440 | tf_op jit(solution)/shard_map/ppermute | solution.py:61
Sparse Core Ops, SparseCore 0:
  9.5 48.2 all-gather.4
  70.9 58.2 all-gather.6

commit v12 on v7

--- a/solution.py
+++ b/solution.py
@@ -1,6 +1,7 @@
 import jax
 import jax.numpy as jnp
 from jax import lax
+from jax.experimental.layout import Layout, with_layout_constraint
 from jax.sharding import Mesh, PartitionSpec as P
 
 QH = 4
@@ -93,6 +94,7 @@
     dest_block = group_index * blocks_group + jnp.arange(lane_count, dtype=jnp.int32) // 2
     dest_pick = chosen[dest_block, jnp.arange(lane_count, dtype=jnp.int32) % 2]
     outgoing = jnp.take(candidates, dest_pick // blocks_group, axis=0, mode="clip")
+    outgoing = with_layout_constraint(outgoing, Layout(major_to_minor=(0, 2, 1)))
     incoming = lax.all_to_all(outgoing, "fsdp", split_axis=0, concat_axis=0, tiled=True)
 
     mine = lax.dynamic_index_in_dim(chosen, my_block, 0, keepdims=False)

time: 212 us -> 217 us (1.024)
  local copies, waits for them, and re-layouts: 23.6 us -> 27.6 us
    gather x1 -> x2, local copies, waits for them, and re-layouts: 4.23 us -> 8.14 us  [per_device(): jnp.take(candidates, dest_pick // blocks_group, axis=0, mode='clip')]
  transfers between devices with their start and end apart: 13 -> 13, of which waited for: 9 -> 9; matrix products, arithmetic and copies ran while one was open for 13% -> 12% of each run, Pallas kernels for 0% -> 0%
where the time goes in v12:
time: 217 us; the launch traced here: 216 us
  waiting for transfers between devices  87.9 us (41%)
  starting transfers between devices  53.8 us (25%)
  local copies, waits for them, and re-layouts  27.6 us (13%)
  between operations  17.8 us (8%)
  blocking collectives  10.6 us (5%)
  other arithmetic  10.4 us (5%)
  matrix products  7.79 us (4%)
    ppermute x1, waiting for transfers between devices, from_behind(): return lax.ppermute(array, axis, pairs)  38.8 us
    all_gather x1, waiting for transfers between devices, per_device(): lax.all_gather(jnp.concatenate([key_weight, value_weight], axis=1), 'fsdp...  20.6 us
    ppermute x3, starting transfers between devices, ring_gather_rows(): behind = lax.ppermute(behind, axis, shift_pairs(-2))  17.7 us
    ppermute x4, waiting for transfers between devices, ring_gather_rows(): ahead = lax.ppermute(ahead, axis, shift_pairs(2))  16.6 us
    unnamed x28, local copies, waits for them, and re-layouts  13.6 us
    all_gather x1, waiting for transfers between devices, per_device(): lax.all_gather(along_x[None], 'cy', axis=0, tiled=True)  11 us
    ppermute x4, starting transfers between devices, ring_gather_rows(): ahead = lax.ppermute(ahead, axis, shift_pairs(2))  11 us
    all_gather x1, blocking collectives, per_device(): along_x = lax.all_gather(key_value[None], 'cx', axis=0, tiled=True)  10.6 us
  transfers between devices with their start and end apart: 13, of which 9 were waited for; matrix products, arithmetic and copies ran while one was open for 12% of the time, Pallas kernels for 0%

profile of v12, /device:TPU:7, one launch (start us, length us, event | category | flops | bytes accessed | tf_op | source)
XLA Modules:
  0.0 215.9 jit_solution(10143169605341670871)
XLA Ops:
  6.5 1.7 pad_maximum_fusion.2
  8.2 0.0 all-gather.5.cloned.1.call-update
  8.3 0.0 copy-start.3
  8.3 0.0 all-gather.7.cloned.1.call-start
  8.3 4.1 %collective-permute-start = (bf16[256,512]{1,0:T(8,128)(2,1)}, bf16[256,512]{1,0:T(8,128)(2,1)S(1)}, u32[]{:S(2)}, u32[]{:S(2)}) collective-permute-start(bf16[256,512]{1,0:T(8,128)(2,1)} %param.6), channel_id=1, source_target_pairs={{0,2},{1,3},{2,4},{3,5},{4,6},{5,7},{6,8},{7,9},{8,10},{9,11},{10,... | collective-permute-start | bytes 786440 | tf_op jit(solution)/shard_map/ppermute | solution.py:37
  12.5 8.6 %collective-permute-start.2 = (bf16[256,512]{1,0:T(8,128)(2,1)}, bf16[256,512]{1,0:T(8,128)(2,1)S(1)}, u32[]{:S(2)}, u32[]{:S(2)}) collective-permute-start(bf16[256,512]{1,0:T(8,128)(2,1)} %param.6), channel_id=1, source_target_pairs={{0,14},{1,15},{2,0},{3,1},{4,2},{5,3},{6,4},{7,5},{8,6},{9,7},{10,... | collective-permute-start | bytes 786440 | tf_op jit(solution)/shard_map/ppermute | solution.py:40
  21.1 4.3 %collective-permute-done = bf16[256,512]{1,0:T(8,128)(2,1)S(1)} collective-permute-done((bf16[256,512]{1,0:T(8,128)(2,1)}, bf16[256,512]{1,0:T(8,128)(2,1)S(1)}, u32[]{:S(2)}, u32[]{:S(2)}) %collective-permute-start) | collective-permute-done | bytes 262176 | tf_op jit(solution)/shard_map/ppermute | solution.py:37
  25.4 1.9 collective-permute-start.1
  27.3 4.6 %collective-permute-start.3 = (bf16[256,512]{1,0:T(8,128)(2,1)S(1)}, bf16[256,512]{1,0:T(8,128)(2,1)S(1)}, u32[]{:S(2)}, u32[]{:S(2)}) collective-permute-start(bf16[256,512]{1,0:T(8,128)(2,1)S(1)} %collective-permute-done.2), channel_id=1, source_target_pairs={{0,14},{1,15},{2,0},{3,1},{4,2},{5,3},{6,4},{7,5},{8,6},{9,7},{10,... | collective-permute-start | bytes 786440 | tf_op jit(solution)/shard_map/ppermute | solution.py:40
  31.9 5.2 %collective-permute-done.1 = bf16[256,512]{1,0:T(8,128)(2,1)S(1)} collective-permute-done((bf16[256,512]{1,0:T(8,128)(2,1)S(1)}, bf16[256,512]{1,0:T(8,128)(2,1)S(1)}, u32[]{:S(2)}, u32[]{:S(2)}) %collective-permute-start.1) | collective-permute-done | bytes 262176 | tf_op jit(solution)/shard_map/ppermute | solution.py:37
  37.0 0.2 collective-permute-done.3
  37.2 20.6 %all-gather.5.cloned.1.call-done = bf16[4096,256]{1,0:T(8,128)(2,1)} async-done(((bf16[256,256]{1,0:T(8,128)(2,1)}), bf16[4096,256]{1,0:T(8,128)(2,1)}) %all-gather.5.cloned.1.call-update) | async-done | bytes 2097168 | tf_op jit(solution)/shard_map/all_gather | solution.py:75
  57.8 2.3 %fusion.16 = bf16[256,256]{1,0:T(8,128)(2,1)S(1)} fusion(bf16[256,4096]{1,0:T(8,128)(2,1)S(1)} %copy-done, bf16[4096,256]{1,0:T(8,128)(2,1)} %all-gather.5.cloned.1.call-done), kind=kOutput, calls=%fused_computation.24 | convolution fusion | flops 536936448 | bytes 4325376 | tf_op jit(solution)/shard_map/dot_general | solution.py:79
  60.1 10.6 %all-gather = bf16[1024,256]{1,0:T(8,128)(2,1)} all-gather(bf16[256,256]{1,0:T(8,128)(2,1)S(1)} %fusion.16), channel_id=2, replica_groups=mesh['cy'=8,'cx'=4,'fsdp'=16] {'cx'}, dimensions={0}, use_global_device_ids=true | all-gather | bytes 655360 | tf_op jit(solution)/shard_map/all_gather | solution.py:82
  70.8 0.0 all-gather.7.cloned.1.call-update
  70.8 3.0 %collective-permute-start.4 = (bf16[256,512]{1,0:T(8,128)(2,1)S(1)}, bf16[256,512]{1,0:T(8,128)(2,1)S(1)}, u32[]{:S(2)}, u32[]{:S(2)}) collective-permute-start(bf16[256,512]{1,0:T(8,128)(2,1)S(1)} %collective-permute-done.1), channel_id=1, source_target_pairs={{0,2},{1,3},{2,4},{3,5},{4,6},{5,7},{6,8},{7,9},{8,10},{9,11},{10,... | collective-permute-start | bytes 786440 | tf_op jit(solution)/shard_map/ppermute | solution.py:37
  73.8 5.3 %collective-permute-done.4 = bf16[256,512]{1,0:T(8,128)(2,1)S(1)} collective-permute-done((bf16[256,512]{1,0:T(8,128)(2,1)S(1)}, bf16[256,512]{1,0:T(8,128)(2,1)S(1)}, u32[]{:S(2)}, u32[]{:S(2)}) %collective-permute-start.4) | collective-permute-done | bytes 262176 | tf_op jit(solution)/shard_map/ppermute | solution.py:37
  79.1 1.9 collective-permute-start.5
  81.0 4.6 %collective-permute-start.6 = (bf16[256,512]{1,0:T(8,128)(2,1)S(1)}, bf16[256,512]{1,0:T(8,128)(2,1)S(1)}, u32[]{:S(2)}, u32[]{:S(2)}) collective-permute-start(bf16[256,512]{1,0:T(8,128)(2,1)S(1)} %collective-permute-done.3), channel_id=1, source_target_pairs={{0,14},{1,15},{2,0},{3,1},{4,2},{5,3},{6,4},{7,5},{8,6},{9,7},{10,... | collective-permute-start | bytes 786440 | tf_op jit(solution)/shard_map/ppermute | solution.py:40
  85.6 1.8 collective-permute-done.5
  87.4 0.9 bitcast_dynamic-update-slice_fusion.22
  88.3 0.8 bitcast_dynamic-update-slice_fusion.19
  89.1 0.8 bitcast_dynamic-update-slice_fusion.16
  90.0 0.8 bitcast_dynamic-update-slice_fusion.13
  90.8 0.8 bitcast_dynamic-update-slice_fusion.10
  91.6 0.8 bitcast_dynamic-update-slice_fusion.7
  92.5 0.8 bitcast_dynamic-update-slice_fusion.4
  93.3 0.7 copy-done.4
  94.0 0.8 bitcast_dynamic-update-slice_fusion.1
  94.9 7.6 %collective-permute-start.7 = (bf16[8,256,512]{2,1,0:T(8,128)(2,1)}, bf16[8,256,512]{2,1,0:T(8,128)(2,1)}, u32[]{:S(2)}, u32[]{:S(2)}) collective-permute-start(bf16[8,256,512]{2,1,0:T(8,128)(2,1)} %get-tuple-element.17), channel_id=1, source_target_pairs={{0,1},{1,0},{2,3},{3,2},{4,5},{5,4},{6,7},{7,6},{8,9},{9,8},{10,11... | collective-permute-start | bytes 6291464 | tf_op jit(solution)/shard_map/ppermute | solution.py:43
  102.5 1.7 bitcast_dynamic-update-slice_fusion.23
  104.2 1.7 bitcast_dynamic-update-slice_fusion.20
  105.9 0.7 bitcast_dynamic-update-slice_fusion.17
  106.6 0.7 bitcast_dynamic-update-slice_fusion.14
  107.3 0.7 bitcast_dynamic-update-slice_fusion.11
  108.0 0.7 bitcast_dynamic-update-slice_fusion.8
  108.7 0.7 bitcast_dynamic-update-slice_fusion.5
  109.5 1.7 bitcast_dynamic-update-slice_fusion.2
  111.2 4.5 %select_bitcast_fusion.1 = (bf16[8,1,256,512]{3,2,1,0:T(8,128)(2,1)S(1)}, bf16[8,1,256,512]{3,2,1,0:T(8,128)(2,1)S(1)}) fusion(pred[]{:T(512)S(6)} %eq.14, bf16[16,256,512]{2,1,0:T(8,128)(2,1)} %bitcast_dynamic-update-slice_fusion.2, s32[]{:T(128)S(6)} %select_n.118, bf16[8,256,512]{2,1,0:T(8,128)(2,1)} %collective-permute-done.7), kind=kLoop, calls=%fused_computation.14 | loop fusion | flops 4194304 | bytes 8388613 | tf_op jit(solution)/shard_map/stack | solution.py:55
  115.7 0.4 pad_maximum_fusion
  116.1 0.0 copy-start.1
  116.1 1.3 convolution_convert_fusion
  117.4 0.7 gather_fusion
  118.2 11.0 %all-gather.7.cloned.1.call-done = bf16[32,256,256]{2,1,0:T(8,128)(2,1)} async-done(((bf16[4,256,256]{2,1,0:T(8,128)(2,1)}), bf16[32,256,256]{2,1,0:T(8,128)(2,1)}) %all-gather.7.cloned.1.call-update) | async-done | bytes 4194320 | tf_op jit(solution)/shard_map/all_gather | solution.py:83
  129.2 4.2 %gather_fusion.1 = bf16[16,256,256]{2,1,0:T(8,128)(2,1)} fusion(bf16[32,256,256]{2,1,0:T(8,128)(2,1)} %all-gather.7.cloned.1.call-done, s32[1024]{0:T(1024)S(1)} %pad_clamp_fusion), kind=kCustom, calls=%fused_computation.1 | custom fusion | bytes 4194368 | tf_op jit(solution)/shard_map/jit(_take)/gather | solution.py:96
  133.4 3.9 %copy.23 = bf16[16,256,256]{1,2,0:T(8,128)(2,1)} copy(bf16[16,256,256]{2,1,0:T(8,128)(2,1)} %gather_fusion.1) | data formatting | bytes 4194304 | tf_op jit(solution)/shard_map/jit(_take)/gather | solution.py:96
  137.3 8.1 %all-to-all-start = ((bf16[16,256,256]{1,2,0:T(8,128)(2,1)}), bf16[16,256,256]{1,2,0:T(8,128)(2,1)}, u32[]{:S(2)}, u32[]{:S(2)}) async-start(bf16[16,256,256]{1,2,0:T(8,128)(2,1)} %copy.23), calls=%async_computation | async-start | bytes 4194304 | tf_op jit(solution)/shard_map/all_to_all | solution.py:98
  145.4 0.1 fusion.19
  145.5 3.5 %collective-permute-start.8 = (bf16[256,256]{1,0:T(8,128)(2,1)S(1)}, bf16[256,256]{1,0:T(8,128)(2,1)S(1)}, u32[]{:S(2)}, u32[]{:S(2)}) collective-permute-start(bf16[256,256]{1,0:T(8,128)(2,1)S(1)} %fusion.16), channel_id=1, source_target_pairs={{0,1},{1,2},{2,3},{3,4},{4,5},{5,6},{6,7},{7,8},{8,9},{9,10},{10,1... | collective-permute-start | bytes 393224 | tf_op jit(solution)/shard_map/ppermute | solution.py:13
  149.1 0.1 constant_dynamic-slice_fusion.1
  149.2 0.6 fusion.43
  153.8 38.8 %collective-permute-done.8 = bf16[256,256]{1,0:T(8,128)(2,1)S(1)} collective-permute-done((bf16[256,256]{1,0:T(8,128)(2,1)S(1)}, bf16[256,256]{1,0:T(8,128)(2,1)S(1)}, u32[]{:S(2)}, u32[]{:S(2)}) %collective-permute-start.8) | collective-permute-done | bytes 131104 | tf_op jit(solution)/shard_map/ppermute | solution.py:13
  192.6 1.8 convolution_bitcast_fusion.2
  194.4 1.4 add_add_fusion
  195.8 1.0 constant_dynamic-slice_fusion
  196.8 0.1 copy.24
  196.9 5.9 %collective-permute-start.9 = (bf16[512,256]{1,0:T(8,128)(2,1)S(1)}, bf16[512,256]{1,0:T(8,128)(2,1)S(1)}, u32[]{:S(2)}, u32[]{:S(2)}) collective-permute-start(bf16[512,256]{1,0:T(8,128)(2,1)S(1)} %bitcast.100), channel_id=1, source_target_pairs={{0,1},{1,0},{2,3},{3,2},{4,5},{5,4},{6,7},{7,6},{8,9},{9,8},{10,11... | collective-permute-start | bytes 786440 | tf_op jit(solution)/shard_map/ppermute | solution.py:62
  202.9 0.4 convolution_bitcast_fusion.1
  203.3 0.7 collective-permute-done.9
  204.0 0.4 convolution_bitcast_fusion
  204.4 0.8 fusion.18
  205.2 1.4 fusion.1
  206.6 1.6 fusion.13
  208.2 0.8 copy.29
  (27 shorter events, 0.1 us)
Async XLA Ops:
  6.5 51.3 %copy-start = (bf16[256,4096]{1,0:T(8,128)(2,1)S(1)}, bf16[256,4096]{1,0:T(8,128)(2,1)}, u32[]{:S(2)}) copy-start(bf16[256,4096]{1,0:T(8,128)(2,1)} %param.5) | copy-start | bytes 6291460
  6.5 51.3 %all-gather.5.cloned.1.call-start = ((), (), s32[]{:S(2)}) async-start(), calls=%async_computation.1 | async-start | bytes 2228224 | tf_op jit(solution)/shard_map/all_gather | solution.py:75
  8.3 82.6 %copy-start.3 = (bf16[256,512]{1,0:T(8,128)(2,1)S(1)}, bf16[256,512]{1,0:T(8,128)(2,1)}, u32[]{:S(2)}) copy-start(bf16[256,512]{1,0:T(8,128)(2,1)} %param.6) | copy-start | bytes 786436
  8.3 120.9 %all-gather.7.cloned.1.call-start = ((), (), s32[]{:S(2)}) async-start(), calls=%async_computation.2 | async-start | bytes 4718592 | tf_op jit(solution)/shard_map/all_gather | solution.py:83
  8.3 17.0 %collective-permute-start = (bf16[256,512]{1,0:T(8,128)(2,1)}, bf16[256,512]{1,0:T(8,128)(2,1)S(1)}, u32[]{:S(2)}, u32[]{:S(2)}) collective-permute-start(bf16[256,512]{1,0:T(8,128)(2,1)} %param.6), channel_id=1, source_target_pairs={{0,2},{1,3},{2,4},{3,5},{4,6},{5,7},{6,8},{7,9},{8,10},{9,11},{10,... | collective-permute-start | bytes 786440 | tf_op jit(solution)/shard_map/ppermute | solution.py:37
  12.5 14.8 %collective-permute-start.2 = (bf16[256,512]{1,0:T(8,128)(2,1)}, bf16[256,512]{1,0:T(8,128)(2,1)S(1)}, u32[]{:S(2)}, u32[]{:S(2)}) collective-permute-start(bf16[256,512]{1,0:T(8,128)(2,1)} %param.6), channel_id=1, source_target_pairs={{0,14},{1,15},{2,0},{3,1},{4,2},{5,3},{6,4},{7,5},{8,6},{9,7},{10,... | collective-permute-start | bytes 786440 | tf_op jit(solution)/shard_map/ppermute | solution.py:40
  25.4 11.7 %collective-permute-start.1 = (bf16[256,512]{1,0:T(8,128)(2,1)S(1)}, bf16[256,512]{1,0:T(8,128)(2,1)S(1)}, u32[]{:S(2)}, u32[]{:S(2)}) collective-permute-start(bf16[256,512]{1,0:T(8,128)(2,1)S(1)} %collective-permute-done), channel_id=1, source_target_pairs={{0,2},{1,3},{2,4},{3,5},{4,6},{5,7},{6,8},{7,9},{8,10},{9,11},{10,... | collective-permute-start | bytes 786440 | tf_op jit(solution)/shard_map/ppermute | solution.py:37
  27.3 9.9 %collective-permute-start.3 = (bf16[256,512]{1,0:T(8,128)(2,1)S(1)}, bf16[256,512]{1,0:T(8,128)(2,1)S(1)}, u32[]{:S(2)}, u32[]{:S(2)}) collective-permute-start(bf16[256,512]{1,0:T(8,128)(2,1)S(1)} %collective-permute-done.2), channel_id=1, source_target_pairs={{0,14},{1,15},{2,0},{3,1},{4,2},{5,3},{6,4},{7,5},{8,6},{9,7},{10,... | collective-permute-start | bytes 786440 | tf_op jit(solution)/shard_map/ppermute | solution.py:40
  70.8 8.3 %collective-permute-start.4 = (bf16[256,512]{1,0:T(8,128)(2,1)S(1)}, bf16[256,512]{1,0:T(8,128)(2,1)S(1)}, u32[]{:S(2)}, u32[]{:S(2)}) collective-permute-start(bf16[256,512]{1,0:T(8,128)(2,1)S(1)} %collective-permute-done.1), channel_id=1, source_target_pairs={{0,2},{1,3},{2,4},{3,5},{4,6},{5,7},{6,8},{7,9},{8,10},{9,11},{10,... | collective-permute-start | bytes 786440 | tf_op jit(solution)/shard_map/ppermute | solution.py:37
  79.1 15.8 %copy-start.5 = (bf16[256,512]{1,0:T(8,128)(2,1)}, bf16[256,512]{1,0:T(8,128)(2,1)S(1)}, u32[]{:S(2)}) copy-start(bf16[256,512]{1,0:T(8,128)(2,1)S(1)} %collective-permute-done.4) | copy-start | bytes 786436
  79.1 8.3 %collective-permute-start.5 = (bf16[256,512]{1,0:T(8,128)(2,1)S(1)}, bf16[256,512]{1,0:T(8,128)(2,1)S(1)}, u32[]{:S(2)}, u32[]{:S(2)}) collective-permute-start(bf16[256,512]{1,0:T(8,128)(2,1)S(1)} %collective-permute-done.4), channel_id=1, source_target_pairs={{0,2},{1,3},{2,4},{3,5},{4,6},{5,7},{6,8},{7,9},{8,10},{9,11},{10,... | collective-permute-start | bytes 786440 | tf_op jit(solution)/shard_map/ppermute | solution.py:37
  81.0 12.3 %collective-permute-start.6 = (bf16[256,512]{1,0:T(8,128)(2,1)S(1)}, bf16[256,512]{1,0:T(8,128)(2,1)S(1)}, u32[]{:S(2)}, u32[]{:S(2)}) collective-permute-start(bf16[256,512]{1,0:T(8,128)(2,1)S(1)} %collective-permute-done.3), channel_id=1, source_target_pairs={{0,14},{1,15},{2,0},{3,1},{4,2},{5,3},{6,4},{7,5},{8,6},{9,7},{10,... | collective-permute-start | bytes 786440 | tf_op jit(solution)/shard_map/ppermute | solution.py:40
  87.4 7.4 %copy-start.6 = (bf16[256,512]{1,0:T(8,128)(2,1)}, bf16[256,512]{1,0:T(8,128)(2,1)S(1)}, u32[]{:S(2)}) copy-start(bf16[256,512]{1,0:T(8,128)(2,1)S(1)} %collective-permute-done.5) | copy-start | bytes 786436
  93.3 0.7 copy-start.4
  94.9 16.3 %collective-permute-start.7 = (bf16[8,256,512]{2,1,0:T(8,128)(2,1)}, bf16[8,256,512]{2,1,0:T(8,128)(2,1)}, u32[]{:S(2)}, u32[]{:S(2)}) collective-permute-start(bf16[8,256,512]{2,1,0:T(8,128)(2,1)} %get-tuple-element.17), channel_id=1, source_target_pairs={{0,1},{1,0},{2,3},{3,2},{4,5},{5,4},{6,7},{7,6},{8,9},{9,8},{10,11... | collective-permute-start | bytes 6291464 | tf_op jit(solution)/shard_map/ppermute | solution.py:43
  116.1 1.3 copy-start.1
  137.3 58.5 %all-to-all-start = ((bf16[16,256,256]{1,2,0:T(8,128)(2,1)}), bf16[16,256,256]{1,2,0:T(8,128)(2,1)}, u32[]{:S(2)}, u32[]{:S(2)}) async-start(bf16[16,256,256]{1,2,0:T(8,128)(2,1)} %copy.23), calls=%async_computation | async-start | bytes 4194304 | tf_op jit(solution)/shard_map/all_to_all | solution.py:98
  145.5 47.0 %collective-permute-start.8 = (bf16[256,256]{1,0:T(8,128)(2,1)S(1)}, bf16[256,256]{1,0:T(8,128)(2,1)S(1)}, u32[]{:S(2)}, u32[]{:S(2)}) collective-permute-start(bf16[256,256]{1,0:T(8,128)(2,1)S(1)} %fusion.16), channel_id=1, source_target_pairs={{0,1},{1,2},{2,3},{3,4},{4,5},{5,6},{6,7},{7,8},{8,9},{9,10},{10,1... | collective-permute-start | bytes 393224 | tf_op jit(solution)/shard_map/ppermute | solution.py:13
  196.9 7.5 %copy-start.2 = (f32[4,256,512]{1,2,0:T(8,128)S(1)}, f32[4,256,512]{1,2,0:T(8,128)}, u32[]{:S(2)}) copy-start(f32[4,256,512]{1,2,0:T(8,128)} %convolution_bitcast_fusion.2) | copy-start | bytes 6291460
  196.9 7.1 %collective-permute-start.9 = (bf16[512,256]{1,0:T(8,128)(2,1)S(1)}, bf16[512,256]{1,0:T(8,128)(2,1)S(1)}, u32[]{:S(2)}, u32[]{:S(2)}) collective-permute-start(bf16[512,256]{1,0:T(8,128)(2,1)S(1)} %bitcast.100), channel_id=1, source_target_pairs={{0,1},{1,0},{2,3},{3,2},{4,5},{5,4},{6,7},{7,6},{8,9},{9,8},{10,11... | collective-permute-start | bytes 786440 | tf_op jit(solution)/shard_map/ppermute | solution.py:62
Sparse Core Ops, SparseCore 0:
  9.5 48.2 all-gather.4
  70.9 58.2 all-gather.6

commit v13 on v7

--- a/solution.py
+++ b/solution.py
@@ -74,7 +74,7 @@
     kv_weight = lax.all_gather(
         jnp.concatenate([key_weight, value_weight], axis=1), "fsdp", axis=0, tiled=True
     )
-    q_weight, kv_weight = ring_gather_rows(query_weight, "fsdp", 2, kv_weight)
+    q_weight, kv_weight = ring_gather_rows(query_weight, "fsdp", 3, kv_weight)
     kv_f32 = jnp.dot(tokens, kv_weight, preferred_element_type=jnp.float32)
     key_value = kv_f32.astype(jnp.bfloat16)
 

time: 212 us -> 213 us (level)
  local copies, waits for them, and re-layouts: 23.6 us -> 26.3 us
    all_gather x1, waiting for transfers between devices: 20.6 us -> 8.56 us  [per_device(): lax.all_gather(jnp.concatenate([key_weight, value_weight], axis=1), 'fsdp...]
    all_gather x1, waiting for transfers between devices: 11 us -> 18 us  [per_device(): lax.all_gather(along_x[None], 'cy', axis=0, tiled=True)]
    ppermute x4, waiting for transfers between devices: 16.6 us -> 20.9 us  [ring_gather_rows(): ahead = lax.ppermute(ahead, axis, shift_pairs(2))]
    unnamed x28 -> x26, local copies, waits for them, and re-layouts: 13.6 us -> 15.2 us
  transfers between devices with their start and end apart: 13 -> 13, of which waited for: 9 -> 8; matrix products, arithmetic and copies ran while one was open for 13% -> 13% of each run, Pallas kernels for 0% -> 0%
where the time goes in v13:
time: 213 us; the launch traced here: 212 us
  waiting for transfers between devices  87.1 us (41%)
  starting transfers between devices  52.7 us (25%)
  local copies, waits for them, and re-layouts  26.3 us (12%)
  between operations  17.6 us (8%)
  blocking collectives  10.6 us (5%)
  other arithmetic  10.4 us (5%)
  matrix products  7.73 us (4%)
    ppermute x1, waiting for transfers between devices, from_behind(): return lax.ppermute(array, axis, pairs)  39 us
    ppermute x4, waiting for transfers between devices, ring_gather_rows(): ahead = lax.ppermute(ahead, axis, shift_pairs(2))  20.9 us
    all_gather x1, waiting for transfers between devices, per_device(): lax.all_gather(along_x[None], 'cy', axis=0, tiled=True)  18 us
    ppermute x3, starting transfers between devices, ring_gather_rows(): behind = lax.ppermute(behind, axis, shift_pairs(-2))  17.7 us
    unnamed x26, local copies, waits for them, and re-layouts  15.2 us
    ppermute x4, starting transfers between devices, ring_gather_rows(): ahead = lax.ppermute(ahead, axis, shift_pairs(2))  11 us
    all_gather x1, blocking collectives, per_device(): along_x = lax.all_gather(key_value[None], 'cx', axis=0, tiled=True)  10.6 us
    all_gather x1, waiting for transfers between devices, per_device(): lax.all_gather(jnp.concatenate([key_weight, value_weight], axis=1), 'fsdp...  8.56 us
  transfers between devices with their start and end apart: 13, of which 8 were waited for; matrix products, arithmetic and copies ran while one was open for 13% of the time, Pallas kernels for 0%

profile of v13, /device:TPU:7, one launch (start us, length us, event | category | flops | bytes accessed | tf_op | source)
XLA Modules:
  0.0 212.4 jit_solution(5998008725206318618)
XLA Ops:
  6.5 1.7 pad_maximum_fusion.2
  8.2 0.0 all-gather.5.cloned.1.call-update
  8.2 0.0 copy-start.3
  8.3 0.0 all-gather.7.cloned.1.call-start
  8.3 4.1 %collective-permute-start = (bf16[256,512]{1,0:T(8,128)(2,1)}, bf16[256,512]{1,0:T(8,128)(2,1)S(1)}, u32[]{:S(2)}, u32[]{:S(2)}) collective-permute-start(bf16[256,512]{1,0:T(8,128)(2,1)} %param.6), channel_id=1, source_target_pairs={{0,2},{1,3},{2,4},{3,5},{4,6},{5,7},{6,8},{7,9},{8,10},{9,11},{10,... | collective-permute-start | bytes 786440 | tf_op jit(solution)/shard_map/ppermute | solution.py:36
  12.5 8.6 %collective-permute-start.3 = (bf16[256,512]{1,0:T(8,128)(2,1)}, bf16[256,512]{1,0:T(8,128)(2,1)S(1)}, u32[]{:S(2)}, u32[]{:S(2)}) collective-permute-start(bf16[256,512]{1,0:T(8,128)(2,1)} %param.6), channel_id=1, source_target_pairs={{0,14},{1,15},{2,0},{3,1},{4,2},{5,3},{6,4},{7,5},{8,6},{9,7},{10,... | collective-permute-start | bytes 786440 | tf_op jit(solution)/shard_map/ppermute | solution.py:39
  21.0 4.3 %collective-permute-done = bf16[256,512]{1,0:T(8,128)(2,1)S(1)} collective-permute-done((bf16[256,512]{1,0:T(8,128)(2,1)}, bf16[256,512]{1,0:T(8,128)(2,1)S(1)}, u32[]{:S(2)}, u32[]{:S(2)}) %collective-permute-start) | collective-permute-done | bytes 262176 | tf_op jit(solution)/shard_map/ppermute | solution.py:36
  25.3 1.9 collective-permute-start.1
  27.3 4.6 %collective-permute-start.4 = (bf16[256,512]{1,0:T(8,128)(2,1)S(1)}, bf16[256,512]{1,0:T(8,128)(2,1)S(1)}, u32[]{:S(2)}, u32[]{:S(2)}) collective-permute-start(bf16[256,512]{1,0:T(8,128)(2,1)S(1)} %collective-permute-done.3), channel_id=1, source_target_pairs={{0,14},{1,15},{2,0},{3,1},{4,2},{5,3},{6,4},{7,5},{8,6},{9,7},{10,... | collective-permute-start | bytes 786440 | tf_op jit(solution)/shard_map/ppermute | solution.py:39
  31.9 5.2 %collective-permute-done.1 = bf16[256,512]{1,0:T(8,128)(2,1)S(1)} collective-permute-done((bf16[256,512]{1,0:T(8,128)(2,1)S(1)}, bf16[256,512]{1,0:T(8,128)(2,1)S(1)}, u32[]{:S(2)}, u32[]{:S(2)}) %collective-permute-start.1) | collective-permute-done | bytes 262176 | tf_op jit(solution)/shard_map/ppermute | solution.py:36
  37.0 1.9 collective-permute-start.2
  38.9 4.6 %collective-permute-start.5 = (bf16[256,512]{1,0:T(8,128)(2,1)S(1)}, bf16[256,512]{1,0:T(8,128)(2,1)}, u32[]{:S(2)}, u32[]{:S(2)}) collective-permute-start(bf16[256,512]{1,0:T(8,128)(2,1)S(1)} %collective-permute-done.4), channel_id=1, source_target_pairs={{0,14},{1,15},{2,0},{3,1},{4,2},{5,3},{6,4},{7,5},{8,6},{9,7},{10,... | collective-permute-start | bytes 786440 | tf_op jit(solution)/shard_map/ppermute | solution.py:39
  43.5 5.9 %collective-permute-done.2 = bf16[256,512]{1,0:T(8,128)(2,1)S(1)} collective-permute-done((bf16[256,512]{1,0:T(8,128)(2,1)S(1)}, bf16[256,512]{1,0:T(8,128)(2,1)S(1)}, u32[]{:S(2)}, u32[]{:S(2)}) %collective-permute-start.2) | collective-permute-done | bytes 262176 | tf_op jit(solution)/shard_map/ppermute | solution.py:36
  49.5 0.7 copy-done.4
  50.2 8.6 %all-gather.5.cloned.1.call-done = bf16[4096,256]{1,0:T(8,128)(2,1)} async-done(((bf16[256,256]{1,0:T(8,128)(2,1)}), bf16[4096,256]{1,0:T(8,128)(2,1)}) %all-gather.5.cloned.1.call-update) | async-done | bytes 2097168 | tf_op jit(solution)/shard_map/all_gather | solution.py:74
  58.7 2.3 %fusion.16 = bf16[256,256]{1,0:T(8,128)(2,1)S(1)} fusion(bf16[256,4096]{1,0:T(8,128)(2,1)S(1)} %copy-done, bf16[4096,256]{1,0:T(8,128)(2,1)} %all-gather.5.cloned.1.call-done), kind=kOutput, calls=%fused_computation.24 | convolution fusion | flops 536936448 | bytes 4325376 | tf_op jit(solution)/shard_map/dot_general | solution.py:78
  61.0 10.6 %all-gather = bf16[1024,256]{1,0:T(8,128)(2,1)} all-gather(bf16[256,256]{1,0:T(8,128)(2,1)S(1)} %fusion.16), channel_id=2, replica_groups=mesh['cy'=8,'cx'=4,'fsdp'=16] {'cx'}, dimensions={0}, use_global_device_ids=true | all-gather | bytes 655360 | tf_op jit(solution)/shard_map/all_gather | solution.py:81
  71.7 0.0 all-gather.7.cloned.1.call-update
  71.7 3.1 %collective-permute-start.6 = (bf16[256,512]{1,0:T(8,128)(2,1)}, bf16[256,512]{1,0:T(8,128)(2,1)S(1)}, u32[]{:S(2)}, u32[]{:S(2)}) collective-permute-start(bf16[256,512]{1,0:T(8,128)(2,1)} %copy-done.4), channel_id=1, source_target_pairs={{0,2},{1,3},{2,4},{3,5},{4,6},{5,7},{6,8},{7,9},{8,10},{9,11},{10,... | collective-permute-start | bytes 786440 | tf_op jit(solution)/shard_map/ppermute | solution.py:36
  74.8 5.5 %collective-permute-done.6 = bf16[256,512]{1,0:T(8,128)(2,1)S(1)} collective-permute-done((bf16[256,512]{1,0:T(8,128)(2,1)}, bf16[256,512]{1,0:T(8,128)(2,1)S(1)}, u32[]{:S(2)}, u32[]{:S(2)}) %collective-permute-start.6) | collective-permute-done | bytes 262176 | tf_op jit(solution)/shard_map/ppermute | solution.py:36
  80.2 0.7 copy-done.5
  80.9 0.8 bitcast_dynamic-update-slice_fusion.22
  81.8 1.8 bitcast_dynamic-update-slice_fusion.19
  83.6 0.8 bitcast_dynamic-update-slice_fusion.16
  84.4 0.8 bitcast_dynamic-update-slice_fusion.13
  85.2 0.9 bitcast_dynamic-update-slice_fusion.10
  86.1 0.8 bitcast_dynamic-update-slice_fusion.7
  86.9 0.8 bitcast_dynamic-update-slice_fusion.4
  87.8 1.8 bitcast_dynamic-update-slice_fusion.1
  89.6 6.5 %collective-permute-start.7 = (bf16[8,256,512]{2,1,0:T(8,128)(2,1)}, bf16[8,256,512]{2,1,0:T(8,128)(2,1)}, u32[]{:S(2)}, u32[]{:S(2)}) collective-permute-start(bf16[8,256,512]{2,1,0:T(8,128)(2,1)} %get-tuple-element.17), channel_id=1, source_target_pairs={{0,1},{1,0},{2,3},{3,2},{4,5},{5,4},{6,7},{7,6},{8,9},{9,8},{10,11... | collective-permute-start | bytes 6291464 | tf_op jit(solution)/shard_map/ppermute | solution.py:42
  96.1 1.7 bitcast_dynamic-update-slice_fusion.23
  97.8 1.7 bitcast_dynamic-update-slice_fusion.20
  99.5 0.7 bitcast_dynamic-update-slice_fusion.17
  100.2 0.7 bitcast_dynamic-update-slice_fusion.14
  100.9 0.7 bitcast_dynamic-update-slice_fusion.11
  101.6 0.7 bitcast_dynamic-update-slice_fusion.8
  102.4 0.7 bitcast_dynamic-update-slice_fusion.5
  103.1 1.7 bitcast_dynamic-update-slice_fusion.2
  104.8 0.0 collective-permute-done.7
  104.8 4.5 %select_bitcast_fusion.1 = (bf16[8,1,256,512]{3,2,1,0:T(8,128)(2,1)S(1)}, bf16[8,1,256,512]{3,2,1,0:T(8,128)(2,1)S(1)}) fusion(pred[]{:T(512)S(6)} %eq.14, bf16[16,256,512]{2,1,0:T(8,128)(2,1)} %bitcast_dynamic-update-slice_fusion.2, s32[]{:T(128)S(6)} %select_n.118, bf16[8,256,512]{2,1,0:T(8,128)(2,1)} %collective-permute-done.7), kind=kLoop, calls=%fused_computation.14 | loop fusion | flops 4194304 | bytes 8388613 | tf_op jit(solution)/shard_map/stack | solution.py:54
  109.4 0.4 pad_maximum_fusion
  109.7 0.0 copy-start.1
  109.8 1.3 convolution_convert_fusion
  111.1 0.7 gather_fusion
  111.8 18.0 %all-gather.7.cloned.1.call-done = bf16[32,256,256]{2,1,0:T(8,128)(2,1)} async-done(((bf16[4,256,256]{2,1,0:T(8,128)(2,1)}), bf16[32,256,256]{2,1,0:T(8,128)(2,1)}) %all-gather.7.cloned.1.call-update) | async-done | bytes 4194320 | tf_op jit(solution)/shard_map/all_gather | solution.py:82
  129.8 4.2 %gather_fusion.1 = bf16[16,256,256]{2,1,0:T(8,128)(2,1)} fusion(bf16[32,256,256]{2,1,0:T(8,128)(2,1)} %all-gather.7.cloned.1.call-done, s32[1024]{0:T(1024)S(1)} %pad_clamp_fusion), kind=kCustom, calls=%fused_computation.1 | custom fusion | bytes 4194368 | tf_op jit(solution)/shard_map/jit(_take)/gather | solution.py:95
  134.0 8.1 %all-to-all-start = ((bf16[16,256,256]{2,1,0:T(8,128)(2,1)}), bf16[16,256,256]{2,1,0:T(8,128)(2,1)}, u32[]{:S(2)}, u32[]{:S(2)}) async-start(bf16[16,256,256]{2,1,0:T(8,128)(2,1)} %gather_fusion.1), calls=%async_computation | async-start | bytes 4194304 | tf_op jit(solution)/shard_map/all_to_all | solution.py:96
  142.1 0.1 fusion.19
  142.2 3.5 %collective-permute-start.8 = (bf16[256,256]{1,0:T(8,128)(2,1)S(1)}, bf16[256,256]{1,0:T(8,128)(2,1)S(1)}, u32[]{:S(2)}, u32[]{:S(2)}) collective-permute-start(bf16[256,256]{1,0:T(8,128)(2,1)S(1)} %fusion.16), channel_id=1, source_target_pairs={{0,1},{1,2},{2,3},{3,4},{4,5},{5,6},{6,7},{7,8},{8,9},{9,10},{10,1... | collective-permute-start | bytes 393224 | tf_op jit(solution)/shard_map/ppermute | solution.py:12
  145.8 0.1 constant_dynamic-slice_fusion.1
  145.8 0.5 fusion.43
  150.3 39.0 %collective-permute-done.8 = bf16[256,256]{1,0:T(8,128)(2,1)S(1)} collective-permute-done((bf16[256,256]{1,0:T(8,128)(2,1)S(1)}, bf16[256,256]{1,0:T(8,128)(2,1)S(1)}, u32[]{:S(2)}, u32[]{:S(2)}) %collective-permute-start.8) | collective-permute-done | bytes 131104 | tf_op jit(solution)/shard_map/ppermute | solution.py:12
  189.3 1.7 convolution_bitcast_fusion.2
  191.0 1.4 add_add_fusion
  192.4 0.0 all-to-all-done
  192.4 1.1 constant_dynamic-slice_fusion
  193.5 5.8 %collective-permute-start.9 = (bf16[512,256]{1,0:T(8,128)(2,1)S(1)}, bf16[512,256]{1,0:T(8,128)(2,1)S(1)}, u32[]{:S(2)}, u32[]{:S(2)}) collective-permute-start(bf16[512,256]{1,0:T(8,128)(2,1)S(1)} %bitcast.100), channel_id=1, source_target_pairs={{0,1},{1,0},{2,3},{3,2},{4,5},{5,4},{6,7},{7,6},{8,9},{9,8},{10,11... | collective-permute-start | bytes 786440 | tf_op jit(solution)/shard_map/ppermute | solution.py:61
  199.4 0.4 convolution_bitcast_fusion.1
  199.8 0.7 collective-permute-done.9
  200.5 0.4 convolution_bitcast_fusion
  200.9 0.8 fusion.18
  201.7 1.4 fusion.1
  203.1 1.6 fusion.13
  204.7 0.8 copy.25
  (23 shorter events, 0.1 us)
Async XLA Ops:
  6.5 52.2 %copy-start = (bf16[256,4096]{1,0:T(8,128)(2,1)S(1)}, bf16[256,4096]{1,0:T(8,128)(2,1)}, u32[]{:S(2)}) copy-start(bf16[256,4096]{1,0:T(8,128)(2,1)} %param.5) | copy-start | bytes 6291460
  6.5 52.2 %all-gather.5.cloned.1.call-start = ((), (), s32[]{:S(2)}) async-start(), calls=%async_computation.1 | async-start | bytes 2228224 | tf_op jit(solution)/shard_map/all_gather | solution.py:74
  8.2 77.0 %copy-start.3 = (bf16[256,512]{1,0:T(8,128)(2,1)S(1)}, bf16[256,512]{1,0:T(8,128)(2,1)}, u32[]{:S(2)}) copy-start(bf16[256,512]{1,0:T(8,128)(2,1)} %param.6) | copy-start | bytes 786436
  8.3 121.5 %all-gather.7.cloned.1.call-start = ((), (), s32[]{:S(2)}) async-start(), calls=%async_computation.2 | async-start | bytes 4718592 | tf_op jit(solution)/shard_map/all_gather | solution.py:82
  8.3 17.0 %collective-permute-start = (bf16[256,512]{1,0:T(8,128)(2,1)}, bf16[256,512]{1,0:T(8,128)(2,1)S(1)}, u32[]{:S(2)}, u32[]{:S(2)}) collective-permute-start(bf16[256,512]{1,0:T(8,128)(2,1)} %param.6), channel_id=1, source_target_pairs={{0,2},{1,3},{2,4},{3,5},{4,6},{5,7},{6,8},{7,9},{8,10},{9,11},{10,... | collective-permute-start | bytes 786440 | tf_op jit(solution)/shard_map/ppermute | solution.py:36
  12.5 14.8 %collective-permute-start.3 = (bf16[256,512]{1,0:T(8,128)(2,1)}, bf16[256,512]{1,0:T(8,128)(2,1)S(1)}, u32[]{:S(2)}, u32[]{:S(2)}) collective-permute-start(bf16[256,512]{1,0:T(8,128)(2,1)} %param.6), channel_id=1, source_target_pairs={{0,14},{1,15},{2,0},{3,1},{4,2},{5,3},{6,4},{7,5},{8,6},{9,7},{10,... | collective-permute-start | bytes 786440 | tf_op jit(solution)/shard_map/ppermute | solution.py:39
  25.3 11.7 %collective-permute-start.1 = (bf16[256,512]{1,0:T(8,128)(2,1)S(1)}, bf16[256,512]{1,0:T(8,128)(2,1)S(1)}, u32[]{:S(2)}, u32[]{:S(2)}) collective-permute-start(bf16[256,512]{1,0:T(8,128)(2,1)S(1)} %collective-permute-done), channel_id=1, source_target_pairs={{0,2},{1,3},{2,4},{3,5},{4,6},{5,7},{6,8},{7,9},{8,10},{9,11},{10,... | collective-permute-start | bytes 786440 | tf_op jit(solution)/shard_map/ppermute | solution.py:36
  27.3 11.7 %collective-permute-start.4 = (bf16[256,512]{1,0:T(8,128)(2,1)S(1)}, bf16[256,512]{1,0:T(8,128)(2,1)S(1)}, u32[]{:S(2)}, u32[]{:S(2)}) collective-permute-start(bf16[256,512]{1,0:T(8,128)(2,1)S(1)} %collective-permute-done.3), channel_id=1, source_target_pairs={{0,14},{1,15},{2,0},{3,1},{4,2},{5,3},{6,4},{7,5},{8,6},{9,7},{10,... | collective-permute-start | bytes 786440 | tf_op jit(solution)/shard_map/ppermute | solution.py:39
  37.0 12.5 %collective-permute-start.2 = (bf16[256,512]{1,0:T(8,128)(2,1)S(1)}, bf16[256,512]{1,0:T(8,128)(2,1)S(1)}, u32[]{:S(2)}, u32[]{:S(2)}) collective-permute-start(bf16[256,512]{1,0:T(8,128)(2,1)S(1)} %collective-permute-done.1), channel_id=1, source_target_pairs={{0,2},{1,3},{2,4},{3,5},{4,6},{5,7},{6,8},{7,9},{8,10},{9,11},{10,... | collective-permute-start | bytes 786440 | tf_op jit(solution)/shard_map/ppermute | solution.py:36
  38.9 11.2 %collective-permute-start.5 = (bf16[256,512]{1,0:T(8,128)(2,1)S(1)}, bf16[256,512]{1,0:T(8,128)(2,1)}, u32[]{:S(2)}, u32[]{:S(2)}) collective-permute-start(bf16[256,512]{1,0:T(8,128)(2,1)S(1)} %collective-permute-done.4), channel_id=1, source_target_pairs={{0,14},{1,15},{2,0},{3,1},{4,2},{5,3},{6,4},{7,5},{8,6},{9,7},{10,... | collective-permute-start | bytes 786440 | tf_op jit(solution)/shard_map/ppermute | solution.py:39
  49.5 0.7 copy-start.4
  71.7 8.5 %collective-permute-start.6 = (bf16[256,512]{1,0:T(8,128)(2,1)}, bf16[256,512]{1,0:T(8,128)(2,1)S(1)}, u32[]{:S(2)}, u32[]{:S(2)}) collective-permute-start(bf16[256,512]{1,0:T(8,128)(2,1)} %copy-done.4), channel_id=1, source_target_pairs={{0,2},{1,3},{2,4},{3,5},{4,6},{5,7},{6,8},{7,9},{8,10},{9,11},{10,... | collective-permute-start | bytes 786440 | tf_op jit(solution)/shard_map/ppermute | solution.py:36
  80.2 0.7 copy-start.5
  89.6 15.2 %collective-permute-start.7 = (bf16[8,256,512]{2,1,0:T(8,128)(2,1)}, bf16[8,256,512]{2,1,0:T(8,128)(2,1)}, u32[]{:S(2)}, u32[]{:S(2)}) collective-permute-start(bf16[8,256,512]{2,1,0:T(8,128)(2,1)} %get-tuple-element.17), channel_id=1, source_target_pairs={{0,1},{1,0},{2,3},{3,2},{4,5},{5,4},{6,7},{7,6},{8,9},{9,8},{10,11... | collective-permute-start | bytes 6291464 | tf_op jit(solution)/shard_map/ppermute | solution.py:42
  109.7 1.3 copy-start.1
  134.0 58.4 %all-to-all-start = ((bf16[16,256,256]{2,1,0:T(8,128)(2,1)}), bf16[16,256,256]{2,1,0:T(8,128)(2,1)}, u32[]{:S(2)}, u32[]{:S(2)}) async-start(bf16[16,256,256]{2,1,0:T(8,128)(2,1)} %gather_fusion.1), calls=%async_computation | async-start | bytes 4194304 | tf_op jit(solution)/shard_map/all_to_all | solution.py:96
  142.2 47.0 %collective-permute-start.8 = (bf16[256,256]{1,0:T(8,128)(2,1)S(1)}, bf16[256,256]{1,0:T(8,128)(2,1)S(1)}, u32[]{:S(2)}, u32[]{:S(2)}) collective-permute-start(bf16[256,256]{1,0:T(8,128)(2,1)S(1)} %fusion.16), channel_id=1, source_target_pairs={{0,1},{1,2},{2,3},{3,4},{4,5},{5,6},{6,7},{7,8},{8,9},{9,10},{10,1... | collective-permute-start | bytes 393224 | tf_op jit(solution)/shard_map/ppermute | solution.py:12
  192.4 8.5 %copy-start.2 = (f32[4,256,512]{1,2,0:T(8,128)S(1)}, f32[4,256,512]{1,2,0:T(8,128)}, u32[]{:S(2)}) copy-start(f32[4,256,512]{1,2,0:T(8,128)} %convolution_bitcast_fusion.2) | copy-start | bytes 6291460
  193.5 6.9 %collective-permute-start.9 = (bf16[512,256]{1,0:T(8,128)(2,1)S(1)}, bf16[512,256]{1,0:T(8,128)(2,1)S(1)}, u32[]{:S(2)}, u32[]{:S(2)}) collective-permute-start(bf16[512,256]{1,0:T(8,128)(2,1)S(1)} %bitcast.100), channel_id=1, source_target_pairs={{0,1},{1,0},{2,3},{3,2},{4,5},{5,4},{6,7},{7,6},{8,9},{9,8},{10,11... | collective-permute-start | bytes 786440 | tf_op jit(solution)/shard_map/ppermute | solution.py:61
Sparse Core Ops, SparseCore 0:
  9.5 49.2 all-gather.4
  71.8 57.9 all-gather.6
